TPU v7x, 32 devices: a whole 2x2x4 slice. The times are simulated.
32 devices in a mesh: outer: 8 (over z, y), inner: 4 (over x, core).
Axes of the slice: x: 2, y: 2, z: 4, core: 2. Of those that a mesh axis runs over, the one named last changes fastest.
Arguments:
- query: bfloat16 [4096, 2048], P(('outer', 'inner')), may hold values from -6 to 6
- key_in: bfloat16 [4096, 2048], P(('outer', 'inner')), may hold values from -6 to 6
- value_in: bfloat16 [4096, 2048], P(('outer', 'inner')), may hold values from -6 to 6
- filters: bfloat16 [4096, 128], P(('outer', 'inner')), may hold values from -1 to 1
- group_index: int32 [2048], replicated, may hold values from 0 to 127
- skip_gain: float32 [2048], replicated, may hold values from -1 to 1
Outputs:
- hyena_out: bfloat16 [4096, 2048], P(('outer', 'inner'))
All inputs are finite; a program needn't handle non-finite values.
Results may differ from a plain program's by a relative error of at most 0.005.
Values may be sent and summed in bfloat16 or wider, within the bound.
No kernel may reach another device: no remote copies, remote signals or barrier semaphores. Data moves between devices by JAX's collectives and lax.ppermute only.
A program may use at most 64 MiB of HBM per device.

v0:
```python
import math

import jax
import jax.numpy as jnp
from jax import lax
from jax.sharding import PartitionSpec as P


def contract(pattern, left_op, right_op):
    return jnp.einsum(
        pattern,
        left_op,
        right_op,
        precision=lax.Precision.HIGH,
        preferred_element_type=jnp.float32,
    )


def angles_of(numerator, period):
    return 2.0 * math.pi / period * jnp.mod(numerator, period).astype(jnp.float32)


def dft_table(count_out, count_in, period):
    index_grid = (
        jnp.arange(count_out, dtype=jnp.int32)[:, None]
        * jnp.arange(count_in, dtype=jnp.int32)[None, :]
    )
    phases = angles_of(index_grid, period)
    return (jnp.cos(phases), jnp.sin(phases))


def rotate(real_part, imag_part, phases, direction):
    cosine = jnp.cos(phases)
    sine_part = jnp.sin(phases)
    if direction < 0:
        return (
            real_part * cosine + imag_part * sine_part,
            imag_part * cosine - real_part * sine_part,
        )
    return (real_part * cosine - imag_part * sine_part, imag_part * cosine + real_part * sine_part)


def transform(pattern, table_cos, table_sin, real_part, imag_part, direction):
    out_real = contract(pattern, table_cos, real_part) - direction * contract(
        pattern, table_sin, imag_part
    )
    out_imag = contract(pattern, table_cos, imag_part) + direction * contract(
        pattern, table_sin, real_part
    )
    return (out_real, out_imag)


def by_channels(mixed, filters, group_index):
    n_dev = lax.axis_size("outer") * lax.axis_size("inner")
    row_count = mixed.shape[0]
    channels = mixed.shape[1]
    own_width = channels // n_dev
    size_a = 2 * n_dev
    padded = size_a * row_count
    chan_filters = jnp.take(filters, group_index, axis=1)
    sent = jnp.stack([mixed, chan_filters], axis=1).reshape(row_count, 2, n_dev, own_width)
    sent = sent.transpose(2, 0, 1, 3)
    got = lax.all_to_all(sent, ("outer", "inner"), split_axis=0, concat_axis=0, tiled=True)
    stacked = got.reshape(n_dev, row_count, 2 * own_width).astype(jnp.float32)
    first_cos, first_sin = dft_table(size_a, n_dev, size_a)
    real_part = contract("kn,nbc->kbc", first_cos, stacked)
    imag_part = -contract("kn,nbc->kbc", first_sin, stacked)
    twiddle = angles_of(
        jnp.arange(size_a, dtype=jnp.int32)[:, None]
        * jnp.arange(row_count, dtype=jnp.int32)[None, :],
        padded,
    )[:, :, None]
    real_part, imag_part = rotate(real_part, imag_part, twiddle, -1)
    second_cos, second_sin = dft_table(row_count, row_count, row_count)
    real_part, imag_part = transform(
        "qb,kbc->kqc", second_cos, second_sin, real_part, imag_part, -1
    )
    data_real = real_part[:, :, :own_width]
    data_imag = imag_part[:, :, :own_width]
    filter_real = real_part[:, :, own_width:]
    filter_imag = imag_part[:, :, own_width:]
    spec_real = data_real * filter_real - data_imag * filter_imag
    spec_imag = data_real * filter_imag + data_imag * filter_real
    real_part, imag_part = transform("bq,kqc->kbc", second_cos, second_sin, spec_real, spec_imag, 1)
    real_part, imag_part = rotate(real_part, imag_part, twiddle, 1)
    back_cos, back_sin = dft_table(n_dev, size_a, size_a)
    outcome = contract("nk,kbc->nbc", back_cos, real_part) - contract(
        "nk,kbc->nbc", back_sin, imag_part
    )
    outcome = (outcome * (1.0 / padded)).astype(jnp.bfloat16)
    returned = lax.all_to_all(outcome, ("outer", "inner"), split_axis=0, concat_axis=0, tiled=True)
    return returned.transpose(1, 0, 2).reshape(row_count, channels)


def on_device(query, key_in, value_in, filters, group_index, skip_gain):
    mixed = (key_in.astype(jnp.float32) * value_in.astype(jnp.float32)).astype(jnp.bfloat16)
    convolved = by_channels(mixed, filters, group_index)
    mixed_wide = mixed.astype(jnp.float32)
    return (query.astype(jnp.float32) * (convolved + skip_gain[None, :] * mixed_wide)).astype(
        jnp.bfloat16
    )


def solution(mesh):
    placed = (
        P(("outer", "inner"), None),
        P(("outer", "inner"), None),
        P(("outer", "inner"), None),
        P(("outer", "inner"), None),
        P(),
        P(),
    )
    return jax.shard_map(
        on_device,
        mesh=mesh,
        in_specs=placed,
        out_specs=P(("outer", "inner"), None),
        check_vma=False,
    )
```

profile of v0, /device:TPU:0, one launch (start us, length us, event | category | flops | bytes accessed | tf_op | source)
XLA Modules:
  0.0 112.1 jit_solution(11701815625652275968)
XLA Ops:
  0.0 0.0 copy-start.4
  0.0 0.7 fusion.77
  0.7 0.7 compare_and_fusion
  1.4 1.3 %copy.53 = bf16[128,2048]{0,1:T(8,128)(2,1)S(1)} copy(bf16[128,2048]{1,0:T(8,128)(2,1)} %param.7) | data formatting | bytes 1048576 | tf_op args[1]
  2.7 1.3 %copy.54 = bf16[128,2048]{0,1:T(8,128)(2,1)S(1)} copy(bf16[128,2048]{1,0:T(8,128)(2,1)} %param.8) | data formatting | bytes 1048576 | tf_op args[2]
  4.1 0.0 copy-done.4
  4.1 0.1 copy.55
  4.2 0.1 broadcast_in_dim.14
  4.3 0.1 multiply_convert_fusion
  4.4 6.2 %gather_fusion = bf16[2048,128]{1,0:T(8,128)(2,1)S(1)} fusion(bf16[128,128]{0,1:T(8,128)(2,1)S(1)} %copy.55, s32[2048]{0:T(1024)S(1)} %fusion.77), kind=kCustom, calls=%fused_computation | custom fusion | bytes 1056768 | tf_op jit(solution)/shard_map/jit(_take)/gather | solution.py:60
  10.6 0.3 broadcast_select_fusion
  11.0 0.1 maximum_bitcast_fusion
  11.1 1.1 copy.56
  12.1 7.3 %all-to-all-start = ((bf16[32,128,2,64]{1,3,2,0:T(8,128)(2,1)}), bf16[32,128,2,64]{1,3,2,0:T(8,128)(2,1)S(1)}, u32[]{:S(2)}, u32[]{:S(2)}) async-start(bf16[32,128,2,64]{1,3,2,0:T(8,128)(2,1)} %copy.56), calls=%async_computation | async-start | bytes 2097152 | tf_op jit(solution)/shard_map/all_to_all | solution.py:63
  19.4 0.1 fusion.63
  19.6 0.1 copy.58
  19.7 0.1 copy.60
  19.8 25.9 %all-to-all-done = bf16[32,128,2,64]{1,3,2,0:T(8,128)(2,1)S(1)} async-done(((bf16[32,128,2,64]{1,3,2,0:T(8,128)(2,1)}), bf16[32,128,2,64]{1,3,2,0:T(8,128)(2,1)S(1)}, u32[]{:S(2)}, u32[]{:S(2)}) %all-to-all-start) | async-done | bytes 1048608 | tf_op jit(solution)/shard_map/all_to_all | solution.py:63
  45.7 1.0 copy.57
  46.6 1.4 %fusion.56 = f32[64,128,128]{2,0,1:T(8,128)S(1)} fusion(bf16[32,128,128]{2,0,1:T(8,128)(2,1)S(1)} %copy.57), kind=kOutput, calls=%fused_computation.70 | convolution fusion | flops 201355264 | bytes 5242880 | tf_op jit(solution)/shard_map/kn,nbc->kbc/dot_general | solution.py:10
  48.0 5.8 %multiply_add_fusion = (f32[64,128,128]{2,0,1:T(8,128)}, f32[64,128,128]{2,0,1:T(8,128)}) fusion(f32[64,128,128]{2,0,1:T(8,128)S(1)} %fusion.56, f32[64,128]{0,1:T(8,128)S(1)} %copy.60, f32[64,128]{0,1:T(8,128)S(1)} %copy.58, bf16[32,128,128]{2,0,1:T(8,128)(2,1)S(1)} %copy.57), kind=kOutput, calls=%fused_computation.4 | convolution fusion | flops 208695296 | bytes 13697024 | tf_op jit(solution)/shard_map/kn,nbc->kbc/dot_general | solution.py:10
  53.8 5.4 %copy.61 = f32[64,128,128]{1,2,0:T(8,128)} copy(f32[64,128,128]{2,0,1:T(8,128)} %get-tuple-element.5) | data formatting | bytes 8388608 | tf_op jit(solution)/shard_map/add | solution.py:37
  59.2 6.2 %fusion.28 = f32[64,128,128]{2,1,0:T(8,128)} fusion(f32[64,128,128]{1,2,0:T(8,128)} %copy.61), kind=kOutput, calls=%fused_computation.40 | convolution fusion | flops 805535744 | bytes 8388608 | tf_op jit(solution)/shard_map/qb,kbc->kqc/dot_general | solution.py:10
  65.4 5.4 %copy.62 = f32[64,128,128]{1,2,0:T(8,128)} copy(f32[64,128,128]{2,0,1:T(8,128)} %get-tuple-element.6) | data formatting | bytes 8388608 | tf_op jit(solution)/shard_map/sub | solution.py:38
  70.8 0.0 copy-start.1
  70.8 4.4 %fusion.26 = f32[64,128,128]{2,1,0:T(8,128)S(1)} fusion(f32[64,128,128]{1,2,0:T(8,128)} %copy.62), kind=kOutput, calls=%fused_computation.38 | convolution fusion | flops 805535744 | bytes 8388608 | tf_op jit(solution)/shard_map/qb,kbc->kqc/dot_general | solution.py:10
  75.2 0.0 copy-done.1
  75.3 0.3 copy-done.2
  75.5 2.2 %subtract_bitcast_fusion = f32[64,128,128]{1,2,0:T(8,128)S(1)} fusion(f32[64,128,128]{2,1,0:T(8,128)S(1)} %copy-done.2, f32[64,128,128]{1,2,0:T(8,128)S(1)} %copy-done.1), kind=kOutput, calls=%fused_computation.2 | convolution fusion | flops 807632896 | bytes 12582912 | tf_op jit(solution)/shard_map/qb,kbc->kqc/dot_general | solution.py:10
  77.8 0.0 copy-done
  77.8 2.1 %add_bitcast_fusion = f32[64,128,128]{1,2,0:T(8,128)S(1)} fusion(f32[64,128,128]{2,1,0:T(8,128)S(1)} %fusion.26, f32[64,128,128]{1,2,0:T(8,128)S(1)} %copy-done), kind=kOutput, calls=%fused_computation.1 | convolution fusion | flops 807632896 | bytes 12582912 | tf_op jit(solution)/shard_map/qb,kbc->kqc/dot_general | solution.py:10
  79.9 1.4 %multiply_add_fusion.1 = (f32[64,128,64]{1,2,0:T(8,128)S(1)}, f32[64,128,64]{1,2,0:T(8,128)S(1)}) fusion(f32[64,128,128]{1,2,0:T(8,128)S(1)} %add_bitcast_fusion, f32[64,128,128]{1,2,0:T(8,128)S(1)} %subtract_bitcast_fusion), kind=kLoop, calls=%fused_computation.11 | loop fusion | flops 3145728 | bytes 12582912 | tf_op jit(solution)/shard_map/add | solution.py:83
  81.3 1.2 %fusion.22 = f32[64,64,128]{2,1,0:T(8,128)S(1)} fusion(f32[64,128,64]{1,2,0:T(8,128)S(1)} %get-tuple-element.7), kind=kOutput, calls=%fused_computation.34 | convolution fusion | flops 402882560 | bytes 4194304 | tf_op jit(solution)/shard_map/bq,kqc->kbc/dot_general | solution.py:10
  82.6 1.2 %fusion.24 = f32[64,64,128]{2,1,0:T(8,128)S(1)} fusion(f32[64,128,64]{1,2,0:T(8,128)S(1)} %get-tuple-element.8), kind=kOutput, calls=%fused_computation.36 | convolution fusion | flops 402882560 | bytes 4194304 | tf_op jit(solution)/shard_map/bq,kqc->kbc/dot_general | solution.py:10
  83.8 1.2 %convolution_add_fusion = f32[64,64,128]{2,1,0:T(8,128)S(1)} fusion(f32[64,64,128]{2,1,0:T(8,128)S(1)} %fusion.22, f32[64,128,64]{1,2,0:T(8,128)S(1)} %get-tuple-element.8), kind=kOutput, calls=%fused_computation.13 | convolution fusion | flops 403406848 | bytes 6291456 | tf_op jit(solution)/shard_map/bq,kqc->kbc/dot_general | solution.py:10
  85.1 1.5 %subtract_bitcast_fusion.1 = (f32[64,128,64]{1,2,0:T(8,128)S(1)}, f32[64,128,64]{1,2,0:T(8,128)S(1)}) fusion(f32[64,64,128]{2,1,0:T(8,128)S(1)} %convolution_add_fusion, f32[64,128]{1,0:T(8,128)S(1)} %get-tuple-element.11, f32[64,128]{1,0:T(8,128)S(1)} %get-tuple-element.12, f32[64,64,128]{2,1,0:T(8,128)S(1)} %fusion.24, ...), kind=kOutput, calls=%fused_computation.10 | convolution fusion | flops 406552576 | bytes 10551296 | tf_op jit(solution)/shard_map/bq,kqc->kbc/dot_general | solution.py:10
  86.6 2.1 %fusion = f32[32,128,64]{1,0,2:T(8,128)S(1)} fusion(f32[64,128,64]{1,2,0:T(8,128)S(1)} %get-tuple-element.10), kind=kOutput, calls=%fused_computation.5 | convolution fusion | flops 100691968 | bytes 3145728 | tf_op jit(solution)/shard_map/nk,kbc->nbc/dot_general | solution.py:10
  88.7 0.0 copy-start.3
  88.7 1.8 %fusion.10 = bf16[32,128,64]{1,0,2:T(8,128)(2,1)S(1)} fusion(f32[32,128,64]{1,0,2:T(8,128)S(1)} %fusion, f32[64,128,64]{1,2,0:T(8,128)S(1)} %get-tuple-element.9), kind=kOutput, calls=%fused_computation.17 | convolution fusion | flops 101478400 | bytes 3670016 | tf_op jit(solution)/shard_map/nk,kbc->nbc/dot_general | solution.py:10
  90.6 0.0 copy-start.5
  90.6 1.0 copy.67
  91.6 3.6 %all-to-all-start.1 = ((bf16[32,128,64]{1,2,0:T(8,128)(2,1)}), bf16[32,128,64]{1,2,0:T(8,128)(2,1)S(1)}, u32[]{:S(2)}, u32[]{:S(2)}) async-start(bf16[32,128,64]{1,2,0:T(8,128)(2,1)} %copy.67), calls=%async_computation.1 | async-start | bytes 1048576 | tf_op jit(solution)/shard_map/all_to_all | solution.py:91
  95.2 0.0 copy-done.3
  95.2 0.3 copy.52
  95.5 15.3 %all-to-all-done.1 = bf16[32,128,64]{1,2,0:T(8,128)(2,1)S(1)} async-done(((bf16[32,128,64]{1,2,0:T(8,128)(2,1)}), bf16[32,128,64]{1,2,0:T(8,128)(2,1)S(1)}, u32[]{:S(2)}, u32[]{:S(2)}) %all-to-all-start.1) | async-done | bytes 524320 | tf_op jit(solution)/shard_map/all_to_all | solution.py:91
  110.7 0.0 copy-done.5
  110.8 0.3 fusion.14
  111.1 1.0 copy.68
  (2 shorter events, 0.0 us)
Async XLA Ops:
  0.0 4.1 %copy-start.4 = (bf16[128,128]{1,0:T(8,128)(2,1)S(1)}, bf16[128,128]{1,0:T(8,128)(2,1)}, u32[]{:S(2)}) copy-start(bf16[128,128]{1,0:T(8,128)(2,1)} %param.9) | copy-start | bytes 98308
  12.1 33.5 %all-to-all-start = ((bf16[32,128,2,64]{1,3,2,0:T(8,128)(2,1)}), bf16[32,128,2,64]{1,3,2,0:T(8,128)(2,1)S(1)}, u32[]{:S(2)}, u32[]{:S(2)}) async-start(bf16[32,128,2,64]{1,3,2,0:T(8,128)(2,1)} %copy.56), calls=%async_computation | async-start | bytes 2097152 | tf_op jit(solution)/shard_map/all_to_all | solution.py:63
  70.8 4.4 %copy-start.1 = (f32[64,128,128]{1,2,0:T(8,128)S(1)}, f32[64,128,128]{1,2,0:T(8,128)}, u32[]{:S(2)}) copy-start(f32[64,128,128]{1,2,0:T(8,128)} %copy.62) | copy-start | bytes 12582916
  70.8 4.7 %copy-start.2 = (f32[64,128,128]{2,1,0:T(8,128)S(1)}, f32[64,128,128]{2,1,0:T(8,128)}, u32[]{:S(2)}) copy-start(f32[64,128,128]{2,1,0:T(8,128)} %fusion.28) | copy-start | bytes 12582916
  75.5 2.2 %copy-start = (f32[64,128,128]{1,2,0:T(8,128)S(1)}, f32[64,128,128]{1,2,0:T(8,128)}, u32[]{:S(2)}) copy-start(f32[64,128,128]{1,2,0:T(8,128)} %copy.61) | copy-start | bytes 12582916
  88.7 6.5 %copy-start.3 = (bf16[128,2048]{1,0:T(8,128)(2,1)S(1)}, bf16[128,2048]{1,0:T(8,128)(2,1)}, u32[]{:S(2)}) copy-start(bf16[128,2048]{1,0:T(8,128)(2,1)} %param.6) | copy-start | bytes 1572868
  90.6 20.2 %copy-start.5 = (f32[2048]{0:T(1024)S(1)}, f32[2048]{0:T(1024)}, u32[]{:S(2)}) copy-start(f32[2048]{0:T(1024)} %param.11) | copy-start | bytes 24580
  91.6 19.2 %all-to-all-start.1 = ((bf16[32,128,64]{1,2,0:T(8,128)(2,1)}), bf16[32,128,64]{1,2,0:T(8,128)(2,1)S(1)}, u32[]{:S(2)}, u32[]{:S(2)}) async-start(bf16[32,128,64]{1,2,0:T(8,128)(2,1)} %copy.67), calls=%async_computation.1 | async-start | bytes 1048576 | tf_op jit(solution)/shard_map/all_to_all | solution.py:91
where the time goes:
time: 113 us; the launch traced here: 112 us
  waiting for transfers between devices  41.1 us (36%)
  matrix products  31.2 us (28%)
  local copies, waits for them, and re-layouts  24.6 us (22%)
  starting transfers between devices  10.9 us (10%)
  other arithmetic  3.93 us (3%)
    dot_general x12, matrix products, contract(): jnp.einsum(pattern, left_op, right_op, precision=lax.Precision.HIGH, pref...  31.2 us
    all_to_all x1, waiting for transfers between devices, by_channels(): lax.all_to_all(sent, ('outer', 'inner'), split_axis=0, concat_axis=0, til...  25.9 us
    all_to_all x1, waiting for transfers between devices, by_channels(): lax.all_to_all(outcome, ('outer', 'inner'), split_axis=0, concat_axis=0,...  15.3 us
    all_to_all x1, starting transfers between devices, by_channels(): lax.all_to_all(sent, ('outer', 'inner'), split_axis=0, concat_axis=0, til...  7.3 us
    gather x1, local copies, waits for them, and re-layouts, by_channels(): chan_filters = jnp.take(filters, group_index, axis=1)  6.18 us
    add x1, local copies, waits for them, and re-layouts, rotate(): real_part * cosine + imag_part * sine_part  5.43 us
    sub x1, local copies, waits for them, and re-layouts, rotate(): imag_part * cosine - real_part * sine_part  5.4 us
    all_to_all x1, starting transfers between devices, by_channels(): lax.all_to_all(outcome, ('outer', 'inner'), split_axis=0, concat_axis=0,...  3.63 us
  transfers between devices with their start and end apart: 2, of which 2 were waited for; matrix products, arithmetic and copies ran while one was open for 1% of the time, Pallas kernels for 0%

commit v1 on v0

--- a/solution.py
+++ b/solution.py
@@ -63,8 +63,9 @@
     got = lax.all_to_all(sent, ("outer", "inner"), split_axis=0, concat_axis=0, tiled=True)
     stacked = got.reshape(n_dev, row_count, 2 * own_width).astype(jnp.float32)
     first_cos, first_sin = dft_table(size_a, n_dev, size_a)
-    real_part = contract("kn,nbc->kbc", first_cos, stacked)
-    imag_part = -contract("kn,nbc->kbc", first_sin, stacked)
+    first = contract("kn,nbc->kbc", jnp.concatenate([first_cos, -first_sin], axis=0), stacked)
+    real_part = first[:size_a]
+    imag_part = first[size_a:]
     twiddle = angles_of(
         jnp.arange(size_a, dtype=jnp.int32)[:, None]
         * jnp.arange(row_count, dtype=jnp.int32)[None, :],
@@ -72,20 +73,31 @@
     )[:, :, None]
     real_part, imag_part = rotate(real_part, imag_part, twiddle, -1)
     second_cos, second_sin = dft_table(row_count, row_count, row_count)
-    real_part, imag_part = transform(
-        "qb,kbc->kqc", second_cos, second_sin, real_part, imag_part, -1
-    )
+    wide_cos = jnp.broadcast_to(second_cos[None], (size_a, row_count, row_count))
+    wide_sin = jnp.broadcast_to(second_sin[None], (size_a, row_count, row_count))
+    both = jnp.concatenate([real_part, imag_part], axis=2)
+    by_cos = contract("kqb,kbc->kqc", wide_cos, both)
+    by_sin = contract("kqb,kbc->kqc", wide_sin, both)
+    width = 2 * own_width
+    real_part = by_cos[:, :, :width] + by_sin[:, :, width:]
+    imag_part = by_cos[:, :, width:] - by_sin[:, :, :width]
     data_real = real_part[:, :, :own_width]
     data_imag = imag_part[:, :, :own_width]
     filter_real = real_part[:, :, own_width:]
     filter_imag = imag_part[:, :, own_width:]
     spec_real = data_real * filter_real - data_imag * filter_imag
     spec_imag = data_real * filter_imag + data_imag * filter_real
-    real_part, imag_part = transform("bq,kqc->kbc", second_cos, second_sin, spec_real, spec_imag, 1)
+    both = jnp.concatenate([spec_real, spec_imag], axis=2)
+    by_cos = contract("kbq,kqc->kbc", wide_cos, both)
+    by_sin = contract("kbq,kqc->kbc", wide_sin, both)
+    real_part = by_cos[:, :, :own_width] - by_sin[:, :, own_width:]
+    imag_part = by_cos[:, :, own_width:] + by_sin[:, :, :own_width]
     real_part, imag_part = rotate(real_part, imag_part, twiddle, 1)
     back_cos, back_sin = dft_table(n_dev, size_a, size_a)
-    outcome = contract("nk,kbc->nbc", back_cos, real_part) - contract(
-        "nk,kbc->nbc", back_sin, imag_part
+    outcome = contract(
+        "nk,kbc->nbc",
+        jnp.concatenate([back_cos, -back_sin], axis=1),
+        jnp.concatenate([real_part, imag_part], axis=0),
     )
     outcome = (outcome * (1.0 / padded)).astype(jnp.bfloat16)
     returned = lax.all_to_all(outcome, ("outer", "inner"), split_axis=0, concat_axis=0, tiled=True)

time: 113 us -> 127 us (1.12)
  other arithmetic: 3.93 us -> 24.4 us
  local copies, waits for them, and re-layouts: 24.6 us -> 14.3 us
  matrix products: 31.2 us -> 36 us
    add x1 -> x2, other arithmetic: 1.44 us -> 12.8 us  [the longest x1 10 us: by_channels(): real_part = by_cos[:, :, :width] + by_sin[:, :, width:]]
    sub x0 -> x2, other arithmetic: none -> 7.15 us  [the longest x1 5.94 us: by_channels(): spec_real = data_real * filter_real - data_imag * filter_imag]
    add x1 -> x0, local copies, waits for them, and re-layouts: 5.43 us -> none  [rotate(): real_part * cosine + imag_part * sine_part]
    sub x1 -> x0, local copies, waits for them, and re-layouts: 5.4 us -> none  [rotate(): imag_part * cosine - real_part * sine_part]
    dot_general x12 -> x6, matrix products: 31.2 us -> 36 us  [contract(): jnp.einsum(pattern, left_op, right_op, precision=lax.Precision.HIGH, pref...]
    concatenate x0 -> x2, other arithmetic: none -> 1.3 us  [the longest x1 0.99 us: by_channels(): both = jnp.concatenate([real_part, imag_part], axis=2)]
    unnamed x16 -> x8, local copies, waits for them, and re-layouts: 3.32 us -> 3.77 us
where the time goes in v1:
time: 127 us; the launch traced here: 126 us
  waiting for transfers between devices  40.4 us (32%)
  matrix products  36 us (28%)
  other arithmetic  24.4 us (19%)
  local copies, waits for them, and re-layouts  14.3 us (11%)
  starting transfers between devices  10.9 us (9%)
    dot_general x6, matrix products, contract(): jnp.einsum(pattern, left_op, right_op, precision=lax.Precision.HIGH, pref...  36 us
    all_to_all x1, waiting for transfers between devices, by_channels(): lax.all_to_all(sent, ('outer', 'inner'), split_axis=0, concat_axis=0, til...  25.2 us
    all_to_all x1, waiting for transfers between devices, by_channels(): lax.all_to_all(outcome, ('outer', 'inner'), split_axis=0, concat_axis=0,...  15.3 us
    add x1, other arithmetic, by_channels(): real_part = by_cos[:, :, :width] + by_sin[:, :, width:]  10 us
    all_to_all x1, starting transfers between devices, by_channels(): lax.all_to_all(sent, ('outer', 'inner'), split_axis=0, concat_axis=0, til...  7.3 us
    gather x1, local copies, waits for them, and re-layouts, by_channels(): chan_filters = jnp.take(filters, group_index, axis=1)  6.18 us
    sub x1, other arithmetic, by_channels(): spec_real = data_real * filter_real - data_imag * filter_imag  5.94 us
    unnamed x8, local copies, waits for them, and re-layouts  3.77 us
  transfers between devices with their start and end apart: 2, of which 2 were waited for; matrix products, arithmetic and copies ran while one was open for 1% of the time, Pallas kernels for 0%

profile of v1, /device:TPU:0, one launch (start us, length us, event | category | flops | bytes accessed | tf_op | source)
XLA Modules:
  0.0 126.3 jit_solution(3957092599746837402)
XLA Ops:
  0.0 0.7 fusion.55
  0.7 0.7 compare_and_fusion
  1.4 1.3 %copy.48 = bf16[128,2048]{0,1:T(8,128)(2,1)S(1)} copy(bf16[128,2048]{1,0:T(8,128)(2,1)} %param.7) | data formatting | bytes 1048576 | tf_op args[1]
  2.7 1.3 %copy.49 = bf16[128,2048]{0,1:T(8,128)(2,1)S(1)} copy(bf16[128,2048]{1,0:T(8,128)(2,1)} %param.8) | data formatting | bytes 1048576 | tf_op args[2]
  4.0 0.9 copy.50
  4.9 0.1 broadcast_in_dim.23
  5.0 0.1 multiply_convert_fusion
  5.1 6.2 %gather_fusion = bf16[2048,128]{1,0:T(8,128)(2,1)S(1)} fusion(bf16[128,128]{0,1:T(8,128)(2,1)S(1)} %copy.50, s32[2048]{0:T(1024)S(1)} %fusion.55), kind=kCustom, calls=%fused_computation | custom fusion | bytes 1056768 | tf_op jit(solution)/shard_map/jit(_take)/gather | solution.py:60
  11.3 0.3 broadcast_select_fusion
  11.7 0.1 maximum_bitcast_fusion
  11.8 1.1 copy.51
  12.9 7.3 %all-to-all-start = ((bf16[32,128,2,64]{1,3,2,0:T(8,128)(2,1)}), bf16[32,128,2,64]{1,3,2,0:T(8,128)(2,1)S(1)}, u32[]{:S(2)}, u32[]{:S(2)}) async-start(bf16[32,128,2,64]{1,3,2,0:T(8,128)(2,1)} %copy.51), calls=%async_computation | async-start | bytes 2097152 | tf_op jit(solution)/shard_map/all_to_all | solution.py:63
  20.2 0.1 fusion.45
  20.3 0.1 copy.53
  20.4 0.1 copy.54
  20.5 0.1 sine_negate_fusion
  20.6 0.1 sine_negate_fusion.1
  20.7 0.3 fusion.32
  21.0 0.3 fusion.31
  21.2 25.2 %all-to-all-done = bf16[32,128,2,64]{1,3,2,0:T(8,128)(2,1)S(1)} async-done(((bf16[32,128,2,64]{1,3,2,0:T(8,128)(2,1)}), bf16[32,128,2,64]{1,3,2,0:T(8,128)(2,1)S(1)}, u32[]{:S(2)}, u32[]{:S(2)}) %all-to-all-start) | async-done | bytes 1048608 | tf_op jit(solution)/shard_map/all_to_all | solution.py:63
  46.4 1.0 copy.52
  47.4 2.5 %fusion.42 = f32[128,128,128]{2,0,1:T(8,128)S(1)} fusion(bf16[32,128,128]{2,0,1:T(8,128)(2,1)S(1)} %copy.52, f32[64,32]{0,1:T(8,128)S(1)} %get-tuple-element.13, f32[64,32]{0,1:T(8,128)S(1)} %get-tuple-element.14), kind=kOutput, calls=%fused_computation.71 | convolution fusion | flops 402657280 | bytes 9453568 | tf_op jit(solution)/shard_map/kn,nbc->kbc/dot_general | solution.py:10
  49.9 2.8 %multiply_add_fusion.1 = (f32[64,128,128]{2,0,1:T(8,128)S(1)}, f32[64,128,128]{2,0,1:T(8,128)S(1)}) fusion(f32[128,128,128]{2,0,1:T(8,128)S(1)} %fusion.42, f32[64,128]{0,1:T(8,128)S(1)} %copy.54, f32[64,128]{0,1:T(8,128)S(1)} %copy.53), kind=kLoop, calls=%fused_computation.15 | loop fusion | flops 6291456 | bytes 16842752 | tf_op jit(solution)/shard_map/add | solution.py:37
  52.7 1.0 pad_maximum_fusion
  53.7 10.3 %fusion.2 = f32[64,128,256]{2,1,0:T(8,128)} fusion(f32[64,128,256]{2,0,1:T(8,128)S(1)} %pad_maximum_fusion, f32[128,128]{1,0:T(8,128)S(1)} %fusion.32), kind=kOutput, calls=%fused_computation.4 | convolution fusion | flops 1610612736 | bytes 16842752 | tf_op jit(solution)/shard_map/kqb,kbc->kqc/dot_general | solution.py:10
  64.0 10.3 %fusion = f32[64,128,256]{2,1,0:T(8,128)} fusion(f32[64,128,256]{2,0,1:T(8,128)S(1)} %pad_maximum_fusion, f32[128,128]{1,0:T(8,128)S(1)} %fusion.31), kind=kOutput, calls=%fused_computation.2 | convolution fusion | flops 1610612736 | bytes 16842752 | tf_op jit(solution)/shard_map/kqb,kbc->kqc/dot_general | solution.py:10
  74.3 10.0 %slice_add_fusion = (f32[64,128,128]{2,1,0:T(8,128)S(1)}, f32[64,128,128]{2,1,0:T(8,128)}) fusion(f32[64,128,256]{2,1,0:T(8,128)} %fusion, f32[64,128,256]{2,1,0:T(8,128)} %fusion.2), kind=kLoop, calls=%fused_computation.7 | loop fusion | flops 2097152 | bytes 25165824 | tf_op jit(solution)/shard_map/add | solution.py:82
  84.4 5.9 %multiply_subtract_fusion = (f32[64,128,64]{2,1,0:T(8,128)S(1)}, f32[64,128,64]{2,1,0:T(8,128)S(1)}) fusion(f32[64,128,128]{2,1,0:T(8,128)} %get-tuple-element.6, f32[64,128,128]{2,1,0:T(8,128)S(1)} %get-tuple-element.5), kind=kLoop, calls=%fused_computation.13 | loop fusion | flops 3145728 | bytes 12582912 | tf_op jit(solution)/shard_map/sub | solution.py:88
  90.3 4.6 %fusion.9 = f32[64,128,128]{1,2,0:T(8,128)S(1)} fusion(f32[128,128]{1,0:T(8,128)S(1)} %fusion.32, f32[64,128,64]{2,1,0:T(8,128)S(1)} %get-tuple-element.12, f32[64,128,64]{2,1,0:T(8,128)S(1)} %get-tuple-element.11), kind=kOutput, calls=%fused_computation.23 | convolution fusion | flops 806354944 | bytes 8454144 | tf_op jit(solution)/shard_map/kbq,kqc->kbc/dot_general | solution.py:10
  95.0 4.6 %fusion.6 = f32[64,128,128]{1,2,0:T(8,128)S(1)} fusion(f32[128,128]{1,0:T(8,128)S(1)} %fusion.31, f32[64,128,64]{2,1,0:T(8,128)S(1)} %get-tuple-element.12, f32[64,128,64]{2,1,0:T(8,128)S(1)} %get-tuple-element.11), kind=kOutput, calls=%fused_computation.20 | convolution fusion | flops 806354944 | bytes 8454144 | tf_op jit(solution)/shard_map/kbq,kqc->kbc/dot_general | solution.py:10
  99.6 1.2 multiply_subtract_fusion.2
  100.8 0.3 pad_maximum_fusion.2
  101.1 0.0 copy-start
  101.1 0.0 copy-start.1
  101.1 3.6 %fusion.15 = bf16[32,128,64]{1,0,2:T(8,128)(2,1)S(1)} fusion(f32[128,128,64]{1,2,0:T(8,128)S(1)} %pad_maximum_fusion.2, f32[32,64]{1,0:T(8,128)S(1)} %get-tuple-element.17, f32[32,64]{1,0:T(8,128)S(1)} %get-tuple-element.18), kind=kOutput, calls=%fused_computation.27 | convolution fusion | flops 201854976 | bytes 4734976 | tf_op jit(solution)/shard_map/nk,kbc->nbc/dot_general | solution.py:10
  104.7 1.0 copy.60
  105.7 3.6 %all-to-all-start.1 = ((bf16[32,128,64]{1,2,0:T(8,128)(2,1)}), bf16[32,128,64]{1,2,0:T(8,128)(2,1)S(1)}, u32[]{:S(2)}, u32[]{:S(2)}) async-start(bf16[32,128,64]{1,2,0:T(8,128)(2,1)} %copy.60), calls=%async_computation.1 | async-start | bytes 1048576 | tf_op jit(solution)/shard_map/all_to_all | solution.py:103
  109.4 0.0 copy-done
  109.4 0.3 copy.47
  109.6 15.3 %all-to-all-done.1 = bf16[32,128,64]{1,2,0:T(8,128)(2,1)S(1)} async-done(((bf16[32,128,64]{1,2,0:T(8,128)(2,1)}), bf16[32,128,64]{1,2,0:T(8,128)(2,1)S(1)}, u32[]{:S(2)}, u32[]{:S(2)}) %all-to-all-start.1) | async-done | bytes 524320 | tf_op jit(solution)/shard_map/all_to_all | solution.py:103
  124.9 0.0 copy-done.1
  124.9 0.3 fusion.19
  125.3 1.0 copy.61
Async XLA Ops:
  12.9 33.5 %all-to-all-start = ((bf16[32,128,2,64]{1,3,2,0:T(8,128)(2,1)}), bf16[32,128,2,64]{1,3,2,0:T(8,128)(2,1)S(1)}, u32[]{:S(2)}, u32[]{:S(2)}) async-start(bf16[32,128,2,64]{1,3,2,0:T(8,128)(2,1)} %copy.51), calls=%async_computation | async-start | bytes 2097152 | tf_op jit(solution)/shard_map/all_to_all | solution.py:63
  101.1 8.2 %copy-start = (bf16[128,2048]{1,0:T(8,128)(2,1)S(1)}, bf16[128,2048]{1,0:T(8,128)(2,1)}, u32[]{:S(2)}) copy-start(bf16[128,2048]{1,0:T(8,128)(2,1)} %param.6) | copy-start | bytes 1572868
  101.1 23.8 %copy-start.1 = (f32[2048]{0:T(1024)S(1)}, f32[2048]{0:T(1024)}, u32[]{:S(2)}) copy-start(f32[2048]{0:T(1024)} %param.11) | copy-start | bytes 24580
  105.7 19.2 %all-to-all-start.1 = ((bf16[32,128,64]{1,2,0:T(8,128)(2,1)}), bf16[32,128,64]{1,2,0:T(8,128)(2,1)S(1)}, u32[]{:S(2)}, u32[]{:S(2)}) async-start(bf16[32,128,64]{1,2,0:T(8,128)(2,1)} %copy.60), calls=%async_computation.1 | async-start | bytes 1048576 | tf_op jit(solution)/shard_map/all_to_all | solution.py:103

commit v2 on v0

--- a/solution.py
+++ b/solution.py
@@ -57,39 +57,43 @@
     own_width = channels // n_dev
     size_a = 2 * n_dev
     padded = size_a * row_count
-    chan_filters = jnp.take(filters, group_index, axis=1)
-    sent = jnp.stack([mixed, chan_filters], axis=1).reshape(row_count, 2, n_dev, own_width)
-    sent = sent.transpose(2, 0, 1, 3)
+    chan_filters = jnp.take(filters.T, group_index, axis=0)
+    sent = jnp.stack([mixed.T, chan_filters], axis=0).reshape(2, n_dev, own_width, row_count)
+    sent = sent.transpose(1, 0, 2, 3)
     got = lax.all_to_all(sent, ("outer", "inner"), split_axis=0, concat_axis=0, tiled=True)
-    stacked = got.reshape(n_dev, row_count, 2 * own_width).astype(jnp.float32)
+    stacked = got.reshape(n_dev, 2 * own_width, row_count).astype(jnp.float32)
     first_cos, first_sin = dft_table(size_a, n_dev, size_a)
-    real_part = contract("kn,nbc->kbc", first_cos, stacked)
-    imag_part = -contract("kn,nbc->kbc", first_sin, stacked)
+    first = contract("kn,ncb->kcb", jnp.concatenate([first_cos, -first_sin], axis=0), stacked)
     twiddle = angles_of(
         jnp.arange(size_a, dtype=jnp.int32)[:, None]
         * jnp.arange(row_count, dtype=jnp.int32)[None, :],
         padded,
-    )[:, :, None]
-    real_part, imag_part = rotate(real_part, imag_part, twiddle, -1)
+    )[:, None, :]
+    real_part, imag_part = rotate(first[:size_a], first[size_a:], twiddle, -1)
     second_cos, second_sin = dft_table(row_count, row_count, row_count)
-    real_part, imag_part = transform(
-        "qb,kbc->kqc", second_cos, second_sin, real_part, imag_part, -1
-    )
-    data_real = real_part[:, :, :own_width]
-    data_imag = imag_part[:, :, :own_width]
-    filter_real = real_part[:, :, own_width:]
-    filter_imag = imag_part[:, :, own_width:]
+    table = jnp.concatenate([second_cos, second_sin], axis=1)
+    prod = contract("kcb,bq->kcq", jnp.concatenate([real_part, imag_part], axis=0), table)
+    real_part = prod[:size_a, :, :row_count] + prod[size_a:, :, row_count:]
+    imag_part = prod[size_a:, :, :row_count] - prod[:size_a, :, row_count:]
+    data_real = real_part[:, :own_width]
+    data_imag = imag_part[:, :own_width]
+    filter_real = real_part[:, own_width:]
+    filter_imag = imag_part[:, own_width:]
     spec_real = data_real * filter_real - data_imag * filter_imag
     spec_imag = data_real * filter_imag + data_imag * filter_real
-    real_part, imag_part = transform("bq,kqc->kbc", second_cos, second_sin, spec_real, spec_imag, 1)
+    prod = contract("kcq,qb->kcb", jnp.concatenate([spec_real, spec_imag], axis=0), table)
+    real_part = prod[:size_a, :, :row_count] - prod[size_a:, :, row_count:]
+    imag_part = prod[size_a:, :, :row_count] + prod[:size_a, :, row_count:]
     real_part, imag_part = rotate(real_part, imag_part, twiddle, 1)
     back_cos, back_sin = dft_table(n_dev, size_a, size_a)
-    outcome = contract("nk,kbc->nbc", back_cos, real_part) - contract(
-        "nk,kbc->nbc", back_sin, imag_part
+    outcome = contract(
+        "nk,kcb->ncb",
+        jnp.concatenate([back_cos, -back_sin], axis=1),
+        jnp.concatenate([real_part, imag_part], axis=0),
     )
     outcome = (outcome * (1.0 / padded)).astype(jnp.bfloat16)
     returned = lax.all_to_all(outcome, ("outer", "inner"), split_axis=0, concat_axis=0, tiled=True)
-    return returned.transpose(1, 0, 2).reshape(row_count, channels)
+    return returned.reshape(channels, row_count).T
 
 
 def on_device(query, key_in, value_in, filters, group_index, skip_gain):

time: 113 us -> 116 us (1.027)
  other arithmetic: 3.93 us -> 23.7 us
  local copies, waits for them, and re-layouts: 24.6 us -> 13.8 us
  matrix products: 31.2 us -> 26.3 us
    add x1 -> x2, other arithmetic: 1.44 us -> 13.2 us  [the longest x1 10 us: by_channels(): real_part = prod[:size_a, :, :row_count] + prod[size_a:, :, row_count:]]
    add x1 -> x0, local copies, waits for them, and re-layouts: 5.43 us -> none  [rotate(): real_part * cosine + imag_part * sine_part]
    sub x1 -> x0, local copies, waits for them, and re-layouts: 5.4 us -> none  [rotate(): imag_part * cosine - real_part * sine_part]
    dot_general x12 -> x4, matrix products: 31.2 us -> 26.3 us  [contract(): jnp.einsum(pattern, left_op, right_op, precision=lax.Precision.HIGH, pref...]
    sub x0 -> x2, other arithmetic: none -> 3.97 us  [the longest x1 3.21 us: by_channels(): spec_real = data_real * filter_real - data_imag * filter_imag]
    concatenate x0 -> x2, other arithmetic: none -> 3.62 us  [the longest x1 3.04 us: by_channels(): jnp.concatenate([real_part, imag_part], axis=0)]
    unnamed x16 -> x8, local copies, waits for them, and re-layouts: 3.32 us -> 3.77 us
where the time goes in v2:
time: 116 us
  waiting for transfers between devices  40.9 us (35%)
  matrix products  26.3 us (23%)
  other arithmetic  23.7 us (20%)
  local copies, waits for them, and re-layouts  13.8 us (12%)
  starting transfers between devices  10.9 us (9%)
    dot_general x4, matrix products, contract(): jnp.einsum(pattern, left_op, right_op, precision=lax.Precision.HIGH, pref...  26.3 us
    all_to_all x1, waiting for transfers between devices, by_channels(): lax.all_to_all(sent, ('outer', 'inner'), split_axis=0, concat_axis=0, til...  25.6 us
    all_to_all x1, waiting for transfers between devices, by_channels(): lax.all_to_all(outcome, ('outer', 'inner'), split_axis=0, concat_axis=0,...  15.3 us
    add x1, other arithmetic, by_channels(): real_part = prod[:size_a, :, :row_count] + prod[size_a:, :, row_count:]  10 us
    all_to_all x1, starting transfers between devices, by_channels(): lax.all_to_all(sent, ('outer', 'inner'), split_axis=0, concat_axis=0, til...  7.3 us
    gather x1, local copies, waits for them, and re-layouts, by_channels(): chan_filters = jnp.take(filters.T, group_index, axis=0)  6.18 us
    unnamed x8, local copies, waits for them, and re-layouts  3.77 us
    all_to_all x1, starting transfers between devices, by_channels(): lax.all_to_all(outcome, ('outer', 'inner'), split_axis=0, concat_axis=0,...  3.61 us
  transfers between devices with their start and end apart: 2, of which 2 were waited for; matrix products, arithmetic and copies ran while one was open for 1% of the time, Pallas kernels for 0%

profile of v2, /device:TPU:0, one launch (start us, length us, event | category | flops | bytes accessed | tf_op | source)
XLA Modules:
  0.0 115.8 jit_solution(761996108602322944)
XLA Ops:
  0.0 0.7 fusion.52
  0.7 0.7 compare_and_fusion
  1.4 1.3 %copy.22 = bf16[128,2048]{0,1:T(8,128)(2,1)S(1)} copy(bf16[128,2048]{1,0:T(8,128)(2,1)} %param.7) | data formatting | bytes 1048576 | tf_op args[1]
  2.7 1.3 %copy.23 = bf16[128,2048]{0,1:T(8,128)(2,1)S(1)} copy(bf16[128,2048]{1,0:T(8,128)(2,1)} %param.8) | data formatting | bytes 1048576 | tf_op args[2]
  4.0 0.9 copy.24
  4.9 0.1 broadcast_in_dim.14
  5.0 0.1 multiply_convert_fusion
  5.1 6.2 %gather_fusion = bf16[2048,128]{1,0:T(8,128)(2,1)S(1)} fusion(bf16[128,128]{1,0:T(8,128)(2,1)S(1)} %bitcast.30, s32[2048]{0:T(1024)S(1)} %fusion.52), kind=kCustom, calls=%fused_computation | custom fusion | bytes 1056768 | tf_op jit(solution)/shard_map/jit(_take)/gather | solution.py:60
  11.3 0.3 broadcast_select_fusion
  11.7 0.1 maximum_bitcast_fusion
  11.8 1.1 copy.25
  12.9 7.3 %all-to-all-start = ((bf16[32,2,64,128]{3,2,1,0:T(8,128)(2,1)}), bf16[32,2,64,128]{3,2,1,0:T(8,128)(2,1)S(1)}, u32[]{:S(2)}, u32[]{:S(2)}) async-start(bf16[32,2,64,128]{3,2,1,0:T(8,128)(2,1)} %copy.25), calls=%async_computation | async-start | bytes 2097152 | tf_op jit(solution)/shard_map/all_to_all | solution.py:63
  20.2 0.1 sine_negate_fusion
  20.3 0.1 sine_negate_fusion.1
  20.3 0.1 fusion.42
  20.5 0.3 fusion.26
  20.8 25.6 %all-to-all-done = bf16[32,2,64,128]{3,2,1,0:T(8,128)(2,1)S(1)} async-done(((bf16[32,2,64,128]{3,2,1,0:T(8,128)(2,1)}), bf16[32,2,64,128]{3,2,1,0:T(8,128)(2,1)S(1)}, u32[]{:S(2)}, u32[]{:S(2)}) %all-to-all-start) | async-done | bytes 1048608 | tf_op jit(solution)/shard_map/all_to_all | solution.py:63
  46.4 0.7 copy.26
  47.1 2.4 %fusion.39 = f32[128,128,128]{2,0,1:T(8,128)S(1)} fusion(bf16[32,128,128]{2,0,1:T(8,128)(2,1)S(1)} %bitcast.32, f32[64,32]{0,1:T(8,128)S(1)} %get-tuple-element.13, f32[64,32]{0,1:T(8,128)S(1)} %get-tuple-element.14), kind=kOutput, calls=%fused_computation.68 | convolution fusion | flops 402657280 | bytes 9453568 | tf_op jit(solution)/shard_map/kn,ncb->kcb/dot_general | solution.py:10
  49.5 3.2 %multiply_add_fusion = (f32[64,128,128]{2,0,1:T(8,128)S(1)}, f32[64,128,128]{2,0,1:T(8,128)}) fusion(f32[128,128,128]{2,0,1:T(8,128)S(1)} %fusion.39, f32[64,128]{1,0:T(8,128)S(1)} %get-tuple-element.15, f32[64,128]{1,0:T(8,128)S(1)} %get-tuple-element.16), kind=kLoop, calls=%fused_computation.14 | loop fusion | flops 6291456 | bytes 16842752 | tf_op jit(solution)/shard_map/add | solution.py:37
  52.7 3.0 %pad_maximum_fusion = f32[128,128,128]{2,0,1:T(8,128)S(1)} fusion(f32[64,128,128]{2,0,1:T(8,128)} %get-tuple-element.10, f32[64,128,128]{2,0,1:T(8,128)S(1)} %get-tuple-element.9), kind=kLoop, calls=%fused_computation.1 | loop fusion | flops 2097152 | bytes 16777216 | tf_op jit(solution)/shard_map/concatenate | solution.py:75
  55.8 15.9 %fusion = f32[128,128,256]{2,1,0:T(8,128)} fusion(f32[128,128,128]{2,0,1:T(8,128)S(1)} %pad_maximum_fusion, f32[128,128]{1,0:T(8,128)S(1)} %get-tuple-element.17, f32[128,128]{1,0:T(8,128)S(1)} %get-tuple-element.18), kind=kOutput, calls=%fused_computation.2 | convolution fusion | flops 3221258240 | bytes 25296896 | tf_op jit(solution)/shard_map/kcb,bq->kcq/dot_general | solution.py:10
  71.7 10.0 %slice_add_fusion = (f32[64,128,128]{2,1,0:T(8,128)S(1)}, f32[64,128,128]{2,1,0:T(8,128)}) fusion(f32[128,128,256]{2,1,0:T(8,128)} %fusion), kind=kLoop, calls=%fused_computation.5 | loop fusion | flops 2097152 | bytes 25165824 | tf_op jit(solution)/shard_map/add | solution.py:76
  81.7 3.2 %multiply_subtract_fusion.2 = (f32[64,64,128]{2,1,0:T(8,128)S(1)}, f32[64,64,128]{2,1,0:T(8,128)S(1)}) fusion(f32[64,128,128]{2,1,0:T(8,128)} %get-tuple-element.6, f32[64,128,128]{2,1,0:T(8,128)S(1)} %get-tuple-element.5), kind=kLoop, calls=%fused_computation.20 | loop fusion | flops 3145728 | bytes 12582912 | tf_op jit(solution)/shard_map/sub | solution.py:82
  84.9 0.6 pad_maximum_fusion.1
  85.5 6.4 %fusion.6 = f32[128,64,256]{2,0,1:T(8,128)S(1)} fusion(f32[128,64,128]{2,1,0:T(8,128)S(1)} %pad_maximum_fusion.1, f32[128,128]{1,0:T(8,128)S(1)} %get-tuple-element.17, f32[128,128]{1,0:T(8,128)S(1)} %get-tuple-element.18), kind=kOutput, calls=%fused_computation.11 | convolution fusion | flops 1610645504 | bytes 12713984 | tf_op jit(solution)/shard_map/kcq,qb->kcb/dot_general | solution.py:10
  91.9 0.8 multiply_subtract_fusion.1
  92.7 0.0 copy-start
  92.7 0.0 copy-start.1
  92.7 1.6 %fusion.11 = bf16[32,64,128]{2,0,1:T(8,128)(2,1)S(1)} fusion(f32[64,64,128]{2,0,1:T(8,128)S(1)} %get-tuple-element.8, f32[64,64,128]{2,0,1:T(8,128)S(1)} %get-tuple-element.7, f32[32,64]{1,0:T(8,128)S(1)} %get-tuple-element.19, f32[32,64]{1,0:T(8,128)S(1)} %get-tuple-element.20), kind=kOutput, calls=%fused_computation.22 | convolution fusion | flops 202903552 | bytes 4734976 | tf_op jit(solution)/shard_map/nk,kcb->ncb/dot_general | solution.py:10
  94.3 1.0 copy.29
  95.3 3.6 %all-to-all-start.1 = ((bf16[32,64,128]{2,1,0:T(8,128)(2,1)}), bf16[32,64,128]{2,1,0:T(8,128)(2,1)S(1)}, u32[]{:S(2)}, u32[]{:S(2)}) async-start(bf16[32,64,128]{2,1,0:T(8,128)(2,1)} %copy.29), calls=%async_computation.1 | async-start | bytes 1048576 | tf_op jit(solution)/shard_map/all_to_all | solution.py:95
  98.9 0.0 copy-done
  98.9 0.3 copy.21
  99.2 15.3 %all-to-all-done.1 = bf16[32,64,128]{2,1,0:T(8,128)(2,1)S(1)} async-done(((bf16[32,64,128]{2,1,0:T(8,128)(2,1)}), bf16[32,64,128]{2,1,0:T(8,128)(2,1)S(1)}, u32[]{:S(2)}, u32[]{:S(2)}) %all-to-all-start.1) | async-done | bytes 524320 | tf_op jit(solution)/shard_map/all_to_all | solution.py:95
  114.5 0.0 copy-done.1
  114.5 0.3 fusion.16
  114.8 1.0 copy.30
Async XLA Ops:
  12.9 33.5 %all-to-all-start = ((bf16[32,2,64,128]{3,2,1,0:T(8,128)(2,1)}), bf16[32,2,64,128]{3,2,1,0:T(8,128)(2,1)S(1)}, u32[]{:S(2)}, u32[]{:S(2)}) async-start(bf16[32,2,64,128]{3,2,1,0:T(8,128)(2,1)} %copy.25), calls=%async_computation | async-start | bytes 2097152 | tf_op jit(solution)/shard_map/all_to_all | solution.py:63
  92.7 6.2 %copy-start = (bf16[128,2048]{1,0:T(8,128)(2,1)S(1)}, bf16[128,2048]{1,0:T(8,128)(2,1)}, u32[]{:S(2)}) copy-start(bf16[128,2048]{1,0:T(8,128)(2,1)} %param.6) | copy-start | bytes 1572868
  92.7 21.8 %copy-start.1 = (f32[2048]{0:T(1024)S(1)}, f32[2048]{0:T(1024)}, u32[]{:S(2)}) copy-start(f32[2048]{0:T(1024)} %param.11) | copy-start | bytes 24580
  95.3 19.2 %all-to-all-start.1 = ((bf16[32,64,128]{2,1,0:T(8,128)(2,1)}), bf16[32,64,128]{2,1,0:T(8,128)(2,1)S(1)}, u32[]{:S(2)}, u32[]{:S(2)}) async-start(bf16[32,64,128]{2,1,0:T(8,128)(2,1)} %copy.29), calls=%async_computation.1 | async-start | bytes 1048576 | tf_op jit(solution)/shard_map/all_to_all | solution.py:95

commit v3 on v2

--- a/solution.py
+++ b/solution.py
@@ -4,6 +4,7 @@
 import jax.numpy as jnp
 from jax import lax
 from jax.sharding import PartitionSpec as P
+from jax.experimental import pallas as pl
 
 
 def contract(pattern, left_op, right_op):
@@ -50,6 +51,38 @@
     return (out_real, out_imag)
 
 
+def select_kernel(index_ref, filters_ref, out_ref):
+    index = index_ref[...]
+    groups = filters_ref.shape[1]
+    onehot = (
+        index == lax.broadcasted_iota(jnp.int32, (index.shape[0], groups), 1)
+    ).astype(jnp.bfloat16)
+    out_ref[...] = lax.dot_general(
+        onehot,
+        filters_ref[...],
+        (((1,), (1,)), ((), ())),
+        preferred_element_type=jnp.float32,
+    ).astype(out_ref.dtype)
+
+
+def select_filters(filters, group_index):
+    channels = group_index.shape[0]
+    return pl.pallas_call(
+        select_kernel,
+        out_shape=jax.ShapeDtypeStruct((channels, filters.shape[0]), jnp.bfloat16),
+    )(group_index.reshape(channels, 1), filters)
+
+
+def complex_table(cos_part, sin_part, direction):
+    return jnp.concatenate(
+        [
+            jnp.concatenate([cos_part, direction * sin_part], axis=1),
+            jnp.concatenate([-direction * sin_part, cos_part], axis=1),
+        ],
+        axis=0,
+    )
+
+
 def by_channels(mixed, filters, group_index):
     n_dev = lax.axis_size("outer") * lax.axis_size("inner")
     row_count = mixed.shape[0]
@@ -57,7 +90,7 @@
     own_width = channels // n_dev
     size_a = 2 * n_dev
     padded = size_a * row_count
-    chan_filters = jnp.take(filters.T, group_index, axis=0)
+    chan_filters = select_filters(filters, group_index)
     sent = jnp.stack([mixed.T, chan_filters], axis=0).reshape(2, n_dev, own_width, row_count)
     sent = sent.transpose(1, 0, 2, 3)
     got = lax.all_to_all(sent, ("outer", "inner"), split_axis=0, concat_axis=0, tiled=True)
@@ -71,20 +104,23 @@
     )[:, None, :]
     real_part, imag_part = rotate(first[:size_a], first[size_a:], twiddle, -1)
     second_cos, second_sin = dft_table(row_count, row_count, row_count)
-    table = jnp.concatenate([second_cos, second_sin], axis=1)
-    prod = contract("kcb,bq->kcq", jnp.concatenate([real_part, imag_part], axis=0), table)
-    real_part = prod[:size_a, :, :row_count] + prod[size_a:, :, row_count:]
-    imag_part = prod[size_a:, :, :row_count] - prod[:size_a, :, row_count:]
-    data_real = real_part[:, :own_width]
-    data_imag = imag_part[:, :own_width]
-    filter_real = real_part[:, own_width:]
-    filter_imag = imag_part[:, own_width:]
+    prod = contract(
+        "kcb,bq->kcq",
+        jnp.concatenate([real_part, imag_part], axis=2),
+        complex_table(second_cos, second_sin, -1),
+    )
+    data_real = prod[:, :own_width, :row_count]
+    data_imag = prod[:, :own_width, row_count:]
+    filter_real = prod[:, own_width:, :row_count]
+    filter_imag = prod[:, own_width:, row_count:]
     spec_real = data_real * filter_real - data_imag * filter_imag
     spec_imag = data_real * filter_imag + data_imag * filter_real
-    prod = contract("kcq,qb->kcb", jnp.concatenate([spec_real, spec_imag], axis=0), table)
-    real_part = prod[:size_a, :, :row_count] - prod[size_a:, :, row_count:]
-    imag_part = prod[size_a:, :, :row_count] + prod[:size_a, :, row_count:]
-    real_part, imag_part = rotate(real_part, imag_part, twiddle, 1)
+    prod = contract(
+        "kcq,qb->kcb",
+        jnp.concatenate([spec_real, spec_imag], axis=2),
+        complex_table(second_cos, second_sin, 1),
+    )
+    real_part, imag_part = rotate(prod[:, :, :row_count], prod[:, :, row_count:], twiddle, 1)
     back_cos, back_sin = dft_table(n_dev, size_a, size_a)
     outcome = contract(
         "nk,kcb->ncb",

time: 116 us -> 86.4 us (0.74)
  other arithmetic: 23.7 us -> 7.36 us
  matrix products: 26.3 us -> 15.6 us
  local copies, waits for them, and re-layouts: 13.8 us -> 8.71 us
  Pallas kernels: 0 us -> 2.48 us
    dot_general x4, matrix products: 26.3 us -> 15.6 us  [contract(): jnp.einsum(pattern, left_op, right_op, precision=lax.Precision.HIGH, pref...]
    add x1 -> x0, other arithmetic: 10 us -> none  [by_channels(): real_part = prod[:size_a, :, :row_count] + prod[size_a:, :, row_count:]]
    gather x1 -> x0, local copies, waits for them, and re-layouts: 6.18 us -> none  [by_channels(): chan_filters = jnp.take(filters.T, group_index, axis=0)]
    sub x1, other arithmetic: 3.21 us -> 0.66 us  [by_channels(): spec_real = data_real * filter_real - data_imag * filter_imag]
    pallas_call x0 -> x1, Pallas kernels: none -> 2.48 us  [select_filters(): pl.pallas_call(select_kernel, out_shape=jax.ShapeDtypeStruct((channels, f...]
    concatenate x1, other arithmetic: 3.04 us -> 0.58 us  [by_channels(): jnp.concatenate([real_part, imag_part], axis=0)]
    reshape x0 -> x1, local copies, waits for them, and re-layouts: none -> 2.05 us  [select_filters(): group_index.reshape(channels, 1)]
    unnamed x8 -> x7, local copies, waits for them, and re-layouts: 3.77 us -> 2.9 us
where the time goes in v3:
time: 86.4 us; the launch traced here: 85.9 us
  waiting for transfers between devices  40.6 us (47%)
  matrix products  15.6 us (18%)
  starting transfers between devices  10.9 us (13%)
  local copies, waits for them, and re-layouts  8.71 us (10%)
  other arithmetic  7.36 us (9%)
  Pallas kernels  2.48 us (3%)
    all_to_all x1, waiting for transfers between devices, by_channels(): lax.all_to_all(sent, ('outer', 'inner'), split_axis=0, concat_axis=0, til...  25.4 us
    dot_general x4, matrix products, contract(): jnp.einsum(pattern, left_op, right_op, precision=lax.Precision.HIGH, pref...  15.6 us
    all_to_all x1, waiting for transfers between devices, by_channels(): lax.all_to_all(outcome, ('outer', 'inner'), split_axis=0, concat_axis=0,...  15.3 us
    all_to_all x1, starting transfers between devices, by_channels(): lax.all_to_all(sent, ('outer', 'inner'), split_axis=0, concat_axis=0, til...  7.3 us
    all_to_all x1, starting transfers between devices, by_channels(): lax.all_to_all(outcome, ('outer', 'inner'), split_axis=0, concat_axis=0,...  3.62 us
    unnamed x7, local copies, waits for them, and re-layouts  2.9 us
    pallas_call x1, Pallas kernels, select_filters(): pl.pallas_call(select_kernel, out_shape=jax.ShapeDtypeStruct((channels, f...  2.48 us
    reshape x1, local copies, waits for them, and re-layouts, select_filters(): group_index.reshape(channels, 1)  2.05 us
  transfers between devices with their start and end apart: 2, of which 2 were waited for; matrix products, arithmetic and copies ran while one was open for 1% of the time, Pallas kernels for 0%

profile of v3, /device:TPU:0, one launch (start us, length us, event | category | flops | bytes accessed | tf_op | source)
XLA Modules:
  0.0 85.9 jit_solution(1839298939456758607)
XLA Ops:
  0.0 1.3 %copy.21 = bf16[128,2048]{0,1:T(8,128)(2,1)S(1)} copy(bf16[128,2048]{1,0:T(8,128)(2,1)} %param.7) | data formatting | bytes 1048576 | tf_op args[1]
  1.3 1.3 %copy.22 = bf16[128,2048]{0,1:T(8,128)(2,1)S(1)} copy(bf16[128,2048]{1,0:T(8,128)(2,1)} %param.8) | data formatting | bytes 1048576 | tf_op args[2]
  2.6 2.0 %copy.23.index_ref = s32[2048,1]{1,0:T(8,128)} copy(s32[2048,1]{0,1:T(1,128)} %bitcast.35) | data formatting | bytes 16384 | tf_op jit(solution)/shard_map/reshape | solution.py:73
  4.7 0.1 multiply_convert_fusion
  4.8 2.5 %shard_map.64 = bf16[2048,128]{1,0:T(8,128)(2,1)} custom-call(s32[2048,1]{1,0:T(8,128)} %copy.23.index_ref, bf16[128,128]{1,0:T(8,128)(2,1)} %filters_ref.1), custom_call_target="tpu_custom_call" | custom-call | tf_op jit(solution)/shard_map/pallas_call | solution.py:70
  7.3 1.1 %maximum_bitcast_fusion = bf16[32,2,64,128]{3,2,0,1:T(8,128)(2,1)S(1)} fusion(bf16[1,32,64,128]{3,2,1,0:T(8,128)(2,1)} %bitcast.34, bf16[1,32,64,128]{3,2,1,0:T(8,128)(2,1)S(1)} %bitcast.32), kind=kLoop, calls=%fused_computation.18 | loop fusion | flops 524288 | bytes 2097152 | tf_op jit(solution)/shard_map/transpose | solution.py:95
  8.4 1.1 %copy.24 = bf16[32,2,64,128]{3,2,1,0:T(8,128)(2,1)} copy(bf16[32,2,64,128]{3,2,0,1:T(8,128)(2,1)S(1)} %maximum_bitcast_fusion) | data formatting | bytes 2097152 | tf_op jit(solution)/shard_map/transpose | solution.py:95
  9.5 7.3 %all-to-all-start = ((bf16[32,2,64,128]{3,2,1,0:T(8,128)(2,1)}), bf16[32,2,64,128]{3,2,1,0:T(8,128)(2,1)S(1)}, u32[]{:S(2)}, u32[]{:S(2)}) async-start(bf16[32,2,64,128]{3,2,1,0:T(8,128)(2,1)} %copy.24), calls=%async_computation | async-start | bytes 2097152 | tf_op jit(solution)/shard_map/all_to_all | solution.py:96
  16.8 0.1 sine_negate_fusion
  16.9 0.1 sine_negate_fusion.1
  17.0 0.1 fusion.52
  17.2 0.3 fusion.37
  17.4 0.3 broadcast_multiply_fusion
  17.7 25.4 %all-to-all-done = bf16[32,2,64,128]{3,2,1,0:T(8,128)(2,1)S(1)} async-done(((bf16[32,2,64,128]{3,2,1,0:T(8,128)(2,1)}), bf16[32,2,64,128]{3,2,1,0:T(8,128)(2,1)S(1)}, u32[]{:S(2)}, u32[]{:S(2)}) %all-to-all-start) | async-done | bytes 1048608 | tf_op jit(solution)/shard_map/all_to_all | solution.py:96
  43.1 0.7 copy.25
  43.7 2.4 %fusion.49 = f32[128,128,128]{2,0,1:T(8,128)S(1)} fusion(bf16[32,128,128]{2,0,1:T(8,128)(2,1)S(1)} %bitcast.33, f32[64,32]{0,1:T(8,128)S(1)} %get-tuple-element.11, f32[64,32]{0,1:T(8,128)S(1)} %get-tuple-element.12), kind=kOutput, calls=%fused_computation.73 | convolution fusion | flops 402657280 | bytes 9453568 | tf_op jit(solution)/shard_map/kn,ncb->kcb/dot_general | solution.py:11
  46.2 2.0 %multiply_add_fusion = (f32[64,128,128]{2,0,1:T(8,128)S(1)}, f32[64,128,128]{2,0,1:T(8,128)S(1)}) fusion(f32[128,128,128]{2,0,1:T(8,128)S(1)} %fusion.49, f32[64,128]{1,0:T(8,128)S(1)} %get-tuple-element.13, f32[64,128]{1,0:T(8,128)S(1)} %get-tuple-element.14), kind=kLoop, calls=%fused_computation.11 | loop fusion | flops 6291456 | bytes 16842752 | tf_op jit(solution)/shard_map/add | solution.py:38
  48.2 1.0 %pad_maximum_fusion = f32[64,128,256]{2,0,1:T(8,128)S(1)} fusion(f32[64,128,128]{2,0,1:T(8,128)S(1)} %get-tuple-element.6, f32[64,128,128]{2,0,1:T(8,128)S(1)} %get-tuple-element.5), kind=kLoop, calls=%fused_computation | loop fusion | flops 2097152 | bytes 16777216 | tf_op jit(solution)/shard_map/concatenate | solution.py:109
  49.2 8.0 %fusion = f32[64,128,256]{2,1,0:T(8,128)S(1)} fusion(f32[64,128,256]{2,0,1:T(8,128)S(1)} %pad_maximum_fusion, f32[128,128]{1,0:T(8,128)S(1)} %fusion.37, f32[128,128]{1,0:T(8,128)S(1)} %get-tuple-element.16, f32[128,128]{1,0:T(8,128)S(1)} %get-tuple-element.15), kind=kOutput, calls=%fused_computation.1 | convolution fusion | flops 3221422080 | bytes 16973824 | tf_op jit(solution)/shard_map/kcb,bq->kcq/dot_general | solution.py:11
  57.3 0.7 multiply_subtract_fusion.2
  58.0 1.8 %fusion.2 = f32[64,64,256]{2,1,0:T(8,128)S(1)} fusion(f32[64,64,128]{2,1,0:T(8,128)S(1)} %get-tuple-element.8, f32[64,64,128]{2,1,0:T(8,128)S(1)} %get-tuple-element.7, f32[128,128]{1,0:T(8,128)S(1)} %fusion.37, f32[128,128]{1,0:T(8,128)S(1)} %get-tuple-element.15, f32[128,128]{1,0:T(8,128)S(1)} %get-tuple-element.16), kind=kOutput, calls=%fused_computation.3 | convolution fusion | flops 1611857920 | bytes 8585216 | tf_op jit(solution)/shard_map/kcq,qb->kcb/dot_general | solution.py:11
  59.8 0.6 multiply_subtract_fusion.1
  60.4 0.6 pad_maximum_fusion.1
  61.0 0.0 copy-start
  61.0 0.0 copy-start.1
  61.0 3.3 %fusion.11 = bf16[32,64,128]{2,0,1:T(8,128)(2,1)S(1)} fusion(f32[128,64,128]{2,1,0:T(8,128)S(1)} %pad_maximum_fusion.1, f32[32,64]{1,0:T(8,128)S(1)} %get-tuple-element.17, f32[32,64]{1,0:T(8,128)S(1)} %get-tuple-element.18), kind=kOutput, calls=%fused_computation.17 | convolution fusion | flops 201854976 | bytes 4734976 | tf_op jit(solution)/shard_map/nk,kcb->ncb/dot_general | solution.py:11
  64.4 1.0 %copy.28 = bf16[32,64,128]{2,1,0:T(8,128)(2,1)} copy(bf16[32,64,128]{2,0,1:T(8,128)(2,1)S(1)} %fusion.11) | data formatting | bytes 1048576 | tf_op jit(solution)/shard_map/convert_element_type | solution.py:130
  65.4 3.6 %all-to-all-start.1 = ((bf16[32,64,128]{2,1,0:T(8,128)(2,1)}), bf16[32,64,128]{2,1,0:T(8,128)(2,1)S(1)}, u32[]{:S(2)}, u32[]{:S(2)}) async-start(bf16[32,64,128]{2,1,0:T(8,128)(2,1)} %copy.28), calls=%async_computation.1 | async-start | bytes 1048576 | tf_op jit(solution)/shard_map/all_to_all | solution.py:131
  69.0 0.0 copy-done
  69.0 0.3 copy.20
  69.3 15.3 %all-to-all-done.1 = bf16[32,64,128]{2,1,0:T(8,128)(2,1)S(1)} async-done(((bf16[32,64,128]{2,1,0:T(8,128)(2,1)}), bf16[32,64,128]{2,1,0:T(8,128)(2,1)S(1)}, u32[]{:S(2)}, u32[]{:S(2)}) %all-to-all-start.1) | async-done | bytes 524320 | tf_op jit(solution)/shard_map/all_to_all | solution.py:131
  84.6 0.0 copy-done.1
  84.6 0.3 fusion.16
  84.9 1.0 %copy.29 = bf16[128,2048]{1,0:T(8,128)(2,1)} copy(bf16[128,2048]{0,1:T(8,128)(2,1)S(1)} %fusion.16) | data formatting | bytes 1048576 | tf_op jit(solution)/shard_map/convert_element_type | solution.py:139
Async XLA Ops:
  9.5 33.5 %all-to-all-start = ((bf16[32,2,64,128]{3,2,1,0:T(8,128)(2,1)}), bf16[32,2,64,128]{3,2,1,0:T(8,128)(2,1)S(1)}, u32[]{:S(2)}, u32[]{:S(2)}) async-start(bf16[32,2,64,128]{3,2,1,0:T(8,128)(2,1)} %copy.24), calls=%async_computation | async-start | bytes 2097152 | tf_op jit(solution)/shard_map/all_to_all | solution.py:96
  61.0 8.0 %copy-start = (bf16[128,2048]{1,0:T(8,128)(2,1)S(1)}, bf16[128,2048]{1,0:T(8,128)(2,1)}, u32[]{:S(2)}) copy-start(bf16[128,2048]{1,0:T(8,128)(2,1)} %param.6) | copy-start | bytes 1572868
  61.0 23.5 %copy-start.1 = (f32[2048]{0:T(1024)S(1)}, f32[2048]{0:T(1024)}, u32[]{:S(2)}) copy-start(f32[2048]{0:T(1024)} %param.11) | copy-start | bytes 24580
  65.4 19.2 %all-to-all-start.1 = ((bf16[32,64,128]{2,1,0:T(8,128)(2,1)}), bf16[32,64,128]{2,1,0:T(8,128)(2,1)S(1)}, u32[]{:S(2)}, u32[]{:S(2)}) async-start(bf16[32,64,128]{2,1,0:T(8,128)(2,1)} %copy.28), calls=%async_computation.1 | async-start | bytes 1048576 | tf_op jit(solution)/shard_map/all_to_all | solution.py:131

commit v4 on v3

--- a/solution.py
+++ b/solution.py
@@ -54,23 +54,26 @@
 def select_kernel(index_ref, filters_ref, out_ref):
     index = index_ref[...]
     groups = filters_ref.shape[1]
+    block = out_ref.shape[2]
     onehot = (
         index == lax.broadcasted_iota(jnp.int32, (index.shape[0], groups), 1)
     ).astype(jnp.bfloat16)
-    out_ref[...] = lax.dot_general(
+    picked = lax.dot_general(
         onehot,
         filters_ref[...],
         (((1,), (1,)), ((), ())),
         preferred_element_type=jnp.float32,
-    ).astype(out_ref.dtype)
+    )
+    for n in range(out_ref.shape[0]):
+        out_ref[n] = picked[:, n * block : (n + 1) * block].astype(out_ref.dtype)
 
 
-def select_filters(filters, group_index):
-    channels = group_index.shape[0]
+def select_filters(filters, own_index, n_blocks, block):
+    width = own_index.shape[0]
     return pl.pallas_call(
         select_kernel,
-        out_shape=jax.ShapeDtypeStruct((channels, filters.shape[0]), jnp.bfloat16),
-    )(group_index.reshape(channels, 1), filters)
+        out_shape=jax.ShapeDtypeStruct((n_blocks, width, block), jnp.bfloat16),
+    )(own_index.reshape(width, 1), filters)
 
 
 def complex_table(cos_part, sin_part, direction):
@@ -90,11 +93,13 @@
     own_width = channels // n_dev
     size_a = 2 * n_dev
     padded = size_a * row_count
-    chan_filters = select_filters(filters, group_index)
-    sent = jnp.stack([mixed.T, chan_filters], axis=0).reshape(2, n_dev, own_width, row_count)
-    sent = sent.transpose(1, 0, 2, 3)
+    all_filters = lax.all_gather(filters, ("outer", "inner"), axis=0, tiled=True)
+    me = lax.axis_index("outer") * lax.axis_size("inner") + lax.axis_index("inner")
+    own_index = lax.dynamic_slice(group_index, (me * own_width,), (own_width,))
+    sent = mixed.T.reshape(n_dev, own_width, row_count)
     got = lax.all_to_all(sent, ("outer", "inner"), split_axis=0, concat_axis=0, tiled=True)
-    stacked = got.reshape(n_dev, 2 * own_width, row_count).astype(jnp.float32)
+    chan_filters = select_filters(all_filters, own_index, n_dev, row_count)
+    stacked = jnp.concatenate([got, chan_filters], axis=1).astype(jnp.float32)
     first_cos, first_sin = dft_table(size_a, n_dev, size_a)
     first = contract("kn,ncb->kcb", jnp.concatenate([first_cos, -first_sin], axis=0), stacked)
     twiddle = angles_of(

time: 86.4 us -> 122 us (1.41)
  waiting for transfers between devices: 40.6 us -> 63.8 us
  between operations: 0.17 us -> 13.6 us
  local copies, waits for them, and re-layouts: 8.71 us -> 5.72 us
  other arithmetic: 7.36 us -> 9.19 us
    all_gather x0 -> x1, waiting for transfers between devices: none -> 47.8 us  [by_channels(): lax.all_gather(filters, ('outer', 'inner'), axis=0, tiled=True)]
    all_to_all x1, waiting for transfers between devices: 25.4 us -> 0.01 us  [by_channels(): lax.all_to_all(sent, ('outer', 'inner'), split_axis=0, concat_axis=0, til...]
    reshape x1 -> x2, local copies, waits for them, and re-layouts: 2.05 us -> 0.79 us  [select_filters(): own_index.reshape(width, 1)]
    unnamed x7 -> x9, local copies, waits for them, and re-layouts: 2.9 us -> 2.91 us
  transfers between devices with their start and end apart: 2 -> 3, of which waited for: 2 -> 2; matrix products, arithmetic and copies ran while one was open for 1% -> 4% of each run, Pallas kernels for 0% -> 2%
where the time goes in v4:
time: 122 us; the launch traced here: 121 us
  waiting for transfers between devices  63.8 us (52%)
  matrix products  15.7 us (13%)
  between operations  13.6 us (11%)
  starting transfers between devices  10.9 us (9%)
  other arithmetic  9.19 us (8%)
  local copies, waits for them, and re-layouts  5.72 us (5%)
  Pallas kernels  2.6 us (2%)
    all_gather x1, waiting for transfers between devices, by_channels(): lax.all_gather(filters, ('outer', 'inner'), axis=0, tiled=True)  47.8 us
    dot_general x4, matrix products, contract(): jnp.einsum(pattern, left_op, right_op, precision=lax.Precision.HIGH, pref...  15.7 us
    all_to_all x1, waiting for transfers between devices, by_channels(): lax.all_to_all(outcome, ('outer', 'inner'), split_axis=0, concat_axis=0,...  15.3 us
    all_to_all x1, starting transfers between devices, by_channels(): lax.all_to_all(sent, ('outer', 'inner'), split_axis=0, concat_axis=0, til...  7.3 us
    all_to_all x1, starting transfers between devices, by_channels(): lax.all_to_all(outcome, ('outer', 'inner'), split_axis=0, concat_axis=0,...  3.56 us
    unnamed x9, local copies, waits for them, and re-layouts  2.91 us
    pallas_call x1, Pallas kernels, select_filters(): pl.pallas_call(select_kernel, out_shape=jax.ShapeDtypeStruct((n_blocks, w...  2.6 us
  transfers between devices with their start and end apart: 3, of which 2 were waited for; matrix products, arithmetic and copies ran while one was open for 4% of the time, Pallas kernels for 2%

profile of v4, /device:TPU:0, one launch (start us, length us, event | category | flops | bytes accessed | tf_op | source)
XLA Modules:
  0.0 121.4 jit_solution(3899725846943946841)
XLA Ops:
  6.5 0.0 copy-start
  6.5 0.0 all-gather.2.cloned.1.call-start
  6.5 0.7 all-gather.2.cloned.1.call-update
  7.3 1.3 %copy.22 = bf16[128,2048]{0,1:T(8,128)(2,1)S(1)} copy(bf16[128,2048]{1,0:T(8,128)(2,1)} %param.7) | data formatting | bytes 1048576 | tf_op args[1]
  8.6 1.3 %copy.23 = bf16[128,2048]{0,1:T(8,128)(2,1)S(1)} copy(bf16[128,2048]{1,0:T(8,128)(2,1)} %param.8) | data formatting | bytes 1048576 | tf_op args[2]
  9.9 0.9 multiply_convert_fusion
  10.8 7.3 %all-to-all-start = ((bf16[32,64,128]{2,1,0:T(8,128)(2,1)}), bf16[32,64,128]{2,1,0:T(8,128)(2,1)S(1)}, u32[]{:S(2)}, u32[]{:S(2)}) async-start(bf16[32,64,128]{2,1,0:T(8,128)(2,1)} %bitcast.3), calls=%async_computation | async-start | bytes 1048576 | tf_op jit(solution)/shard_map/all_to_all | solution.py:100
  18.1 0.0 copy-done
  18.2 0.1 dynamic-slice_bitcast_fusion
  18.2 0.7 copy.24.index_ref
  18.9 0.1 sine_negate_fusion
  19.0 0.1 sine_negate_fusion.1
  19.1 0.1 fusion.53
  19.3 0.3 fusion.39
  19.5 0.3 broadcast_multiply_fusion
  19.8 47.8 %all-gather.2.cloned.1.call-done.filters_ref = bf16[4096,128]{1,0:T(8,128)(2,1)} async-done(((bf16[128,128]{1,0:T(8,128)(2,1)}), bf16[4096,128]{1,0:T(8,128)(2,1)}) %all-gather.2.cloned.1.call-update) | async-done | bytes 1048592 | tf_op jit(solution)/shard_map/all_gather | solution.py:96
  67.6 2.6 %shard_map.64 = bf16[32,64,128]{2,1,0:T(8,128)(2,1)} custom-call(s32[64,1]{1,0:T(8,128)} %copy.24.index_ref, bf16[4096,128]{1,0:T(8,128)(2,1)} %all-gather.2.cloned.1.call-done.filters_ref), custom_call_target="tpu_custom_call" | custom-call | tf_op jit(solution)/shard_map/pallas_call | solution.py:73
  70.2 0.0 all-to-all-done
  70.2 1.1 pad_maximum_fusion.2
  71.3 2.4 %fusion.17 = f32[128,128,128]{2,0,1:T(8,128)S(1)} fusion(bf16[32,128,128]{2,1,0:T(8,128)(2,1)S(1)} %pad_maximum_fusion.2, f32[64,32]{0,1:T(8,128)S(1)} %get-tuple-element.11, f32[64,32]{0,1:T(8,128)S(1)} %get-tuple-element.12), kind=kOutput, calls=%fused_computation.23 | convolution fusion | flops 402657280 | bytes 9453568 | tf_op jit(solution)/shard_map/kn,ncb->kcb/dot_general | solution.py:11
  73.8 2.0 %multiply_add_fusion = (f32[64,128,128]{2,0,1:T(8,128)S(1)}, f32[64,128,128]{2,0,1:T(8,128)S(1)}) fusion(f32[128,128,128]{2,0,1:T(8,128)S(1)} %fusion.17, f32[64,128]{1,0:T(8,128)S(1)} %get-tuple-element.13, f32[64,128]{1,0:T(8,128)S(1)} %get-tuple-element.14), kind=kLoop, calls=%fused_computation.11 | loop fusion | flops 6291456 | bytes 16842752 | tf_op jit(solution)/shard_map/add | solution.py:38
  75.8 1.0 pad_maximum_fusion
  76.8 8.0 %fusion = f32[64,128,256]{2,1,0:T(8,128)S(1)} fusion(f32[64,128,256]{2,0,1:T(8,128)S(1)} %pad_maximum_fusion, f32[128,128]{1,0:T(8,128)S(1)} %fusion.39, f32[128,128]{1,0:T(8,128)S(1)} %get-tuple-element.16, f32[128,128]{1,0:T(8,128)S(1)} %get-tuple-element.15), kind=kOutput, calls=%fused_computation.1 | convolution fusion | flops 3221422080 | bytes 16973824 | tf_op jit(solution)/shard_map/kcb,bq->kcq/dot_general | solution.py:11
  84.9 0.6 multiply_subtract_fusion.2
  85.5 1.9 %fusion.2 = f32[64,64,256]{2,1,0:T(8,128)S(1)} fusion(f32[64,64,128]{2,1,0:T(8,128)S(1)} %get-tuple-element.8, f32[64,64,128]{2,1,0:T(8,128)S(1)} %get-tuple-element.7, f32[128,128]{1,0:T(8,128)S(1)} %fusion.39, f32[128,128]{1,0:T(8,128)S(1)} %get-tuple-element.15, f32[128,128]{1,0:T(8,128)S(1)} %get-tuple-element.16), kind=kOutput, calls=%fused_computation.3 | convolution fusion | flops 1611857920 | bytes 8585216 | tf_op jit(solution)/shard_map/kcq,qb->kcb/dot_general | solution.py:11
  87.4 0.7 multiply_subtract_fusion.1
  88.1 0.6 pad_maximum_fusion.1
  88.7 0.0 copy-start.1
  88.7 0.0 copy-start.2
  88.7 3.3 %fusion.11 = bf16[32,64,128]{2,0,1:T(8,128)(2,1)S(1)} fusion(f32[128,64,128]{2,1,0:T(8,128)S(1)} %pad_maximum_fusion.1, f32[32,64]{1,0:T(8,128)S(1)} %get-tuple-element.17, f32[32,64]{1,0:T(8,128)S(1)} %get-tuple-element.18), kind=kOutput, calls=%fused_computation.17 | convolution fusion | flops 201854976 | bytes 4734976 | tf_op jit(solution)/shard_map/nk,kcb->ncb/dot_general | solution.py:11
  92.0 1.0 copy.28
  93.0 3.6 %all-to-all-start.1 = ((bf16[32,64,128]{2,1,0:T(8,128)(2,1)}), bf16[32,64,128]{2,1,0:T(8,128)(2,1)S(1)}, u32[]{:S(2)}, u32[]{:S(2)}) async-start(bf16[32,64,128]{2,1,0:T(8,128)(2,1)} %copy.28), calls=%async_computation.1 | async-start | bytes 1048576 | tf_op jit(solution)/shard_map/all_to_all | solution.py:136
  96.6 0.0 copy-done.1
  96.6 0.3 copy.21
  96.9 15.3 %all-to-all-done.1 = bf16[32,64,128]{2,1,0:T(8,128)(2,1)S(1)} async-done(((bf16[32,64,128]{2,1,0:T(8,128)(2,1)}), bf16[32,64,128]{2,1,0:T(8,128)(2,1)S(1)}, u32[]{:S(2)}, u32[]{:S(2)}) %all-to-all-start.1) | async-done | bytes 524320 | tf_op jit(solution)/shard_map/all_to_all | solution.py:136
  112.1 0.0 copy-done.2
  112.1 1.4 %fusion.16 = bf16[128,2048]{0,1:T(8,128)(2,1)S(1)} fusion(bf16[128,2048]{0,1:T(8,128)(2,1)} %multiply_convert_fusion, bf16[128,2048]{0,1:T(8,128)(2,1)S(1)} %copy.21, bf16[32,64,128]{2,1,0:T(8,128)(2,1)S(1)} %all-to-all-done.1, f32[2048]{0:T(1024)S(1)} %copy-done.2), kind=kLoop, calls=%fused_computation.22 | loop fusion | flops 1835008 | bytes 2105344 | tf_op jit(solution)/shard_map/convert_element_type | solution.py:144
  113.5 1.0 copy.29
Async XLA Ops:
  6.5 11.6 %copy-start = (s32[2048]{0:T(1024)S(1)}, s32[2048]{0:T(1024)}, u32[]{:S(2)}) copy-start(s32[2048]{0:T(1024)} %param.10) | copy-start | bytes 24580
  6.5 61.1 %all-gather.2.cloned.1.call-start = ((), (), s32[]{:S(2)}) async-start(), calls=%async_computation.2 | async-start | bytes 1081344 | tf_op jit(solution)/shard_map/all_gather | solution.py:96
  10.8 59.4 %all-to-all-start = ((bf16[32,64,128]{2,1,0:T(8,128)(2,1)}), bf16[32,64,128]{2,1,0:T(8,128)(2,1)S(1)}, u32[]{:S(2)}, u32[]{:S(2)}) async-start(bf16[32,64,128]{2,1,0:T(8,128)(2,1)} %bitcast.3), calls=%async_computation | async-start | bytes 1048576 | tf_op jit(solution)/shard_map/all_to_all | solution.py:100
  88.7 7.9 %copy-start.1 = (bf16[128,2048]{1,0:T(8,128)(2,1)S(1)}, bf16[128,2048]{1,0:T(8,128)(2,1)}, u32[]{:S(2)}) copy-start(bf16[128,2048]{1,0:T(8,128)(2,1)} %param.6) | copy-start | bytes 1572868
  88.7 23.5 %copy-start.2 = (f32[2048]{0:T(1024)S(1)}, f32[2048]{0:T(1024)}, u32[]{:S(2)}) copy-start(f32[2048]{0:T(1024)} %param.11) | copy-start | bytes 24580
  93.0 19.1 %all-to-all-start.1 = ((bf16[32,64,128]{2,1,0:T(8,128)(2,1)}), bf16[32,64,128]{2,1,0:T(8,128)(2,1)S(1)}, u32[]{:S(2)}, u32[]{:S(2)}) async-start(bf16[32,64,128]{2,1,0:T(8,128)(2,1)} %copy.28), calls=%async_computation.1 | async-start | bytes 1048576 | tf_op jit(solution)/shard_map/all_to_all | solution.py:136
Sparse Core Ops, SparseCore 0:
  10.2 57.3 all-gather.1

commit v5 on v3

--- a/solution.py
+++ b/solution.py
@@ -83,17 +83,10 @@
     )
 
 
-def by_channels(mixed, filters, group_index):
-    n_dev = lax.axis_size("outer") * lax.axis_size("inner")
-    row_count = mixed.shape[0]
-    channels = mixed.shape[1]
-    own_width = channels // n_dev
+def convolve_block(got, n_dev, row_count):
+    own_width = got.shape[2]
     size_a = 2 * n_dev
     padded = size_a * row_count
-    chan_filters = select_filters(filters, group_index)
-    sent = jnp.stack([mixed.T, chan_filters], axis=0).reshape(2, n_dev, own_width, row_count)
-    sent = sent.transpose(1, 0, 2, 3)
-    got = lax.all_to_all(sent, ("outer", "inner"), split_axis=0, concat_axis=0, tiled=True)
     stacked = got.reshape(n_dev, 2 * own_width, row_count).astype(jnp.float32)
     first_cos, first_sin = dft_table(size_a, n_dev, size_a)
     first = contract("kn,ncb->kcb", jnp.concatenate([first_cos, -first_sin], axis=0), stacked)
@@ -127,8 +120,36 @@
         jnp.concatenate([back_cos, -back_sin], axis=1),
         jnp.concatenate([real_part, imag_part], axis=0),
     )
-    outcome = (outcome * (1.0 / padded)).astype(jnp.bfloat16)
-    returned = lax.all_to_all(outcome, ("outer", "inner"), split_axis=0, concat_axis=0, tiled=True)
+    return (outcome * (1.0 / padded)).astype(jnp.bfloat16)
+
+
+def by_channels(mixed, filters, group_index):
+    n_dev = lax.axis_size("outer") * lax.axis_size("inner")
+    row_count = mixed.shape[0]
+    channels = mixed.shape[1]
+    own_width = channels // n_dev
+    pieces = 2 if own_width % 16 == 0 else 1
+    piece_width = own_width // pieces
+    chan_filters = select_filters(filters, group_index)
+    sent = jnp.stack([mixed.T, chan_filters], axis=0).reshape(
+        2, n_dev, pieces, piece_width, row_count
+    )
+    sent = sent.transpose(2, 1, 0, 3, 4)
+    arrived = [
+        lax.all_to_all(sent[piece], ("outer", "inner"), split_axis=0, concat_axis=0, tiled=True)
+        for piece in range(pieces)
+    ]
+    results = []
+    outcome = None
+    for piece in range(pieces):
+        got = arrived[piece]
+        if outcome is not None:
+            outcome, got = lax.optimization_barrier((outcome, got))
+        outcome = convolve_block(got, n_dev, row_count)
+        results.append(
+            lax.all_to_all(outcome, ("outer", "inner"), split_axis=0, concat_axis=0, tiled=True)
+        )
+    returned = jnp.stack(results, axis=1)
     return returned.reshape(channels, row_count).T
 
 

time: 86.4 us -> 90.1 us (1.043)
  starting transfers between devices: 10.9 us -> 16.2 us
  waiting for transfers between devices: 40.6 us -> 38.7 us
    all_to_all x1 -> x2, waiting for transfers between devices: 25.4 us -> 18.6 us  [by_channels(): lax.all_to_all(sent[piece], ('outer', 'inner'), split_axis=0, concat_axis...]
    all_to_all x1 -> x2, waiting for transfers between devices: 15.3 us -> 20.1 us  [by_channels(): lax.all_to_all(outcome, ('outer', 'inner'), split_axis=0, concat_axis=0,...]
    all_to_all x1 -> x2, starting transfers between devices: 7.3 us -> 10.6 us  [by_channels(): lax.all_to_all(sent[piece], ('outer', 'inner'), split_axis=0, concat_axis...]
    all_to_all x1 -> x2, starting transfers between devices: 3.62 us -> 5.66 us  [by_channels(): lax.all_to_all(outcome, ('outer', 'inner'), split_axis=0, concat_axis=0,...]
    squeeze x0 -> x3, local copies, waits for them, and re-layouts: none -> 1.83 us  [by_channels(): sent[piece]]
    transpose x1 -> x0, local copies, waits for them, and re-layouts: 1.07 us -> none  [by_channels(): sent = sent.transpose(1, 0, 2, 3)]
    dot_general x4 -> x8, matrix products: 15.6 us -> 16.1 us  [contract(): jnp.einsum(pattern, left_op, right_op, precision=lax.Precision.HIGH, pref...]
    add x1 -> x2, other arithmetic: 2.03 us -> 1.62 us  [rotate(): real_part * cosine + imag_part * sine_part]
  transfers between devices with their start and end apart: 2 -> 4, of which waited for: 2 -> 4; matrix products, arithmetic and copies ran while one was open for 1% -> 15% of each run, Pallas kernels for 0% -> 0%
where the time goes in v5:
time: 90.1 us; the launch traced here: 89.6 us
  waiting for transfers between devices  38.7 us (43%)
  starting transfers between devices  16.2 us (18%)
  matrix products  16.1 us (18%)
  local copies, waits for them, and re-layouts  9.08 us (10%)
  other arithmetic  6.75 us (7%)
  Pallas kernels  2.48 us (3%)
    all_to_all x2, waiting for transfers between devices, by_channels(): lax.all_to_all(outcome, ('outer', 'inner'), split_axis=0, concat_axis=0,...  20.1 us
    all_to_all x2, waiting for transfers between devices, by_channels(): lax.all_to_all(sent[piece], ('outer', 'inner'), split_axis=0, concat_axis...  18.6 us
    dot_general x8, matrix products, contract(): jnp.einsum(pattern, left_op, right_op, precision=lax.Precision.HIGH, pref...  16.1 us
    all_to_all x2, starting transfers between devices, by_channels(): lax.all_to_all(sent[piece], ('outer', 'inner'), split_axis=0, concat_axis...  10.6 us
    all_to_all x2, starting transfers between devices, by_channels(): lax.all_to_all(outcome, ('outer', 'inner'), split_axis=0, concat_axis=0,...  5.66 us
    unnamed x9, local copies, waits for them, and re-layouts  2.92 us
    pallas_call x1, Pallas kernels, select_filters(): pl.pallas_call(select_kernel, out_shape=jax.ShapeDtypeStruct((channels, f...  2.48 us
    squeeze x3, local copies, waits for them, and re-layouts, by_channels(): sent[piece]  1.83 us
  transfers between devices with their start and end apart: 4, of which 4 were waited for; matrix products, arithmetic and copies ran while one was open for 15% of the time, Pallas kernels for 0%

profile of v5, /device:TPU:0, one launch (start us, length us, event | category | flops | bytes accessed | tf_op | source)
XLA Modules:
  0.0 89.6 jit_solution(17705454071665739005)
XLA Ops:
  0.0 1.3 %copy.39 = bf16[128,2048]{0,1:T(8,128)(2,1)S(1)} copy(bf16[128,2048]{1,0:T(8,128)(2,1)} %param.7) | data formatting | bytes 1048576 | tf_op args[1]
  1.3 1.3 %copy.40 = bf16[128,2048]{0,1:T(8,128)(2,1)S(1)} copy(bf16[128,2048]{1,0:T(8,128)(2,1)} %param.8) | data formatting | bytes 1048576 | tf_op args[2]
  2.7 1.4 %copy.41.index_ref = s32[2048,1]{1,0:T(8,128)} copy(s32[2048,1]{0,1:T(1,128)S(1)} %bitcast.49) | data formatting | bytes 16384 | tf_op jit(solution)/shard_map/reshape | solution.py:73
  4.0 0.1 multiply_convert_fusion
  4.2 2.5 %shard_map.64 = bf16[2048,128]{1,0:T(8,128)(2,1)} custom-call(s32[2048,1]{1,0:T(8,128)} %copy.41.index_ref, bf16[128,128]{1,0:T(8,128)(2,1)} %filters_ref.1), custom_call_target="tpu_custom_call" | custom-call | tf_op jit(solution)/shard_map/pallas_call | solution.py:70
  6.7 1.1 %maximum_bitcast_fusion = bf16[2,32,2,32,128]{4,3,0,1,2:T(8,128)(2,1)S(1)} fusion(bf16[1,32,2,32,128]{4,3,2,1,0:T(8,128)(2,1)} %bitcast.46, bf16[1,32,2,32,128]{4,3,2,1,0:T(8,128)(2,1)S(1)} %bitcast.43), kind=kLoop, calls=%fused_computation.28 | loop fusion | flops 524288 | bytes 2097152 | tf_op jit(solution)/shard_map/transpose | solution.py:137
  7.8 0.1 slice_bitcast_fusion
  7.9 0.9 copy.42
  8.8 7.3 %all-to-all-start = ((bf16[32,2,32,128]{3,2,1,0:T(8,128)(2,1)}), bf16[32,2,32,128]{3,2,1,0:T(8,128)(2,1)S(1)}, u32[]{:S(2)}, u32[]{:S(2)}) async-start(bf16[32,2,32,128]{3,2,1,0:T(8,128)(2,1)} %copy.42), calls=%async_computation | async-start | bytes 1048576 | tf_op jit(solution)/shard_map/all_to_all | solution.py:139
  16.1 0.9 copy.47
  16.9 0.1 sine_negate_fusion
  17.0 0.1 sine_negate_fusion.1
  17.1 0.1 fusion.61
  17.3 0.3 fusion.51
  17.5 0.3 broadcast_multiply_fusion
  17.8 13.8 %all-to-all-done = bf16[32,2,32,128]{3,2,1,0:T(8,128)(2,1)S(1)} async-done(((bf16[32,2,32,128]{3,2,1,0:T(8,128)(2,1)}), bf16[32,2,32,128]{3,2,1,0:T(8,128)(2,1)S(1)}, u32[]{:S(2)}, u32[]{:S(2)}) %all-to-all-start) | async-done | bytes 524320 | tf_op jit(solution)/shard_map/all_to_all | solution.py:139
  31.6 3.3 %all-to-all-start.2 = ((bf16[32,2,32,128]{3,2,1,0:T(8,128)(2,1)}), bf16[32,2,32,128]{3,2,1,0:T(8,128)(2,1)S(1)}, u32[]{:S(2)}, u32[]{:S(2)}) async-start(bf16[32,2,32,128]{3,2,1,0:T(8,128)(2,1)} %copy.47), calls=%async_computation.2 | async-start | bytes 1048576 | tf_op jit(solution)/shard_map/all_to_all | solution.py:139
  34.9 0.3 copy.43
  35.2 1.4 %fusion.71 = f32[128,64,128]{2,0,1:T(8,128)S(1)} fusion(bf16[32,64,128]{2,0,1:T(8,128)(2,1)S(1)} %bitcast.45, f32[64,32]{0,1:T(8,128)S(1)} %get-tuple-element.21, f32[64,32]{0,1:T(8,128)S(1)} %get-tuple-element.22), kind=kOutput, calls=%fused_computation.102 | convolution fusion | flops 201330688 | bytes 4734976 | tf_op jit(solution)/shard_map/kn,ncb->kcb/dot_general | solution.py:11
  36.6 1.0 %multiply_add_fusion.1 = (f32[64,64,128]{2,0,1:T(8,128)S(1)}, f32[64,64,128]{2,0,1:T(8,128)S(1)}) fusion(f32[128,64,128]{2,0,1:T(8,128)S(1)} %fusion.71, f32[64,128]{1,0:T(8,128)S(1)} %get-tuple-element.23, f32[64,128]{1,0:T(8,128)S(1)} %get-tuple-element.24), kind=kLoop, calls=%fused_computation.23 | loop fusion | flops 3145728 | bytes 8454144 | tf_op jit(solution)/shard_map/add | solution.py:38
  37.6 0.4 pad_maximum_fusion
  38.0 3.9 %fusion.2 = f32[64,64,256]{2,1,0:T(8,128)S(1)} fusion(f32[64,64,256]{2,0,1:T(8,128)S(1)} %pad_maximum_fusion, f32[128,128]{1,0:T(8,128)S(1)} %fusion.51, f32[128,128]{1,0:T(8,128)S(1)} %get-tuple-element.26, f32[128,128]{1,0:T(8,128)S(1)} %get-tuple-element.25), kind=kOutput, calls=%fused_computation.4 | convolution fusion | flops 1610809344 | bytes 8585216 | tf_op jit(solution)/shard_map/kcb,bq->kcq/dot_general | solution.py:11
  41.9 0.3 multiply_subtract_fusion.5
  42.2 1.0 %fusion.4 = f32[64,32,256]{2,1,0:T(8,128)S(1)} fusion(f32[64,32,128]{2,1,0:T(8,128)S(1)} %get-tuple-element.14, f32[64,32,128]{2,1,0:T(8,128)S(1)} %get-tuple-element.13, f32[128,128]{1,0:T(8,128)S(1)} %fusion.51, f32[128,128]{1,0:T(8,128)S(1)} %get-tuple-element.25, f32[128,128]{1,0:T(8,128)S(1)} %get-tuple-element.26), kind=kOutput, calls=%fused_computation.6 | convolution fusion | flops 806027264 | bytes 4390912 | tf_op jit(solution)/shard_map/kcq,qb->kcb/dot_general | solution.py:11
  43.2 0.3 multiply_subtract_fusion.4
  43.6 0.2 pad_maximum_fusion.2
  43.8 1.7 %fusion.25 = bf16[32,32,128]{2,0,1:T(8,128)(2,1)S(1)} fusion(f32[128,32,128]{2,1,0:T(8,128)S(1)} %pad_maximum_fusion.2, f32[32,64]{1,0:T(8,128)S(1)} %get-tuple-element.27, f32[32,64]{1,0:T(8,128)S(1)} %get-tuple-element.28), kind=kOutput, calls=%fused_computation.27 | convolution fusion | flops 100929536 | bytes 2375680 | tf_op jit(solution)/shard_map/nk,kcb->ncb/dot_general | solution.py:11
  45.5 4.8 %all-to-all-done.2 = bf16[32,2,32,128]{3,2,1,0:T(8,128)(2,1)S(1)} async-done(((bf16[32,2,32,128]{3,2,1,0:T(8,128)(2,1)}), bf16[32,2,32,128]{3,2,1,0:T(8,128)(2,1)S(1)}, u32[]{:S(2)}, u32[]{:S(2)}) %all-to-all-start.2) | async-done | bytes 524320 | tf_op jit(solution)/shard_map/all_to_all | solution.py:139
  50.2 1.4 %fusion.31 = f32[128,64,128]{2,0,1:T(8,128)S(1)} fusion(bf16[32,64,128]{2,1,0:T(8,128)(2,1)S(1)} %bitcast.44, f32[64,32]{0,1:T(8,128)S(1)} %get-tuple-element.21, f32[64,32]{0,1:T(8,128)S(1)} %get-tuple-element.22), kind=kOutput, calls=%fused_computation.45 | convolution fusion | flops 201330688 | bytes 4734976 | tf_op jit(solution)/shard_map/kn,ncb->kcb/dot_general | solution.py:11
  51.6 0.7 multiply_add_fusion
  52.3 0.6 pad_maximum_fusion.1
  52.9 4.0 %fusion = f32[64,64,256]{2,1,0:T(8,128)S(1)} fusion(f32[64,64,256]{2,0,1:T(8,128)S(1)} %pad_maximum_fusion.1, f32[128,128]{1,0:T(8,128)S(1)} %fusion.51, f32[128,128]{1,0:T(8,128)S(1)} %get-tuple-element.26, f32[128,128]{1,0:T(8,128)S(1)} %get-tuple-element.25), kind=kOutput, calls=%fused_computation.2 | convolution fusion | flops 1610809344 | bytes 8585216 | tf_op jit(solution)/shard_map/kcb,bq->kcq/dot_general | solution.py:11
  56.9 0.3 multiply_subtract_fusion.3
  57.2 1.0 %fusion.8 = f32[64,32,256]{2,1,0:T(8,128)S(1)} fusion(f32[64,32,128]{2,1,0:T(8,128)S(1)} %get-tuple-element.12, f32[64,32,128]{2,1,0:T(8,128)S(1)} %get-tuple-element.11, f32[128,128]{1,0:T(8,128)S(1)} %fusion.51, f32[128,128]{1,0:T(8,128)S(1)} %get-tuple-element.25, f32[128,128]{1,0:T(8,128)S(1)} %get-tuple-element.26), kind=kOutput, calls=%fused_computation.11 | convolution fusion | flops 806027264 | bytes 4390912 | tf_op jit(solution)/shard_map/kcq,qb->kcb/dot_general | solution.py:11
  58.2 0.3 multiply_subtract_fusion.2
  58.6 0.2 pad_maximum_fusion.3
  58.8 0.0 copy-start
  58.8 1.7 %fusion.22 = bf16[32,32,128]{2,0,1:T(8,128)(2,1)S(1)} fusion(f32[128,32,128]{2,1,0:T(8,128)S(1)} %pad_maximum_fusion.3, f32[32,64]{1,0:T(8,128)S(1)} %get-tuple-element.27, f32[32,64]{1,0:T(8,128)S(1)} %get-tuple-element.28), kind=kOutput, calls=%fused_computation.26 | convolution fusion | flops 100929536 | bytes 2375680 | tf_op jit(solution)/shard_map/nk,kcb->ncb/dot_general | solution.py:11
  60.5 0.0 copy-start.2
  60.5 0.8 copy.51
  61.3 3.1 %all-to-all-start.3 = ((bf16[32,32,128]{2,1,0:T(8,128)(2,1)}), bf16[32,32,128]{2,1,0:T(8,128)(2,1)S(1)}, u32[]{:S(2)}, u32[]{:S(2)}) async-start(bf16[32,32,128]{2,1,0:T(8,128)(2,1)} %copy.51), calls=%async_computation.3 | async-start | bytes 524288 | tf_op jit(solution)/shard_map/all_to_all | solution.py:150
  64.4 0.8 copy.46
  65.2 9.8 %all-to-all-done.3 = bf16[32,32,128]{2,1,0:T(8,128)(2,1)S(1)} async-done(((bf16[32,32,128]{2,1,0:T(8,128)(2,1)}), bf16[32,32,128]{2,1,0:T(8,128)(2,1)S(1)}, u32[]{:S(2)}, u32[]{:S(2)}) %all-to-all-start.3) | async-done | bytes 262176 | tf_op jit(solution)/shard_map/all_to_all | solution.py:150
  75.0 2.6 %all-to-all-start.1 = ((bf16[32,32,128]{2,1,0:T(8,128)(2,1)}), bf16[32,32,128]{2,1,0:T(8,128)(2,1)S(1)}, u32[]{:S(2)}, u32[]{:S(2)}) async-start(bf16[32,32,128]{2,1,0:T(8,128)(2,1)} %copy.46), calls=%async_computation.1 | async-start | bytes 524288 | tf_op jit(solution)/shard_map/all_to_all | solution.py:150
  77.6 0.3 copy.38
  77.9 10.3 %all-to-all-done.1 = bf16[32,32,128]{2,1,0:T(8,128)(2,1)S(1)} async-done(((bf16[32,32,128]{2,1,0:T(8,128)(2,1)}), bf16[32,32,128]{2,1,0:T(8,128)(2,1)S(1)}, u32[]{:S(2)}, u32[]{:S(2)}) %all-to-all-start.1) | async-done | bytes 262176 | tf_op jit(solution)/shard_map/all_to_all | solution.py:150
  88.3 0.3 fusion.30
  88.6 1.0 %copy.52 = bf16[128,2048]{1,0:T(8,128)(2,1)} copy(bf16[128,2048]{0,1:T(8,128)(2,1)S(1)} %fusion.30) | data formatting | bytes 1048576 | tf_op jit(solution)/shard_map/convert_element_type | solution.py:160
  (5 shorter events, 0.1 us)
Async XLA Ops:
  0.0 2.7 %copy-start.1 = (s32[2048]{0:T(1024)S(1)}, s32[2048]{0:T(1024)}, u32[]{:S(2)}) copy-start(s32[2048]{0:T(1024)} %param.10) | copy-start | bytes 24580
  8.8 22.9 %all-to-all-start = ((bf16[32,2,32,128]{3,2,1,0:T(8,128)(2,1)}), bf16[32,2,32,128]{3,2,1,0:T(8,128)(2,1)S(1)}, u32[]{:S(2)}, u32[]{:S(2)}) async-start(bf16[32,2,32,128]{3,2,1,0:T(8,128)(2,1)} %copy.42), calls=%async_computation | async-start | bytes 1048576 | tf_op jit(solution)/shard_map/all_to_all | solution.py:139
  31.6 18.6 %all-to-all-start.2 = ((bf16[32,2,32,128]{3,2,1,0:T(8,128)(2,1)}), bf16[32,2,32,128]{3,2,1,0:T(8,128)(2,1)S(1)}, u32[]{:S(2)}, u32[]{:S(2)}) async-start(bf16[32,2,32,128]{3,2,1,0:T(8,128)(2,1)} %copy.47), calls=%async_computation.2 | async-start | bytes 1048576 | tf_op jit(solution)/shard_map/all_to_all | solution.py:139
  58.8 18.8 %copy-start = (bf16[128,2048]{1,0:T(8,128)(2,1)S(1)}, bf16[128,2048]{1,0:T(8,128)(2,1)}, u32[]{:S(2)}) copy-start(bf16[128,2048]{1,0:T(8,128)(2,1)} %param.6) | copy-start | bytes 1572868
  60.5 27.7 %copy-start.2 = (f32[2048]{0:T(1024)S(1)}, f32[2048]{0:T(1024)}, u32[]{:S(2)}) copy-start(f32[2048]{0:T(1024)} %param.11) | copy-start | bytes 24580
  61.3 13.7 %all-to-all-start.3 = ((bf16[32,32,128]{2,1,0:T(8,128)(2,1)}), bf16[32,32,128]{2,1,0:T(8,128)(2,1)S(1)}, u32[]{:S(2)}, u32[]{:S(2)}) async-start(bf16[32,32,128]{2,1,0:T(8,128)(2,1)} %copy.51), calls=%async_computation.3 | async-start | bytes 524288 | tf_op jit(solution)/shard_map/all_to_all | solution.py:150
  75.0 13.2 %all-to-all-start.1 = ((bf16[32,32,128]{2,1,0:T(8,128)(2,1)}), bf16[32,32,128]{2,1,0:T(8,128)(2,1)S(1)}, u32[]{:S(2)}, u32[]{:S(2)}) async-start(bf16[32,32,128]{2,1,0:T(8,128)(2,1)} %copy.46), calls=%async_computation.1 | async-start | bytes 524288 | tf_op jit(solution)/shard_map/all_to_all | solution.py:150

commit v6 on v5

--- a/solution.py
+++ b/solution.py
@@ -146,10 +146,10 @@
         if outcome is not None:
             outcome, got = lax.optimization_barrier((outcome, got))
         outcome = convolve_block(got, n_dev, row_count)
-        results.append(
-            lax.all_to_all(outcome, ("outer", "inner"), split_axis=0, concat_axis=0, tiled=True)
-        )
-    returned = jnp.stack(results, axis=1)
+        results.append(outcome)
+    returned = lax.all_to_all(
+        jnp.stack(results, axis=1), ("outer", "inner"), split_axis=0, concat_axis=0, tiled=True
+    )
     return returned.reshape(channels, row_count).T
 
 

time: 90.1 us -> 82 us (0.910)
  waiting for transfers between devices: 38.7 us -> 33.8 us
  starting transfers between devices: 16.2 us -> 13.6 us
    all_to_all x2 -> x1, waiting for transfers between devices: 20.1 us -> 15.3 us  [by_channels(): lax.all_to_all(jnp.stack(results, axis=1), ('outer', 'inner'), split_axis...]
    all_to_all x2 -> x1, starting transfers between devices: 5.66 us -> 3.07 us  [by_channels(): lax.all_to_all(jnp.stack(results, axis=1), ('outer', 'inner'), split_axis...]
    convert_element_type x2 -> x0, local copies, waits for them, and re-layouts: 1.61 us -> none  [convolve_block(): return (outcome * (1.0 / padded)).astype(jnp.bfloat16)]
    another operation x0 -> x1, local copies, waits for them, and re-layouts: none -> 1 us  [by_channels(): jnp.stack(results, axis=1)]
  transfers between devices with their start and end apart: 4 -> 3, of which waited for: 4 -> 3; matrix products, arithmetic and copies ran while one was open for 15% -> 15% of each run, Pallas kernels for 0% -> 0%
where the time goes in v6:
time: 82 us; the launch traced here: 81.5 us
  waiting for transfers between devices  33.8 us (41%)
  matrix products  16.1 us (20%)
  starting transfers between devices  13.6 us (17%)
  local copies, waits for them, and re-layouts  8.45 us (10%)
  other arithmetic  6.75 us (8%)
  Pallas kernels  2.48 us (3%)
    all_to_all x2, waiting for transfers between devices, by_channels(): lax.all_to_all(sent[piece], ('outer', 'inner'), split_axis=0, concat_axis...  18.6 us
    dot_general x8, matrix products, contract(): jnp.einsum(pattern, left_op, right_op, precision=lax.Precision.HIGH, pref...  16.1 us
    all_to_all x1, waiting for transfers between devices, by_channels(): lax.all_to_all(jnp.stack(results, axis=1), ('outer', 'inner'), split_axis...  15.3 us
    all_to_all x2, starting transfers between devices, by_channels(): lax.all_to_all(sent[piece], ('outer', 'inner'), split_axis=0, concat_axis...  10.6 us
    all_to_all x1, starting transfers between devices, by_channels(): lax.all_to_all(jnp.stack(results, axis=1), ('outer', 'inner'), split_axis...  3.07 us
    unnamed x9, local copies, waits for them, and re-layouts  2.92 us
    pallas_call x1, Pallas kernels, select_filters(): pl.pallas_call(select_kernel, out_shape=jax.ShapeDtypeStruct((channels, f...  2.48 us
    squeeze x3, local copies, waits for them, and re-layouts, by_channels(): sent[piece]  1.83 us
  transfers between devices with their start and end apart: 3, of which 3 were waited for; matrix products, arithmetic and copies ran while one was open for 15% of the time, Pallas kernels for 0%

profile of v6, /device:TPU:0, one launch (start us, length us, event | category | flops | bytes accessed | tf_op | source)
XLA Modules:
  0.0 81.5 jit_solution(1699924887249367415)
XLA Ops:
  0.0 1.3 %copy.39 = bf16[128,2048]{0,1:T(8,128)(2,1)S(1)} copy(bf16[128,2048]{1,0:T(8,128)(2,1)} %param.7) | data formatting | bytes 1048576 | tf_op args[1]
  1.3 1.3 %copy.40 = bf16[128,2048]{0,1:T(8,128)(2,1)S(1)} copy(bf16[128,2048]{1,0:T(8,128)(2,1)} %param.8) | data formatting | bytes 1048576 | tf_op args[2]
  2.7 0.0 copy-done.1
  2.7 1.4 %copy.41.index_ref = s32[2048,1]{1,0:T(8,128)} copy(s32[2048,1]{0,1:T(1,128)S(1)} %bitcast.49) | data formatting | bytes 16384 | tf_op jit(solution)/shard_map/reshape | solution.py:73
  4.0 0.1 multiply_convert_fusion
  4.2 2.5 %shard_map.64 = bf16[2048,128]{1,0:T(8,128)(2,1)} custom-call(s32[2048,1]{1,0:T(8,128)} %copy.41.index_ref, bf16[128,128]{1,0:T(8,128)(2,1)} %filters_ref.1), custom_call_target="tpu_custom_call" | custom-call | tf_op jit(solution)/shard_map/pallas_call | solution.py:70
  6.6 1.1 %maximum_bitcast_fusion = bf16[2,32,2,32,128]{4,3,0,1,2:T(8,128)(2,1)S(1)} fusion(bf16[1,32,2,32,128]{4,3,2,1,0:T(8,128)(2,1)} %bitcast.47, bf16[1,32,2,32,128]{4,3,2,1,0:T(8,128)(2,1)S(1)} %bitcast.44), kind=kLoop, calls=%fused_computation.29 | loop fusion | flops 524288 | bytes 2097152 | tf_op jit(solution)/shard_map/transpose | solution.py:137
  7.8 0.1 slice_bitcast_fusion
  7.9 0.9 %copy.42 = bf16[32,2,32,128]{3,2,1,0:T(8,128)(2,1)} copy(bf16[32,2,32,128]{3,2,0,1:T(8,128)(2,1)S(1)} %get-tuple-element.20) | data formatting | bytes 1048576 | tf_op jit(solution)/shard_map/squeeze | solution.py:139
  8.8 7.3 %all-to-all-start = ((bf16[32,2,32,128]{3,2,1,0:T(8,128)(2,1)}), bf16[32,2,32,128]{3,2,1,0:T(8,128)(2,1)S(1)}, u32[]{:S(2)}, u32[]{:S(2)}) async-start(bf16[32,2,32,128]{3,2,1,0:T(8,128)(2,1)} %copy.42), calls=%async_computation | async-start | bytes 1048576 | tf_op jit(solution)/shard_map/all_to_all | solution.py:139
  16.1 0.9 %copy.46 = bf16[32,2,32,128]{3,2,1,0:T(8,128)(2,1)} copy(bf16[32,2,32,128]{3,2,0,1:T(8,128)(2,1)S(1)} %get-tuple-element.19) | data formatting | bytes 1048576 | tf_op jit(solution)/shard_map/squeeze | solution.py:139
  16.9 0.1 sine_negate_fusion
  17.0 0.1 sine_negate_fusion.1
  17.1 0.1 fusion.64
  17.3 0.3 fusion.54
  17.5 0.3 broadcast_multiply_fusion
  17.8 13.8 %all-to-all-done = bf16[32,2,32,128]{3,2,1,0:T(8,128)(2,1)S(1)} async-done(((bf16[32,2,32,128]{3,2,1,0:T(8,128)(2,1)}), bf16[32,2,32,128]{3,2,1,0:T(8,128)(2,1)S(1)}, u32[]{:S(2)}, u32[]{:S(2)}) %all-to-all-start) | async-done | bytes 524320 | tf_op jit(solution)/shard_map/all_to_all | solution.py:139
  31.6 3.3 %all-to-all-start.1 = ((bf16[32,2,32,128]{3,2,1,0:T(8,128)(2,1)}), bf16[32,2,32,128]{3,2,1,0:T(8,128)(2,1)S(1)}, u32[]{:S(2)}, u32[]{:S(2)}) async-start(bf16[32,2,32,128]{3,2,1,0:T(8,128)(2,1)} %copy.46), calls=%async_computation.1 | async-start | bytes 1048576 | tf_op jit(solution)/shard_map/all_to_all | solution.py:139
  34.9 0.3 copy.43
  35.2 1.4 %fusion.74 = f32[128,64,128]{2,0,1:T(8,128)S(1)} fusion(bf16[32,64,128]{2,0,1:T(8,128)(2,1)S(1)} %bitcast.46, f32[64,32]{0,1:T(8,128)S(1)} %get-tuple-element.21, f32[64,32]{0,1:T(8,128)S(1)} %get-tuple-element.22), kind=kOutput, calls=%fused_computation.103 | convolution fusion | flops 201330688 | bytes 4734976 | tf_op jit(solution)/shard_map/kn,ncb->kcb/dot_general | solution.py:11
  36.6 1.0 %multiply_add_fusion.1 = (f32[64,64,128]{2,0,1:T(8,128)S(1)}, f32[64,64,128]{2,0,1:T(8,128)S(1)}) fusion(f32[128,64,128]{2,0,1:T(8,128)S(1)} %fusion.74, f32[64,128]{1,0:T(8,128)S(1)} %get-tuple-element.23, f32[64,128]{1,0:T(8,128)S(1)} %get-tuple-element.24), kind=kLoop, calls=%fused_computation.23 | loop fusion | flops 3145728 | bytes 8454144 | tf_op jit(solution)/shard_map/add | solution.py:38
  37.6 0.4 pad_maximum_fusion
  38.0 3.9 %fusion.2 = f32[64,64,256]{2,1,0:T(8,128)S(1)} fusion(f32[64,64,256]{2,0,1:T(8,128)S(1)} %pad_maximum_fusion, f32[128,128]{1,0:T(8,128)S(1)} %fusion.54, f32[128,128]{1,0:T(8,128)S(1)} %get-tuple-element.26, f32[128,128]{1,0:T(8,128)S(1)} %get-tuple-element.25), kind=kOutput, calls=%fused_computation.4 | convolution fusion | flops 1610809344 | bytes 8585216 | tf_op jit(solution)/shard_map/kcb,bq->kcq/dot_general | solution.py:11
  41.9 0.3 multiply_subtract_fusion.5
  42.2 1.0 %fusion.4 = f32[64,32,256]{2,1,0:T(8,128)S(1)} fusion(f32[64,32,128]{2,1,0:T(8,128)S(1)} %get-tuple-element.14, f32[64,32,128]{2,1,0:T(8,128)S(1)} %get-tuple-element.13, f32[128,128]{1,0:T(8,128)S(1)} %fusion.54, f32[128,128]{1,0:T(8,128)S(1)} %get-tuple-element.25, f32[128,128]{1,0:T(8,128)S(1)} %get-tuple-element.26), kind=kOutput, calls=%fused_computation.6 | convolution fusion | flops 806027264 | bytes 4390912 | tf_op jit(solution)/shard_map/kcq,qb->kcb/dot_general | solution.py:11
  43.2 0.3 multiply_subtract_fusion.4
  43.6 0.2 pad_maximum_fusion.2
  43.8 1.7 %fusion.25 = bf16[32,32,128]{2,0,1:T(8,128)(2,1)S(1)} fusion(f32[128,32,128]{2,1,0:T(8,128)S(1)} %pad_maximum_fusion.2, f32[32,64]{1,0:T(8,128)S(1)} %get-tuple-element.27, f32[32,64]{1,0:T(8,128)S(1)} %get-tuple-element.28), kind=kOutput, calls=%fused_computation.27 | convolution fusion | flops 100929536 | bytes 2375680 | tf_op jit(solution)/shard_map/nk,kcb->ncb/dot_general | solution.py:11
  45.5 4.8 %all-to-all-done.1 = bf16[32,2,32,128]{3,2,1,0:T(8,128)(2,1)S(1)} async-done(((bf16[32,2,32,128]{3,2,1,0:T(8,128)(2,1)}), bf16[32,2,32,128]{3,2,1,0:T(8,128)(2,1)S(1)}, u32[]{:S(2)}, u32[]{:S(2)}) %all-to-all-start.1) | async-done | bytes 524320 | tf_op jit(solution)/shard_map/all_to_all | solution.py:139
  50.2 1.4 %fusion.34 = f32[128,64,128]{2,0,1:T(8,128)S(1)} fusion(bf16[32,64,128]{2,1,0:T(8,128)(2,1)S(1)} %bitcast.45, f32[64,32]{0,1:T(8,128)S(1)} %get-tuple-element.21, f32[64,32]{0,1:T(8,128)S(1)} %get-tuple-element.22), kind=kOutput, calls=%fused_computation.46 | convolution fusion | flops 201330688 | bytes 4734976 | tf_op jit(solution)/shard_map/kn,ncb->kcb/dot_general | solution.py:11
  51.6 0.7 multiply_add_fusion
  52.3 0.6 pad_maximum_fusion.1
  52.9 4.0 %fusion = f32[64,64,256]{2,1,0:T(8,128)S(1)} fusion(f32[64,64,256]{2,0,1:T(8,128)S(1)} %pad_maximum_fusion.1, f32[128,128]{1,0:T(8,128)S(1)} %fusion.54, f32[128,128]{1,0:T(8,128)S(1)} %get-tuple-element.26, f32[128,128]{1,0:T(8,128)S(1)} %get-tuple-element.25), kind=kOutput, calls=%fused_computation.2 | convolution fusion | flops 1610809344 | bytes 8585216 | tf_op jit(solution)/shard_map/kcb,bq->kcq/dot_general | solution.py:11
  56.9 0.3 multiply_subtract_fusion.3
  57.2 1.0 %fusion.8 = f32[64,32,256]{2,1,0:T(8,128)S(1)} fusion(f32[64,32,128]{2,1,0:T(8,128)S(1)} %get-tuple-element.12, f32[64,32,128]{2,1,0:T(8,128)S(1)} %get-tuple-element.11, f32[128,128]{1,0:T(8,128)S(1)} %fusion.54, f32[128,128]{1,0:T(8,128)S(1)} %get-tuple-element.25, f32[128,128]{1,0:T(8,128)S(1)} %get-tuple-element.26), kind=kOutput, calls=%fused_computation.11 | convolution fusion | flops 806027264 | bytes 4390912 | tf_op jit(solution)/shard_map/kcq,qb->kcb/dot_general | solution.py:11
  58.2 0.3 multiply_subtract_fusion.2
  58.6 0.2 pad_maximum_fusion.3
  58.7 1.7 %fusion.28 = bf16[32,1,32,128]{3,0,2,1:T(8,128)(2,1)S(1)} fusion(f32[128,32,128]{2,1,0:T(8,128)S(1)} %pad_maximum_fusion.3, f32[32,64]{1,0:T(8,128)S(1)} %get-tuple-element.27, f32[32,64]{1,0:T(8,128)S(1)} %get-tuple-element.28), kind=kOutput, calls=%fused_computation.28 | convolution fusion | flops 100929536 | bytes 2375680 | tf_op jit(solution)/shard_map/nk,kcb->ncb/dot_general | solution.py:11
  60.5 0.0 copy-start
  60.5 0.0 copy-start.2
  60.5 0.1 pad_maximum_fusion.4
  60.6 1.0 %copy.50 = bf16[32,2,32,128]{3,2,1,0:T(8,128)(2,1)} copy(bf16[32,2,32,128]{3,0,2,1:T(8,128)(2,1)S(1)} %pad_maximum_fusion.4) | data formatting | bytes 1048576 | tf_op jit(solution)/shard_map/stack | solution.py:151
  61.6 3.1 %all-to-all-start.2 = ((bf16[32,2,32,128]{3,2,1,0:T(8,128)(2,1)}), bf16[32,2,32,128]{3,2,1,0:T(8,128)(2,1)S(1)}, u32[]{:S(2)}, u32[]{:S(2)}) async-start(bf16[32,2,32,128]{3,2,1,0:T(8,128)(2,1)} %copy.50), calls=%async_computation.2 | async-start | bytes 1048576 | tf_op jit(solution)/shard_map/all_to_all | solution.py:150
  64.6 0.0 copy-done
  64.6 0.3 copy.38
  64.9 15.3 %all-to-all-done.2 = bf16[32,2,32,128]{3,2,1,0:T(8,128)(2,1)S(1)} async-done(((bf16[32,2,32,128]{3,2,1,0:T(8,128)(2,1)}), bf16[32,2,32,128]{3,2,1,0:T(8,128)(2,1)S(1)}, u32[]{:S(2)}, u32[]{:S(2)}) %all-to-all-start.2) | async-done | bytes 524320 | tf_op jit(solution)/shard_map/all_to_all | solution.py:150
  80.2 0.3 fusion.33
  80.5 1.0 %copy.51 = bf16[128,2048]{1,0:T(8,128)(2,1)} copy(bf16[128,2048]{0,1:T(8,128)(2,1)S(1)} %fusion.33) | data formatting | bytes 1048576 | tf_op jit(solution)/shard_map/convert_element_type | solution.py:160
  (2 shorter events, 0.0 us)
Async XLA Ops:
  0.0 2.7 %copy-start.1 = (s32[2048]{0:T(1024)S(1)}, s32[2048]{0:T(1024)}, u32[]{:S(2)}) copy-start(s32[2048]{0:T(1024)} %param.10) | copy-start | bytes 24580
  8.8 22.9 %all-to-all-start = ((bf16[32,2,32,128]{3,2,1,0:T(8,128)(2,1)}), bf16[32,2,32,128]{3,2,1,0:T(8,128)(2,1)S(1)}, u32[]{:S(2)}, u32[]{:S(2)}) async-start(bf16[32,2,32,128]{3,2,1,0:T(8,128)(2,1)} %copy.42), calls=%async_computation | async-start | bytes 1048576 | tf_op jit(solution)/shard_map/all_to_all | solution.py:139
  31.6 18.6 %all-to-all-start.1 = ((bf16[32,2,32,128]{3,2,1,0:T(8,128)(2,1)}), bf16[32,2,32,128]{3,2,1,0:T(8,128)(2,1)S(1)}, u32[]{:S(2)}, u32[]{:S(2)}) async-start(bf16[32,2,32,128]{3,2,1,0:T(8,128)(2,1)} %copy.46), calls=%async_computation.1 | async-start | bytes 1048576 | tf_op jit(solution)/shard_map/all_to_all | solution.py:139
  60.5 4.2 %copy-start = (bf16[128,2048]{1,0:T(8,128)(2,1)S(1)}, bf16[128,2048]{1,0:T(8,128)(2,1)}, u32[]{:S(2)}) copy-start(bf16[128,2048]{1,0:T(8,128)(2,1)} %param.6) | copy-start | bytes 1572868
  60.5 19.7 %copy-start.2 = (f32[2048]{0:T(1024)S(1)}, f32[2048]{0:T(1024)}, u32[]{:S(2)}) copy-start(f32[2048]{0:T(1024)} %param.11) | copy-start | bytes 24580
  61.6 18.6 %all-to-all-start.2 = ((bf16[32,2,32,128]{3,2,1,0:T(8,128)(2,1)}), bf16[32,2,32,128]{3,2,1,0:T(8,128)(2,1)S(1)}, u32[]{:S(2)}, u32[]{:S(2)}) async-start(bf16[32,2,32,128]{3,2,1,0:T(8,128)(2,1)} %copy.50), calls=%async_computation.2 | async-start | bytes 1048576 | tf_op jit(solution)/shard_map/all_to_all | solution.py:150

commit v7 on v6

--- a/solution.py
+++ b/solution.py
@@ -71,6 +71,38 @@
         select_kernel,
         out_shape=jax.ShapeDtypeStruct((channels, filters.shape[0]), jnp.bfloat16),
     )(group_index.reshape(channels, 1), filters)
+
+
+def prep_kernel(key_ref, value_ref, filters_ref, index_ref, out_ref):
+    pieces, n_dev, _, piece_width, _ = out_ref.shape
+    mixed = (key_ref[...].astype(jnp.float32) * value_ref[...].astype(jnp.float32)).astype(
+        jnp.bfloat16
+    )
+    mixed_t = mixed.astype(jnp.float32).T
+    groups = filters_ref.shape[1]
+    channels = index_ref.shape[1]
+    onehot_t = (
+        lax.broadcasted_iota(jnp.int32, (groups, channels), 0) == index_ref[...]
+    ).astype(jnp.float32)
+    picked = jnp.dot(
+        filters_ref[...].astype(jnp.float32), onehot_t, preferred_element_type=jnp.float32
+    ).T
+    for dest in range(n_dev):
+        for piece in range(pieces):
+            low = (dest * pieces + piece) * piece_width
+            out_ref[piece, dest, 0] = mixed_t[low : low + piece_width].astype(out_ref.dtype)
+            out_ref[piece, dest, 1] = picked[low : low + piece_width].astype(out_ref.dtype)
+
+
+def prepare(key_in, value_in, filters, group_index, n_dev, pieces):
+    row_count, channels = key_in.shape
+    piece_width = channels // (n_dev * pieces)
+    return pl.pallas_call(
+        prep_kernel,
+        out_shape=jax.ShapeDtypeStruct(
+            (pieces, n_dev, 2, piece_width, row_count), jnp.bfloat16
+        ),
+    )(key_in, value_in, filters, group_index.reshape(1, channels))
 
 
 def complex_table(cos_part, sin_part, direction):
@@ -123,18 +155,21 @@
     return (outcome * (1.0 / padded)).astype(jnp.bfloat16)
 
 
-def by_channels(mixed, filters, group_index):
+def by_channels(mixed, key_in, value_in, filters, group_index):
     n_dev = lax.axis_size("outer") * lax.axis_size("inner")
     row_count = mixed.shape[0]
     channels = mixed.shape[1]
     own_width = channels // n_dev
     pieces = 2 if own_width % 16 == 0 else 1
     piece_width = own_width // pieces
-    chan_filters = select_filters(filters, group_index)
-    sent = jnp.stack([mixed.T, chan_filters], axis=0).reshape(
-        2, n_dev, pieces, piece_width, row_count
-    )
-    sent = sent.transpose(2, 1, 0, 3, 4)
+    if piece_width % 16 == 0:
+        sent = prepare(key_in, value_in, filters, group_index, n_dev, pieces)
+    else:
+        chan_filters = select_filters(filters, group_index)
+        sent = jnp.stack([mixed.T, chan_filters], axis=0).reshape(
+            2, n_dev, pieces, piece_width, row_count
+        )
+        sent = sent.transpose(2, 1, 0, 3, 4)
     arrived = [
         lax.all_to_all(sent[piece], ("outer", "inner"), split_axis=0, concat_axis=0, tiled=True)
         for piece in range(pieces)
@@ -155,7 +190,7 @@
 
 def on_device(query, key_in, value_in, filters, group_index, skip_gain):
     mixed = (key_in.astype(jnp.float32) * value_in.astype(jnp.float32)).astype(jnp.bfloat16)
-    convolved = by_channels(mixed, filters, group_index)
+    convolved = by_channels(mixed, key_in, value_in, filters, group_index)
     mixed_wide = mixed.astype(jnp.float32)
     return (query.astype(jnp.float32) * (convolved + skip_gain[None, :] * mixed_wide)).astype(
         jnp.bfloat16

time: 82 us -> 78.6 us (0.959)
  local copies, waits for them, and re-layouts: 8.45 us -> 5.09 us
  other arithmetic: 6.75 us -> 5.7 us
  waiting for transfers between devices: 33.8 us -> 34.7 us
    unnamed x9 -> x11, local copies, waits for them, and re-layouts: 2.92 us -> 0.83 us
    all_to_all x2, waiting for transfers between devices: 18.6 us -> 20 us  [by_channels(): lax.all_to_all(sent[piece], ('outer', 'inner'), split_axis=0, concat_axis...]
    reshape x1 -> x0, local copies, waits for them, and re-layouts: 1.35 us -> none  [select_filters(): group_index.reshape(channels, 1)]
    transpose x1 -> x0, other arithmetic: 1.14 us -> none  [by_channels(): sent = sent.transpose(2, 1, 0, 3, 4)]
    squeeze x3 -> x1, local copies, waits for them, and re-layouts: 1.83 us -> 2.25 us  [by_channels(): sent[piece]]
where the time goes in v7:
time: 78.6 us; the launch traced here: 78.1 us
  waiting for transfers between devices  34.7 us (44%)
  matrix products  16.3 us (21%)
  starting transfers between devices  13.4 us (17%)
  other arithmetic  5.7 us (7%)
  local copies, waits for them, and re-layouts  5.09 us (6%)
  Pallas kernels  2.66 us (3%)
    all_to_all x2, waiting for transfers between devices, by_channels(): lax.all_to_all(sent[piece], ('outer', 'inner'), split_axis=0, concat_axis...  20 us
    dot_general x8, matrix products, contract(): jnp.einsum(pattern, left_op, right_op, precision=lax.Precision.HIGH, pref...  16.3 us
    all_to_all x1, waiting for transfers between devices, by_channels(): lax.all_to_all(jnp.stack(results, axis=1), ('outer', 'inner'), split_axis...  14.7 us
    all_to_all x2, starting transfers between devices, by_channels(): lax.all_to_all(sent[piece], ('outer', 'inner'), split_axis=0, concat_axis...  10.4 us
    all_to_all x1, starting transfers between devices, by_channels(): lax.all_to_all(jnp.stack(results, axis=1), ('outer', 'inner'), split_axis...  3.08 us
    pallas_call x1, Pallas kernels, prepare(): pl.pallas_call(prep_kernel, out_shape=jax.ShapeDtypeStruct((pieces, n_dev...  2.66 us
    squeeze x1, local copies, waits for them, and re-layouts, by_channels(): sent[piece]  2.25 us
    add x2, other arithmetic, rotate(): real_part * cosine + imag_part * sine_part  1.92 us
  transfers between devices with their start and end apart: 3, of which 3 were waited for; matrix products, arithmetic and copies ran while one was open for 15% of the time, Pallas kernels for 0%

profile of v7, /device:TPU:0, one launch (start us, length us, event | category | flops | bytes accessed | tf_op | source)
XLA Modules:
  0.0 78.1 jit_solution(6392936792068708843)
XLA Ops:
  0.0 2.7 %shard_map.64 = bf16[2,32,2,32,128]{4,3,2,1,0:T(8,128)(2,1)} custom-call(bf16[128,2048]{1,0:T(8,128)(2,1)} %key_ref.1, bf16[128,2048]{1,0:T(8,128)(2,1)} %value_ref.1, bf16[128,128]{1,0:T(8,128)(2,1)} %filters_ref.1, s32[1,2048]{1,0:T(1,128)} %bitcast.40), custom_call_target="tpu_custom_call" | custom-call | tf_op jit(solution)/shard_map/pallas_call | solution.py:100
  2.7 2.3 %slice_bitcast_fusion = (bf16[32,2,32,128]{3,2,1,0:T(8,128)(2,1)}, bf16[32,2,32,128]{3,2,1,0:T(8,128)(2,1)}) fusion(bf16[2,32,2,32,128]{4,3,2,1,0:T(8,128)(2,1)} %shard_map.64), kind=kLoop, calls=%fused_computation.42 | loop fusion | bytes 2097152 | tf_op jit(solution)/shard_map/squeeze | solution.py:174
  4.9 7.3 %all-to-all-start = ((bf16[32,2,32,128]{3,2,1,0:T(8,128)(2,1)}), bf16[32,2,32,128]{3,2,1,0:T(8,128)(2,1)S(1)}, u32[]{:S(2)}, u32[]{:S(2)}) async-start(bf16[32,2,32,128]{3,2,1,0:T(8,128)(2,1)} %get-tuple-element.20), calls=%async_computation | async-start | bytes 1048576 | tf_op jit(solution)/shard_map/all_to_all | solution.py:174
  12.2 0.1 sine_negate_fusion
  12.3 0.1 sine_negate_fusion.1
  12.4 0.1 fusion.66
  12.6 0.3 fusion.56
  12.8 0.3 broadcast_multiply_fusion
  13.1 14.7 %all-to-all-done = bf16[32,2,32,128]{3,2,1,0:T(8,128)(2,1)S(1)} async-done(((bf16[32,2,32,128]{3,2,1,0:T(8,128)(2,1)}), bf16[32,2,32,128]{3,2,1,0:T(8,128)(2,1)S(1)}, u32[]{:S(2)}, u32[]{:S(2)}) %all-to-all-start) | async-done | bytes 524320 | tf_op jit(solution)/shard_map/all_to_all | solution.py:174
  27.8 3.1 %all-to-all-start.1 = ((bf16[32,2,32,128]{3,2,1,0:T(8,128)(2,1)}), bf16[32,2,32,128]{3,2,1,0:T(8,128)(2,1)S(1)}, u32[]{:S(2)}, u32[]{:S(2)}) async-start(bf16[32,2,32,128]{3,2,1,0:T(8,128)(2,1)} %get-tuple-element.19), calls=%async_computation.1 | async-start | bytes 1048576 | tf_op jit(solution)/shard_map/all_to_all | solution.py:174
  30.9 1.4 %fusion.36 = f32[128,64,128]{2,0,1:T(8,128)S(1)} fusion(bf16[32,64,128]{2,1,0:T(8,128)(2,1)S(1)} %bitcast.38, f32[64,32]{0,1:T(8,128)S(1)} %get-tuple-element.21, f32[64,32]{0,1:T(8,128)S(1)} %get-tuple-element.22), kind=kOutput, calls=%fused_computation.47 | convolution fusion | flops 201330688 | bytes 4734976 | tf_op jit(solution)/shard_map/kn,ncb->kcb/dot_general | solution.py:11
  32.2 1.0 %multiply_add_fusion.1 = (f32[64,64,128]{2,0,1:T(8,128)S(1)}, f32[64,64,128]{2,0,1:T(8,128)S(1)}) fusion(f32[128,64,128]{2,0,1:T(8,128)S(1)} %fusion.36, f32[64,128]{1,0:T(8,128)S(1)} %get-tuple-element.23, f32[64,128]{1,0:T(8,128)S(1)} %get-tuple-element.24), kind=kLoop, calls=%fused_computation.23 | loop fusion | flops 3145728 | bytes 8454144 | tf_op jit(solution)/shard_map/add | solution.py:38
  33.2 0.4 pad_maximum_fusion
  33.6 3.9 %fusion.2 = f32[64,64,256]{2,1,0:T(8,128)S(1)} fusion(f32[64,64,256]{2,0,1:T(8,128)S(1)} %pad_maximum_fusion, f32[128,128]{1,0:T(8,128)S(1)} %fusion.56, f32[128,128]{1,0:T(8,128)S(1)} %get-tuple-element.26, f32[128,128]{1,0:T(8,128)S(1)} %get-tuple-element.25), kind=kOutput, calls=%fused_computation.4 | convolution fusion | flops 1610809344 | bytes 8585216 | tf_op jit(solution)/shard_map/kcb,bq->kcq/dot_general | solution.py:11
  37.5 0.3 multiply_subtract_fusion.5
  37.8 1.0 %fusion.4 = f32[64,32,256]{2,1,0:T(8,128)S(1)} fusion(f32[64,32,128]{2,1,0:T(8,128)S(1)} %get-tuple-element.14, f32[64,32,128]{2,1,0:T(8,128)S(1)} %get-tuple-element.13, f32[128,128]{1,0:T(8,128)S(1)} %fusion.56, f32[128,128]{1,0:T(8,128)S(1)} %get-tuple-element.25, f32[128,128]{1,0:T(8,128)S(1)} %get-tuple-element.26), kind=kOutput, calls=%fused_computation.6 | convolution fusion | flops 806027264 | bytes 4390912 | tf_op jit(solution)/shard_map/kcq,qb->kcb/dot_general | solution.py:11
  38.9 0.3 multiply_subtract_fusion.4
  39.2 0.2 pad_maximum_fusion.2
  39.4 1.7 %fusion.25 = bf16[32,32,128]{2,0,1:T(8,128)(2,1)S(1)} fusion(f32[128,32,128]{2,1,0:T(8,128)S(1)} %pad_maximum_fusion.2, f32[32,64]{1,0:T(8,128)S(1)} %get-tuple-element.27, f32[32,64]{1,0:T(8,128)S(1)} %get-tuple-element.28), kind=kOutput, calls=%fused_computation.27 | convolution fusion | flops 100929536 | bytes 2375680 | tf_op jit(solution)/shard_map/nk,kcb->ncb/dot_general | solution.py:11
  41.1 5.3 %all-to-all-done.1 = bf16[32,2,32,128]{3,2,1,0:T(8,128)(2,1)S(1)} async-done(((bf16[32,2,32,128]{3,2,1,0:T(8,128)(2,1)}), bf16[32,2,32,128]{3,2,1,0:T(8,128)(2,1)S(1)}, u32[]{:S(2)}, u32[]{:S(2)}) %all-to-all-start.1) | async-done | bytes 524320 | tf_op jit(solution)/shard_map/all_to_all | solution.py:174
  46.4 1.4 %fusion.34 = f32[128,64,128]{2,0,1:T(8,128)S(1)} fusion(bf16[32,64,128]{2,1,0:T(8,128)(2,1)S(1)} %bitcast.37, f32[64,32]{0,1:T(8,128)S(1)} %get-tuple-element.21, f32[64,32]{0,1:T(8,128)S(1)} %get-tuple-element.22), kind=kOutput, calls=%fused_computation.45 | convolution fusion | flops 201330688 | bytes 4734976 | tf_op jit(solution)/shard_map/kn,ncb->kcb/dot_general | solution.py:11
  47.8 1.0 %multiply_add_fusion = (f32[64,64,128]{2,0,1:T(8,128)S(1)}, f32[64,64,128]{2,0,1:T(8,128)S(1)}) fusion(f32[128,64,128]{2,0,1:T(8,128)S(1)} %fusion.34, f32[64,128]{1,0:T(8,128)S(1)} %get-tuple-element.23, f32[64,128]{1,0:T(8,128)S(1)} %get-tuple-element.24), kind=kLoop, calls=%fused_computation.21 | loop fusion | flops 3145728 | bytes 8454144 | tf_op jit(solution)/shard_map/add | solution.py:38
  48.7 0.4 pad_maximum_fusion.1
  49.1 4.2 %fusion = f32[64,64,256]{2,1,0:T(8,128)S(1)} fusion(f32[64,64,256]{2,0,1:T(8,128)S(1)} %pad_maximum_fusion.1, f32[128,128]{1,0:T(8,128)S(1)} %fusion.56, f32[128,128]{1,0:T(8,128)S(1)} %get-tuple-element.26, f32[128,128]{1,0:T(8,128)S(1)} %get-tuple-element.25), kind=kOutput, calls=%fused_computation.2 | convolution fusion | flops 1610809344 | bytes 8585216 | tf_op jit(solution)/shard_map/kcb,bq->kcq/dot_general | solution.py:11
  53.3 0.3 multiply_subtract_fusion.3
  53.6 1.0 %fusion.8 = f32[64,32,256]{2,1,0:T(8,128)S(1)} fusion(f32[64,32,128]{2,1,0:T(8,128)S(1)} %get-tuple-element.12, f32[64,32,128]{2,1,0:T(8,128)S(1)} %get-tuple-element.11, f32[128,128]{1,0:T(8,128)S(1)} %fusion.56, f32[128,128]{1,0:T(8,128)S(1)} %get-tuple-element.25, f32[128,128]{1,0:T(8,128)S(1)} %get-tuple-element.26), kind=kOutput, calls=%fused_computation.11 | convolution fusion | flops 806027264 | bytes 4390912 | tf_op jit(solution)/shard_map/kcq,qb->kcb/dot_general | solution.py:11
  54.6 0.3 multiply_subtract_fusion.2
  55.0 0.2 pad_maximum_fusion.3
  55.2 1.7 %fusion.28 = bf16[32,1,32,128]{3,0,2,1:T(8,128)(2,1)S(1)} fusion(f32[128,32,128]{2,1,0:T(8,128)S(1)} %pad_maximum_fusion.3, f32[32,64]{1,0:T(8,128)S(1)} %get-tuple-element.27, f32[32,64]{1,0:T(8,128)S(1)} %get-tuple-element.28), kind=kOutput, calls=%fused_computation.28 | convolution fusion | flops 100929536 | bytes 2375680 | tf_op jit(solution)/shard_map/nk,kcb->ncb/dot_general | solution.py:11
  56.9 0.0 copy-start
  56.9 0.0 copy-start.1
  56.9 0.1 pad_maximum_fusion.4
  57.0 0.0 copy-start.2
  57.0 1.0 %copy.31 = bf16[32,2,32,128]{3,2,1,0:T(8,128)(2,1)} copy(bf16[32,2,32,128]{3,0,2,1:T(8,128)(2,1)S(1)} %pad_maximum_fusion.4) | data formatting | bytes 1048576 | tf_op jit(solution)/shard_map/stack | solution.py:186
  58.0 0.0 copy-start.3
  58.0 3.1 %all-to-all-start.2 = ((bf16[32,2,32,128]{3,2,1,0:T(8,128)(2,1)}), bf16[32,2,32,128]{3,2,1,0:T(8,128)(2,1)S(1)}, u32[]{:S(2)}, u32[]{:S(2)}) async-start(bf16[32,2,32,128]{3,2,1,0:T(8,128)(2,1)} %copy.31), calls=%async_computation.2 | async-start | bytes 1048576 | tf_op jit(solution)/shard_map/all_to_all | solution.py:185
  61.1 0.0 copy-done
  61.1 0.3 copy.32
  61.4 0.0 copy-done.1
  61.4 0.3 copy.33
  61.6 0.0 copy-done.2
  61.7 0.3 copy.24
  61.9 14.7 %all-to-all-done.2 = bf16[32,2,32,128]{3,2,1,0:T(8,128)(2,1)S(1)} async-done(((bf16[32,2,32,128]{3,2,1,0:T(8,128)(2,1)}), bf16[32,2,32,128]{3,2,1,0:T(8,128)(2,1)S(1)}, u32[]{:S(2)}, u32[]{:S(2)}) %all-to-all-start.2) | async-done | bytes 524320 | tf_op jit(solution)/shard_map/all_to_all | solution.py:185
  76.6 0.0 copy-done.3
  76.6 0.5 fusion.33
  77.1 1.0 %copy.34 = bf16[128,2048]{1,0:T(8,128)(2,1)} copy(bf16[128,2048]{0,1:T(8,128)(2,1)S(1)} %fusion.33) | data formatting | bytes 1048576 | tf_op jit(solution)/shard_map/convert_element_type | solution.py:195
Async XLA Ops:
  4.9 22.8 %all-to-all-start = ((bf16[32,2,32,128]{3,2,1,0:T(8,128)(2,1)}), bf16[32,2,32,128]{3,2,1,0:T(8,128)(2,1)S(1)}, u32[]{:S(2)}, u32[]{:S(2)}) async-start(bf16[32,2,32,128]{3,2,1,0:T(8,128)(2,1)} %get-tuple-element.20), calls=%async_computation | async-start | bytes 1048576 | tf_op jit(solution)/shard_map/all_to_all | solution.py:174
  27.8 18.6 %all-to-all-start.1 = ((bf16[32,2,32,128]{3,2,1,0:T(8,128)(2,1)}), bf16[32,2,32,128]{3,2,1,0:T(8,128)(2,1)S(1)}, u32[]{:S(2)}, u32[]{:S(2)}) async-start(bf16[32,2,32,128]{3,2,1,0:T(8,128)(2,1)} %get-tuple-element.19), calls=%async_computation.1 | async-start | bytes 1048576 | tf_op jit(solution)/shard_map/all_to_all | solution.py:174
  56.9 4.2 %copy-start = (bf16[128,2048]{1,0:T(8,128)(2,1)S(1)}, bf16[128,2048]{1,0:T(8,128)(2,1)}, u32[]{:S(2)}) copy-start(bf16[128,2048]{1,0:T(8,128)(2,1)} %key_ref.1) | copy-start | bytes 1572868
  56.9 4.5 %copy-start.1 = (bf16[128,2048]{1,0:T(8,128)(2,1)S(1)}, bf16[128,2048]{1,0:T(8,128)(2,1)}, u32[]{:S(2)}) copy-start(bf16[128,2048]{1,0:T(8,128)(2,1)} %value_ref.1) | copy-start | bytes 1572868
  57.0 4.7 %copy-start.2 = (bf16[128,2048]{1,0:T(8,128)(2,1)S(1)}, bf16[128,2048]{1,0:T(8,128)(2,1)}, u32[]{:S(2)}) copy-start(bf16[128,2048]{1,0:T(8,128)(2,1)} %param.6) | copy-start | bytes 1572868
  58.0 18.6 %copy-start.3 = (f32[2048]{0:T(1024)S(1)}, f32[2048]{0:T(1024)}, u32[]{:S(2)}) copy-start(f32[2048]{0:T(1024)} %param.11) | copy-start | bytes 24580
  58.0 18.6 %all-to-all-start.2 = ((bf16[32,2,32,128]{3,2,1,0:T(8,128)(2,1)}), bf16[32,2,32,128]{3,2,1,0:T(8,128)(2,1)S(1)}, u32[]{:S(2)}, u32[]{:S(2)}) async-start(bf16[32,2,32,128]{3,2,1,0:T(8,128)(2,1)} %copy.31), calls=%async_computation.2 | async-start | bytes 1048576 | tf_op jit(solution)/shard_map/all_to_all | solution.py:185

commit v8 on v7

--- a/solution.py
+++ b/solution.py
@@ -73,8 +73,9 @@
     )(group_index.reshape(channels, 1), filters)
 
 
-def prep_kernel(key_ref, value_ref, filters_ref, index_ref, out_ref):
-    pieces, n_dev, _, piece_width, _ = out_ref.shape
+def prep_kernel(key_ref, value_ref, filters_ref, index_ref, *out_refs):
+    pieces = len(out_refs)
+    n_dev, _, piece_width, _ = out_refs[0].shape
     mixed = (key_ref[...].astype(jnp.float32) * value_ref[...].astype(jnp.float32)).astype(
         jnp.bfloat16
     )
@@ -90,8 +91,8 @@
     for dest in range(n_dev):
         for piece in range(pieces):
             low = (dest * pieces + piece) * piece_width
-            out_ref[piece, dest, 0] = mixed_t[low : low + piece_width].astype(out_ref.dtype)
-            out_ref[piece, dest, 1] = picked[low : low + piece_width].astype(out_ref.dtype)
+            out_refs[piece][dest, 0] = mixed_t[low : low + piece_width].astype(jnp.bfloat16)
+            out_refs[piece][dest, 1] = picked[low : low + piece_width].astype(jnp.bfloat16)
 
 
 def prepare(key_in, value_in, filters, group_index, n_dev, pieces):
@@ -99,10 +100,29 @@
     piece_width = channels // (n_dev * pieces)
     return pl.pallas_call(
         prep_kernel,
-        out_shape=jax.ShapeDtypeStruct(
-            (pieces, n_dev, 2, piece_width, row_count), jnp.bfloat16
+        out_shape=tuple(
+            jax.ShapeDtypeStruct((n_dev, 2, piece_width, row_count), jnp.bfloat16)
+            for _ in range(pieces)
         ),
     )(key_in, value_in, filters, group_index.reshape(1, channels))
+
+
+def finish_kernel(returned_ref, query_ref, key_ref, value_ref, gain_ref, out_ref):
+    convolved = returned_ref[...].astype(jnp.float32).T
+    mixed = (key_ref[...].astype(jnp.float32) * value_ref[...].astype(jnp.float32)).astype(
+        jnp.bfloat16
+    )
+    out_ref[...] = (
+        query_ref[...].astype(jnp.float32)
+        * (convolved + gain_ref[...] * mixed.astype(jnp.float32))
+    ).astype(out_ref.dtype)
+
+
+def finish(returned, query, key_in, value_in, skip_gain):
+    return pl.pallas_call(
+        finish_kernel,
+        out_shape=jax.ShapeDtypeStruct(query.shape, jnp.bfloat16),
+    )(returned, query, key_in, value_in, skip_gain.reshape(1, -1))
 
 
 def complex_table(cos_part, sin_part, direction):
@@ -185,16 +205,13 @@
     returned = lax.all_to_all(
         jnp.stack(results, axis=1), ("outer", "inner"), split_axis=0, concat_axis=0, tiled=True
     )
-    return returned.reshape(channels, row_count).T
+    return returned.reshape(channels, row_count)
 
 
 def on_device(query, key_in, value_in, filters, group_index, skip_gain):
     mixed = (key_in.astype(jnp.float32) * value_in.astype(jnp.float32)).astype(jnp.bfloat16)
-    convolved = by_channels(mixed, key_in, value_in, filters, group_index)
-    mixed_wide = mixed.astype(jnp.float32)
-    return (query.astype(jnp.float32) * (convolved + skip_gain[None, :] * mixed_wide)).astype(
-        jnp.bfloat16
-    )
+    returned = by_channels(mixed, key_in, value_in, filters, group_index)
+    return finish(returned, query, key_in, value_in, skip_gain)
 
 
 def solution(mesh):

time: 78.6 us -> 76.4 us (0.972)
  blocking collectives: 0 us -> 18.5 us
  waiting for transfers between devices: 34.7 us -> 20 us
  local copies, waits for them, and re-layouts: 5.09 us -> 0.21 us
  starting transfers between devices: 13.4 us -> 10.4 us
  Pallas kernels: 2.66 us -> 5.3 us
    all_to_all x0 -> x1, blocking collectives: none -> 18.5 us  [by_channels(): lax.all_to_all(jnp.stack(results, axis=1), ('outer', 'inner'), split_axis...]
    all_to_all x1 -> x0, waiting for transfers between devices: 14.7 us -> none  [by_channels(): lax.all_to_all(jnp.stack(results, axis=1), ('outer', 'inner'), split_axis...]
    all_to_all x1 -> x0, starting transfers between devices: 3.08 us -> none  [by_channels(): lax.all_to_all(jnp.stack(results, axis=1), ('outer', 'inner'), split_axis...]
    pallas_call x1 -> x2, Pallas kernels: 2.66 us -> 5.3 us  [the longest x1 2.67 us: finish(): pl.pallas_call(finish_kernel, out_shape=jax.ShapeDtypeStruct(query.shape,...]
    squeeze x1 -> x0, local copies, waits for them, and re-layouts: 2.25 us -> none  [by_channels(): sent[piece]]
    convert_element_type x1 -> x0, local copies, waits for them, and re-layouts: 1.01 us -> none  [on_device(): (query.astype(jnp.float32) * (convolved + skip_gain[None, :] * mixed_wide...]
    unnamed x11 -> x0, local copies, waits for them, and re-layouts: 0.83 us -> none
    another operation x1, local copies, waits for them, and re-layouts: 1 us -> 0.21 us  [by_channels(): jnp.stack(results, axis=1)]
  transfers between devices with their start and end apart: 3 -> 2, of which waited for: 3 -> 2; matrix products, arithmetic and copies ran while one was open for 15% -> 14% of each run, Pallas kernels for 0% -> 0%
where the time goes in v8:
time: 76.4 us; the launch traced here: 76.1 us
  waiting for transfers between devices  20 us (26%)
  blocking collectives  18.5 us (24%)
  matrix products  16.2 us (21%)
  starting transfers between devices  10.4 us (14%)
  Pallas kernels  5.3 us (7%)
  other arithmetic  5.25 us (7%)
    all_to_all x2, waiting for transfers between devices, by_channels(): lax.all_to_all(sent[piece], ('outer', 'inner'), split_axis=0, concat_axis...  20 us
    all_to_all x1, blocking collectives, by_channels(): lax.all_to_all(jnp.stack(results, axis=1), ('outer', 'inner'), split_axis...  18.5 us
    dot_general x8, matrix products, contract(): jnp.einsum(pattern, left_op, right_op, precision=lax.Precision.HIGH, pref...  16.2 us
    all_to_all x2, starting transfers between devices, by_channels(): lax.all_to_all(sent[piece], ('outer', 'inner'), split_axis=0, concat_axis...  10.4 us
    pallas_call x1, Pallas kernels, finish(): pl.pallas_call(finish_kernel, out_shape=jax.ShapeDtypeStruct(query.shape,...  2.67 us
    pallas_call x1, Pallas kernels, prepare(): pl.pallas_call(prep_kernel, out_shape=tuple((jax.ShapeDtypeStruct((n_dev,...  2.63 us
    add x2, other arithmetic, rotate(): real_part * cosine + imag_part * sine_part  1.91 us
  transfers between devices with their start and end apart: 2, of which 2 were waited for; matrix products, arithmetic and copies ran while one was open for 14% of the time, Pallas kernels for 0%

profile of v8, /device:TPU:0, one launch (start us, length us, event | category | flops | bytes accessed | tf_op | source)
XLA Modules:
  0.0 76.1 jit_solution(11473795033136921025)
XLA Ops:
  0.0 2.6 %shard_map.64 = (bf16[32,2,32,128]{3,2,1,0:T(8,128)(2,1)}, bf16[32,2,32,128]{3,2,1,0:T(8,128)(2,1)}) custom-call(bf16[128,2048]{1,0:T(8,128)(2,1)} %key_ref.3, bf16[128,2048]{1,0:T(8,128)(2,1)} %value_ref.3, bf16[128,128]{1,0:T(8,128)(2,1)} %filters_ref.1, s32[1,2048]{1,0:T(1,128)} %bitcast.28), custom_call_target="tpu_custom_call" | custom-call | tf_op jit(solution)/shard_map/pallas_call | solution.py:101
  2.6 7.3 %all-to-all-start = ((bf16[32,2,32,128]{3,2,1,0:T(8,128)(2,1)}), bf16[32,2,32,128]{3,2,1,0:T(8,128)(2,1)S(1)}, u32[]{:S(2)}, u32[]{:S(2)}) async-start(bf16[32,2,32,128]{3,2,1,0:T(8,128)(2,1)} %get-tuple-element.8), calls=%async_computation | async-start | bytes 1048576 | tf_op jit(solution)/shard_map/all_to_all | solution.py:194
  9.9 0.1 sine_negate_fusion
  10.0 0.1 sine_negate_fusion.1
  10.1 0.1 fusion.63
  10.3 0.3 fusion.53
  10.5 0.3 broadcast_multiply_fusion
  10.8 14.7 %all-to-all-done = bf16[32,2,32,128]{3,2,1,0:T(8,128)(2,1)S(1)} async-done(((bf16[32,2,32,128]{3,2,1,0:T(8,128)(2,1)}), bf16[32,2,32,128]{3,2,1,0:T(8,128)(2,1)S(1)}, u32[]{:S(2)}, u32[]{:S(2)}) %all-to-all-start) | async-done | bytes 524320 | tf_op jit(solution)/shard_map/all_to_all | solution.py:194
  25.5 3.1 %all-to-all-start.1 = ((bf16[32,2,32,128]{3,2,1,0:T(8,128)(2,1)}), bf16[32,2,32,128]{3,2,1,0:T(8,128)(2,1)S(1)}, u32[]{:S(2)}, u32[]{:S(2)}) async-start(bf16[32,2,32,128]{3,2,1,0:T(8,128)(2,1)} %get-tuple-element.9), calls=%async_computation.1 | async-start | bytes 1048576 | tf_op jit(solution)/shard_map/all_to_all | solution.py:194
  28.6 1.4 %fusion.33 = f32[128,64,128]{2,0,1:T(8,128)S(1)} fusion(bf16[32,64,128]{2,1,0:T(8,128)(2,1)S(1)} %bitcast.25, f32[64,32]{0,1:T(8,128)S(1)} %get-tuple-element.23, f32[64,32]{0,1:T(8,128)S(1)} %get-tuple-element.24), kind=kOutput, calls=%fused_computation.40 | convolution fusion | flops 201330688 | bytes 4734976 | tf_op jit(solution)/shard_map/kn,ncb->kcb/dot_general | solution.py:11
  29.9 1.0 %multiply_add_fusion.1 = (f32[64,64,128]{2,0,1:T(8,128)S(1)}, f32[64,64,128]{2,0,1:T(8,128)S(1)}) fusion(f32[128,64,128]{2,0,1:T(8,128)S(1)} %fusion.33, f32[64,128]{1,0:T(8,128)S(1)} %get-tuple-element.25, f32[64,128]{1,0:T(8,128)S(1)} %get-tuple-element.26), kind=kLoop, calls=%fused_computation.23 | loop fusion | flops 3145728 | bytes 8454144 | tf_op jit(solution)/shard_map/add | solution.py:38
  30.9 0.4 pad_maximum_fusion
  31.3 3.9 %fusion.2 = f32[64,64,256]{2,1,0:T(8,128)S(1)} fusion(f32[64,64,256]{2,0,1:T(8,128)S(1)} %pad_maximum_fusion, f32[128,128]{1,0:T(8,128)S(1)} %fusion.53, f32[128,128]{1,0:T(8,128)S(1)} %get-tuple-element.28, f32[128,128]{1,0:T(8,128)S(1)} %get-tuple-element.27), kind=kOutput, calls=%fused_computation.4 | convolution fusion | flops 1610809344 | bytes 8585216 | tf_op jit(solution)/shard_map/kcb,bq->kcq/dot_general | solution.py:11
  35.2 0.3 multiply_subtract_fusion.5
  35.5 1.0 %fusion.4 = f32[64,32,256]{2,1,0:T(8,128)S(1)} fusion(f32[64,32,128]{2,1,0:T(8,128)S(1)} %get-tuple-element.18, f32[64,32,128]{2,1,0:T(8,128)S(1)} %get-tuple-element.17, f32[128,128]{1,0:T(8,128)S(1)} %fusion.53, f32[128,128]{1,0:T(8,128)S(1)} %get-tuple-element.27, f32[128,128]{1,0:T(8,128)S(1)} %get-tuple-element.28), kind=kOutput, calls=%fused_computation.6 | convolution fusion | flops 806027264 | bytes 4390912 | tf_op jit(solution)/shard_map/kcq,qb->kcb/dot_general | solution.py:11
  36.6 0.3 multiply_subtract_fusion.4
  36.9 0.2 pad_maximum_fusion.2
  37.1 1.7 %fusion.25 = bf16[32,32,128]{2,0,1:T(8,128)(2,1)S(1)} fusion(f32[128,32,128]{2,1,0:T(8,128)S(1)} %pad_maximum_fusion.2, f32[32,64]{1,0:T(8,128)S(1)} %get-tuple-element.29, f32[32,64]{1,0:T(8,128)S(1)} %get-tuple-element.30), kind=kOutput, calls=%fused_computation.27 | convolution fusion | flops 100929536 | bytes 2375680 | tf_op jit(solution)/shard_map/nk,kcb->ncb/dot_general | solution.py:11
  38.8 5.3 %all-to-all-done.1 = bf16[32,2,32,128]{3,2,1,0:T(8,128)(2,1)S(1)} async-done(((bf16[32,2,32,128]{3,2,1,0:T(8,128)(2,1)}), bf16[32,2,32,128]{3,2,1,0:T(8,128)(2,1)S(1)}, u32[]{:S(2)}, u32[]{:S(2)}) %all-to-all-start.1) | async-done | bytes 524320 | tf_op jit(solution)/shard_map/all_to_all | solution.py:194
  44.1 1.4 %fusion.31 = f32[128,64,128]{2,0,1:T(8,128)S(1)} fusion(bf16[32,64,128]{2,1,0:T(8,128)(2,1)S(1)} %bitcast.24, f32[64,32]{0,1:T(8,128)S(1)} %get-tuple-element.23, f32[64,32]{0,1:T(8,128)S(1)} %get-tuple-element.24), kind=kOutput, calls=%fused_computation.38 | convolution fusion | flops 201330688 | bytes 4734976 | tf_op jit(solution)/shard_map/kn,ncb->kcb/dot_general | solution.py:11
  45.5 1.0 %multiply_add_fusion = (f32[64,64,128]{2,0,1:T(8,128)S(1)}, f32[64,64,128]{2,0,1:T(8,128)S(1)}) fusion(f32[128,64,128]{2,0,1:T(8,128)S(1)} %fusion.31, f32[64,128]{1,0:T(8,128)S(1)} %get-tuple-element.25, f32[64,128]{1,0:T(8,128)S(1)} %get-tuple-element.26), kind=kLoop, calls=%fused_computation.21 | loop fusion | flops 3145728 | bytes 8454144 | tf_op jit(solution)/shard_map/add | solution.py:38
  46.4 0.4 pad_maximum_fusion.1
  46.8 4.1 %fusion = f32[64,64,256]{2,1,0:T(8,128)S(1)} fusion(f32[64,64,256]{2,0,1:T(8,128)S(1)} %pad_maximum_fusion.1, f32[128,128]{1,0:T(8,128)S(1)} %fusion.53, f32[128,128]{1,0:T(8,128)S(1)} %get-tuple-element.28, f32[128,128]{1,0:T(8,128)S(1)} %get-tuple-element.27), kind=kOutput, calls=%fused_computation.2 | convolution fusion | flops 1610809344 | bytes 8585216 | tf_op jit(solution)/shard_map/kcb,bq->kcq/dot_general | solution.py:11
  51.0 0.3 multiply_subtract_fusion.3
  51.3 1.0 %fusion.8 = f32[64,32,256]{2,1,0:T(8,128)S(1)} fusion(f32[64,32,128]{2,1,0:T(8,128)S(1)} %get-tuple-element.16, f32[64,32,128]{2,1,0:T(8,128)S(1)} %get-tuple-element.15, f32[128,128]{1,0:T(8,128)S(1)} %fusion.53, f32[128,128]{1,0:T(8,128)S(1)} %get-tuple-element.27, f32[128,128]{1,0:T(8,128)S(1)} %get-tuple-element.28), kind=kOutput, calls=%fused_computation.11 | convolution fusion | flops 806027264 | bytes 4390912 | tf_op jit(solution)/shard_map/kcq,qb->kcb/dot_general | solution.py:11
  52.3 0.3 multiply_subtract_fusion.2
  52.7 0.2 pad_maximum_fusion.3
  52.8 1.7 %fusion.28 = bf16[32,1,32,128]{3,0,2,1:T(8,128)(2,1)S(1)} fusion(f32[128,32,128]{2,1,0:T(8,128)S(1)} %pad_maximum_fusion.3, f32[32,64]{1,0:T(8,128)S(1)} %get-tuple-element.29, f32[32,64]{1,0:T(8,128)S(1)} %get-tuple-element.30), kind=kOutput, calls=%fused_computation.28 | convolution fusion | flops 100929536 | bytes 2375680 | tf_op jit(solution)/shard_map/nk,kcb->ncb/dot_general | solution.py:11
  54.6 0.1 pad_maximum_fusion.4
  54.6 0.2 copy.20
  54.8 18.5 %all_to_all.15 = bf16[32,2,32,128]{3,2,1,0:T(8,128)(2,1)} all-to-all(bf16[32,2,32,128]{3,2,1,0:T(8,128)(2,1)S(1)} %copy.20), channel_id=1, replica_groups=mesh['outer'=8,'inner'=4] {'outer','inner'}, dimensions={0} | all-to-all | bytes 1048576 | tf_op jit(solution)/shard_map/all_to_all | solution.py:205
  73.4 2.7 %shard_map.65 = bf16[128,2048]{1,0:T(8,128)(2,1)} custom-call(bf16[2048,128]{1,0:T(8,128)(2,1)} %bitcast.26, bf16[128,2048]{1,0:T(8,128)(2,1)} %query_ref.1, bf16[128,2048]{1,0:T(8,128)(2,1)} %key_ref.3, bf16[128,2048]{1,0:T(8,128)(2,1)} %value_ref.3, f32[1,2048]{1,0:T(1,128)} %bitcast.29), custom_call_target="tpu_custom_call" | custom-call | tf_op jit(solution)/shard_map/pallas_call | solution.py:122
Async XLA Ops:
  2.6 22.9 %all-to-all-start = ((bf16[32,2,32,128]{3,2,1,0:T(8,128)(2,1)}), bf16[32,2,32,128]{3,2,1,0:T(8,128)(2,1)S(1)}, u32[]{:S(2)}, u32[]{:S(2)}) async-start(bf16[32,2,32,128]{3,2,1,0:T(8,128)(2,1)} %get-tuple-element.8), calls=%async_computation | async-start | bytes 1048576 | tf_op jit(solution)/shard_map/all_to_all | solution.py:194
  25.5 18.6 %all-to-all-start.1 = ((bf16[32,2,32,128]{3,2,1,0:T(8,128)(2,1)}), bf16[32,2,32,128]{3,2,1,0:T(8,128)(2,1)S(1)}, u32[]{:S(2)}, u32[]{:S(2)}) async-start(bf16[32,2,32,128]{3,2,1,0:T(8,128)(2,1)} %get-tuple-element.9), calls=%async_computation.1 | async-start | bytes 1048576 | tf_op jit(solution)/shard_map/all_to_all | solution.py:194

commit v9 on v8

--- a/solution.py
+++ b/solution.py
@@ -75,7 +75,7 @@
 
 def prep_kernel(key_ref, value_ref, filters_ref, index_ref, *out_refs):
     pieces = len(out_refs)
-    n_dev, _, piece_width, _ = out_refs[0].shape
+    n_local, _, piece_width, _ = out_refs[0].shape
     mixed = (key_ref[...].astype(jnp.float32) * value_ref[...].astype(jnp.float32)).astype(
         jnp.bfloat16
     )
@@ -88,18 +88,39 @@
     picked = jnp.dot(
         filters_ref[...].astype(jnp.float32), onehot_t, preferred_element_type=jnp.float32
     ).T
-    for dest in range(n_dev):
+    for dest in range(n_local):
         for piece in range(pieces):
             low = (dest * pieces + piece) * piece_width
             out_refs[piece][dest, 0] = mixed_t[low : low + piece_width].astype(jnp.bfloat16)
             out_refs[piece][dest, 1] = picked[low : low + piece_width].astype(jnp.bfloat16)
 
 
+def channel_block(channels, own_width):
+    for size in (512, 256, 128):
+        if channels % size == 0 and size % own_width == 0:
+            return size
+    return channels
+
+
 def prepare(key_in, value_in, filters, group_index, n_dev, pieces):
     row_count, channels = key_in.shape
-    piece_width = channels // (n_dev * pieces)
+    own_width = channels // n_dev
+    piece_width = own_width // pieces
+    block = channel_block(channels, own_width)
+    n_local = block // own_width
     return pl.pallas_call(
         prep_kernel,
+        grid=(channels // block,),
+        in_specs=[
+            pl.BlockSpec((row_count, block), lambda i: (0, i)),
+            pl.BlockSpec((row_count, block), lambda i: (0, i)),
+            pl.BlockSpec(filters.shape, lambda i: (0, 0)),
+            pl.BlockSpec((1, block), lambda i: (0, i)),
+        ],
+        out_specs=tuple(
+            pl.BlockSpec((n_local, 2, piece_width, row_count), lambda i: (i, 0, 0, 0))
+            for _ in range(pieces)
+        ),
         out_shape=tuple(
             jax.ShapeDtypeStruct((n_dev, 2, piece_width, row_count), jnp.bfloat16)
             for _ in range(pieces)
@@ -119,8 +140,20 @@
 
 
 def finish(returned, query, key_in, value_in, skip_gain):
+    row_count, channels = query.shape
+    block = channel_block(channels, 128)
+    row_spec = pl.BlockSpec((row_count, block), lambda i: (0, i))
     return pl.pallas_call(
         finish_kernel,
+        grid=(channels // block,),
+        in_specs=[
+            pl.BlockSpec((block, row_count), lambda i: (i, 0)),
+            row_spec,
+            row_spec,
+            row_spec,
+            pl.BlockSpec((1, block), lambda i: (0, i)),
+        ],
+        out_specs=row_spec,
         out_shape=jax.ShapeDtypeStruct(query.shape, jnp.bfloat16),
     )(returned, query, key_in, value_in, skip_gain.reshape(1, -1))
 

time: 76.4 us -> 78.7 us (1.030)
  Pallas kernels: 5.3 us -> 7.54 us
    pallas_call x2, Pallas kernels: 5.3 us -> 7.54 us  [the longest x1 3.85 us: prepare(): pl.pallas_call(prep_kernel, grid=(channels // block,), in_specs=[pl.Block...]
where the time goes in v9:
time: 78.7 us; the launch traced here: 78.3 us
  waiting for transfers between devices  20 us (25%)
  blocking collectives  18.5 us (24%)
  matrix products  16.2 us (21%)
  starting transfers between devices  10.4 us (13%)
  Pallas kernels  7.54 us (10%)
  other arithmetic  5.25 us (7%)
    all_to_all x2, waiting for transfers between devices, by_channels(): lax.all_to_all(sent[piece], ('outer', 'inner'), split_axis=0, concat_axis...  20 us
    all_to_all x1, blocking collectives, by_channels(): lax.all_to_all(jnp.stack(results, axis=1), ('outer', 'inner'), split_axis...  18.5 us
    dot_general x8, matrix products, contract(): jnp.einsum(pattern, left_op, right_op, precision=lax.Precision.HIGH, pref...  16.2 us
    all_to_all x2, starting transfers between devices, by_channels(): lax.all_to_all(sent[piece], ('outer', 'inner'), split_axis=0, concat_axis...  10.4 us
    pallas_call x1, Pallas kernels, prepare(): pl.pallas_call(prep_kernel, grid=(channels // block,), in_specs=[pl.Block...  3.85 us
    pallas_call x1, Pallas kernels, finish(): pl.pallas_call(finish_kernel, grid=(channels // block,), in_specs=[pl.Blo...  3.7 us
    add x2, other arithmetic, rotate(): real_part * cosine + imag_part * sine_part  1.91 us
  transfers between devices with their start and end apart: 2, of which 2 were waited for; matrix products, arithmetic and copies ran while one was open for 14% of the time, Pallas kernels for 0%

profile of v9, /device:TPU:0, one launch (start us, length us, event | category | flops | bytes accessed | tf_op | source)
XLA Modules:
  0.0 78.3 jit_solution(17354848701025941986)
XLA Ops:
  0.0 3.8 %shard_map.64 = (bf16[32,2,32,128]{3,2,1,0:T(8,128)(2,1)}, bf16[32,2,32,128]{3,2,1,0:T(8,128)(2,1)}) custom-call(bf16[128,2048]{1,0:T(8,128)(2,1)} %key_ref.3, bf16[128,2048]{1,0:T(8,128)(2,1)} %value_ref.3, bf16[128,128]{1,0:T(8,128)(2,1)} %filters_ref.1, s32[1,2048]{1,0:T(1,128)} %bitcast.28), custom_call_target="tpu_custom_call" | custom-call | tf_op jit(solution)/shard_map/pallas_call | solution.py:111
  3.8 7.3 %all-to-all-start = ((bf16[32,2,32,128]{3,2,1,0:T(8,128)(2,1)}), bf16[32,2,32,128]{3,2,1,0:T(8,128)(2,1)S(1)}, u32[]{:S(2)}, u32[]{:S(2)}) async-start(bf16[32,2,32,128]{3,2,1,0:T(8,128)(2,1)} %get-tuple-element.8), calls=%async_computation | async-start | bytes 1048576 | tf_op jit(solution)/shard_map/all_to_all | solution.py:227
  11.2 0.1 sine_negate_fusion
  11.2 0.1 sine_negate_fusion.1
  11.3 0.1 fusion.63
  11.5 0.3 fusion.53
  11.7 0.3 broadcast_multiply_fusion
  12.0 14.7 %all-to-all-done = bf16[32,2,32,128]{3,2,1,0:T(8,128)(2,1)S(1)} async-done(((bf16[32,2,32,128]{3,2,1,0:T(8,128)(2,1)}), bf16[32,2,32,128]{3,2,1,0:T(8,128)(2,1)S(1)}, u32[]{:S(2)}, u32[]{:S(2)}) %all-to-all-start) | async-done | bytes 524320 | tf_op jit(solution)/shard_map/all_to_all | solution.py:227
  26.7 3.1 %all-to-all-start.1 = ((bf16[32,2,32,128]{3,2,1,0:T(8,128)(2,1)}), bf16[32,2,32,128]{3,2,1,0:T(8,128)(2,1)S(1)}, u32[]{:S(2)}, u32[]{:S(2)}) async-start(bf16[32,2,32,128]{3,2,1,0:T(8,128)(2,1)} %get-tuple-element.9), calls=%async_computation.1 | async-start | bytes 1048576 | tf_op jit(solution)/shard_map/all_to_all | solution.py:227
  29.8 1.4 %fusion.33 = f32[128,64,128]{2,0,1:T(8,128)S(1)} fusion(bf16[32,64,128]{2,1,0:T(8,128)(2,1)S(1)} %bitcast.25, f32[64,32]{0,1:T(8,128)S(1)} %get-tuple-element.23, f32[64,32]{0,1:T(8,128)S(1)} %get-tuple-element.24), kind=kOutput, calls=%fused_computation.40 | convolution fusion | flops 201330688 | bytes 4734976 | tf_op jit(solution)/shard_map/kn,ncb->kcb/dot_general | solution.py:11
  31.2 1.0 %multiply_add_fusion.1 = (f32[64,64,128]{2,0,1:T(8,128)S(1)}, f32[64,64,128]{2,0,1:T(8,128)S(1)}) fusion(f32[128,64,128]{2,0,1:T(8,128)S(1)} %fusion.33, f32[64,128]{1,0:T(8,128)S(1)} %get-tuple-element.25, f32[64,128]{1,0:T(8,128)S(1)} %get-tuple-element.26), kind=kLoop, calls=%fused_computation.23 | loop fusion | flops 3145728 | bytes 8454144 | tf_op jit(solution)/shard_map/add | solution.py:38
  32.1 0.4 pad_maximum_fusion
  32.5 3.9 %fusion.2 = f32[64,64,256]{2,1,0:T(8,128)S(1)} fusion(f32[64,64,256]{2,0,1:T(8,128)S(1)} %pad_maximum_fusion, f32[128,128]{1,0:T(8,128)S(1)} %fusion.53, f32[128,128]{1,0:T(8,128)S(1)} %get-tuple-element.28, f32[128,128]{1,0:T(8,128)S(1)} %get-tuple-element.27), kind=kOutput, calls=%fused_computation.4 | convolution fusion | flops 1610809344 | bytes 8585216 | tf_op jit(solution)/shard_map/kcb,bq->kcq/dot_general | solution.py:11
  36.4 0.3 multiply_subtract_fusion.5
  36.8 1.0 %fusion.4 = f32[64,32,256]{2,1,0:T(8,128)S(1)} fusion(f32[64,32,128]{2,1,0:T(8,128)S(1)} %get-tuple-element.18, f32[64,32,128]{2,1,0:T(8,128)S(1)} %get-tuple-element.17, f32[128,128]{1,0:T(8,128)S(1)} %fusion.53, f32[128,128]{1,0:T(8,128)S(1)} %get-tuple-element.27, f32[128,128]{1,0:T(8,128)S(1)} %get-tuple-element.28), kind=kOutput, calls=%fused_computation.6 | convolution fusion | flops 806027264 | bytes 4390912 | tf_op jit(solution)/shard_map/kcq,qb->kcb/dot_general | solution.py:11
  37.8 0.3 multiply_subtract_fusion.4
  38.1 0.2 pad_maximum_fusion.2
  38.3 1.7 %fusion.25 = bf16[32,32,128]{2,0,1:T(8,128)(2,1)S(1)} fusion(f32[128,32,128]{2,1,0:T(8,128)S(1)} %pad_maximum_fusion.2, f32[32,64]{1,0:T(8,128)S(1)} %get-tuple-element.29, f32[32,64]{1,0:T(8,128)S(1)} %get-tuple-element.30), kind=kOutput, calls=%fused_computation.27 | convolution fusion | flops 100929536 | bytes 2375680 | tf_op jit(solution)/shard_map/nk,kcb->ncb/dot_general | solution.py:11
  40.0 5.3 %all-to-all-done.1 = bf16[32,2,32,128]{3,2,1,0:T(8,128)(2,1)S(1)} async-done(((bf16[32,2,32,128]{3,2,1,0:T(8,128)(2,1)}), bf16[32,2,32,128]{3,2,1,0:T(8,128)(2,1)S(1)}, u32[]{:S(2)}, u32[]{:S(2)}) %all-to-all-start.1) | async-done | bytes 524320 | tf_op jit(solution)/shard_map/all_to_all | solution.py:227
  45.3 1.4 %fusion.31 = f32[128,64,128]{2,0,1:T(8,128)S(1)} fusion(bf16[32,64,128]{2,1,0:T(8,128)(2,1)S(1)} %bitcast.24, f32[64,32]{0,1:T(8,128)S(1)} %get-tuple-element.23, f32[64,32]{0,1:T(8,128)S(1)} %get-tuple-element.24), kind=kOutput, calls=%fused_computation.38 | convolution fusion | flops 201330688 | bytes 4734976 | tf_op jit(solution)/shard_map/kn,ncb->kcb/dot_general | solution.py:11
  46.7 1.0 %multiply_add_fusion = (f32[64,64,128]{2,0,1:T(8,128)S(1)}, f32[64,64,128]{2,0,1:T(8,128)S(1)}) fusion(f32[128,64,128]{2,0,1:T(8,128)S(1)} %fusion.31, f32[64,128]{1,0:T(8,128)S(1)} %get-tuple-element.25, f32[64,128]{1,0:T(8,128)S(1)} %get-tuple-element.26), kind=kLoop, calls=%fused_computation.21 | loop fusion | flops 3145728 | bytes 8454144 | tf_op jit(solution)/shard_map/add | solution.py:38
  47.7 0.4 pad_maximum_fusion.1
  48.1 4.1 %fusion = f32[64,64,256]{2,1,0:T(8,128)S(1)} fusion(f32[64,64,256]{2,0,1:T(8,128)S(1)} %pad_maximum_fusion.1, f32[128,128]{1,0:T(8,128)S(1)} %fusion.53, f32[128,128]{1,0:T(8,128)S(1)} %get-tuple-element.28, f32[128,128]{1,0:T(8,128)S(1)} %get-tuple-element.27), kind=kOutput, calls=%fused_computation.2 | convolution fusion | flops 1610809344 | bytes 8585216 | tf_op jit(solution)/shard_map/kcb,bq->kcq/dot_general | solution.py:11
  52.2 0.3 multiply_subtract_fusion.3
  52.5 1.0 %fusion.8 = f32[64,32,256]{2,1,0:T(8,128)S(1)} fusion(f32[64,32,128]{2,1,0:T(8,128)S(1)} %get-tuple-element.16, f32[64,32,128]{2,1,0:T(8,128)S(1)} %get-tuple-element.15, f32[128,128]{1,0:T(8,128)S(1)} %fusion.53, f32[128,128]{1,0:T(8,128)S(1)} %get-tuple-element.27, f32[128,128]{1,0:T(8,128)S(1)} %get-tuple-element.28), kind=kOutput, calls=%fused_computation.11 | convolution fusion | flops 806027264 | bytes 4390912 | tf_op jit(solution)/shard_map/kcq,qb->kcb/dot_general | solution.py:11
  53.5 0.3 multiply_subtract_fusion.2
  53.9 0.2 pad_maximum_fusion.3
  54.1 1.7 %fusion.28 = bf16[32,1,32,128]{3,0,2,1:T(8,128)(2,1)S(1)} fusion(f32[128,32,128]{2,1,0:T(8,128)S(1)} %pad_maximum_fusion.3, f32[32,64]{1,0:T(8,128)S(1)} %get-tuple-element.29, f32[32,64]{1,0:T(8,128)S(1)} %get-tuple-element.30), kind=kOutput, calls=%fused_computation.28 | convolution fusion | flops 100929536 | bytes 2375680 | tf_op jit(solution)/shard_map/nk,kcb->ncb/dot_general | solution.py:11
  55.8 0.1 pad_maximum_fusion.4
  55.9 0.2 copy.20
  56.1 18.5 %all_to_all.15 = bf16[32,2,32,128]{3,2,1,0:T(8,128)(2,1)} all-to-all(bf16[32,2,32,128]{3,2,1,0:T(8,128)(2,1)S(1)} %copy.20), channel_id=1, replica_groups=mesh['outer'=8,'inner'=4] {'outer','inner'}, dimensions={0} | all-to-all | bytes 1048576 | tf_op jit(solution)/shard_map/all_to_all | solution.py:238
  74.6 3.7 %shard_map.65 = bf16[128,2048]{1,0:T(8,128)(2,1)} custom-call(bf16[2048,128]{1,0:T(8,128)(2,1)} %bitcast.26, bf16[128,2048]{1,0:T(8,128)(2,1)} %query_ref.1, bf16[128,2048]{1,0:T(8,128)(2,1)} %key_ref.3, bf16[128,2048]{1,0:T(8,128)(2,1)} %value_ref.3, f32[1,2048]{1,0:T(1,128)} %bitcast.29), custom_call_target="tpu_custom_call" | custom-call | tf_op jit(solution)/shard_map/pallas_call | solution.py:146
Async XLA Ops:
  3.8 22.9 %all-to-all-start = ((bf16[32,2,32,128]{3,2,1,0:T(8,128)(2,1)}), bf16[32,2,32,128]{3,2,1,0:T(8,128)(2,1)S(1)}, u32[]{:S(2)}, u32[]{:S(2)}) async-start(bf16[32,2,32,128]{3,2,1,0:T(8,128)(2,1)} %get-tuple-element.8), calls=%async_computation | async-start | bytes 1048576 | tf_op jit(solution)/shard_map/all_to_all | solution.py:227
  26.7 18.6 %all-to-all-start.1 = ((bf16[32,2,32,128]{3,2,1,0:T(8,128)(2,1)}), bf16[32,2,32,128]{3,2,1,0:T(8,128)(2,1)S(1)}, u32[]{:S(2)}, u32[]{:S(2)}) async-start(bf16[32,2,32,128]{3,2,1,0:T(8,128)(2,1)} %get-tuple-element.9), calls=%async_computation.1 | async-start | bytes 1048576 | tf_op jit(solution)/shard_map/all_to_all | solution.py:227

commit v10 on v8

--- a/solution.py
+++ b/solution.py
@@ -180,7 +180,7 @@
     row_count = mixed.shape[0]
     channels = mixed.shape[1]
     own_width = channels // n_dev
-    pieces = 2 if own_width % 16 == 0 else 1
+    pieces = 4 if own_width % 64 == 0 else (2 if own_width % 16 == 0 else 1)
     piece_width = own_width // pieces
     if piece_width % 16 == 0:
         sent = prepare(key_in, value_in, filters, group_index, n_dev, pieces)
@@ -210,8 +210,11 @@
 
 def on_device(query, key_in, value_in, filters, group_index, skip_gain):
     mixed = (key_in.astype(jnp.float32) * value_in.astype(jnp.float32)).astype(jnp.bfloat16)
-    returned = by_channels(mixed, key_in, value_in, filters, group_index)
-    return finish(returned, query, key_in, value_in, skip_gain)
+    convolved = by_channels(mixed, key_in, value_in, filters, group_index).T.astype(jnp.float32)
+    mixed_wide = mixed.astype(jnp.float32)
+    return (query.astype(jnp.float32) * (convolved + skip_gain[None, :] * mixed_wide)).astype(
+        jnp.bfloat16
+    )
 
 
 def solution(mesh):

time: 76.4 us -> 86.6 us (1.13)
  waiting for transfers between devices: 20 us -> 40.8 us
  blocking collectives: 18.5 us -> 0 us
  starting transfers between devices: 10.4 us -> 18 us
  Pallas kernels: 5.3 us -> 2.64 us
  local copies, waits for them, and re-layouts: 0.21 us -> 2.84 us
    all_to_all x1 -> x0, blocking collectives: 18.5 us -> none  [by_channels(): lax.all_to_all(jnp.stack(results, axis=1), ('outer', 'inner'), split_axis...]
    all_to_all x0 -> x1, waiting for transfers between devices: none -> 14.7 us  [by_channels(): lax.all_to_all(jnp.stack(results, axis=1), ('outer', 'inner'), split_axis...]
    all_to_all x2 -> x4, waiting for transfers between devices: 20 us -> 26.1 us  [by_channels(): lax.all_to_all(sent[piece], ('outer', 'inner'), split_axis=0, concat_axis...]
    all_to_all x2 -> x4, starting transfers between devices: 10.4 us -> 15.2 us  [by_channels(): lax.all_to_all(sent[piece], ('outer', 'inner'), split_axis=0, concat_axis...]
    all_to_all x0 -> x1, starting transfers between devices: none -> 2.74 us  [by_channels(): lax.all_to_all(jnp.stack(results, axis=1), ('outer', 'inner'), split_axis...]
    pallas_call x1 -> x0, Pallas kernels: 2.67 us -> none  [finish(): pl.pallas_call(finish_kernel, out_shape=jax.ShapeDtypeStruct(query.shape,...]
    convert_element_type x0 -> x1, local copies, waits for them, and re-layouts: none -> 1.01 us  [on_device(): (query.astype(jnp.float32) * (convolved + skip_gain[None, :] * mixed_wide...]
    add x2 -> x4, other arithmetic: 1.91 us -> 1.69 us  [rotate(): real_part * cosine + imag_part * sine_part]
  transfers between devices with their start and end apart: 2 -> 5, of which waited for: 2 -> 5; matrix products, arithmetic and copies ran while one was open for 14% -> 19% of each run, Pallas kernels for 0% -> 0%
where the time goes in v10:
time: 86.6 us; the launch traced here: 86.1 us
  waiting for transfers between devices  40.8 us (47%)
  starting transfers between devices  18 us (21%)
  matrix products  16.2 us (19%)
  other arithmetic  5.15 us (6%)
  local copies, waits for them, and re-layouts  2.84 us (3%)
  Pallas kernels  2.64 us (3%)
    all_to_all x4, waiting for transfers between devices, by_channels(): lax.all_to_all(sent[piece], ('outer', 'inner'), split_axis=0, concat_axis...  26.1 us
    dot_general x16, matrix products, contract(): jnp.einsum(pattern, left_op, right_op, precision=lax.Precision.HIGH, pref...  16.2 us
    all_to_all x4, starting transfers between devices, by_channels(): lax.all_to_all(sent[piece], ('outer', 'inner'), split_axis=0, concat_axis...  15.2 us
    all_to_all x1, waiting for transfers between devices, by_channels(): lax.all_to_all(jnp.stack(results, axis=1), ('outer', 'inner'), split_axis...  14.7 us
    all_to_all x1, starting transfers between devices, by_channels(): lax.all_to_all(jnp.stack(results, axis=1), ('outer', 'inner'), split_axis...  2.74 us
    pallas_call x1, Pallas kernels, prepare(): pl.pallas_call(prep_kernel, out_shape=tuple((jax.ShapeDtypeStruct((n_dev,...  2.64 us
  transfers between devices with their start and end apart: 5, of which 5 were waited for; matrix products, arithmetic and copies ran while one was open for 19% of the time, Pallas kernels for 0%

profile of v10, /device:TPU:0, one launch (start us, length us, event | category | flops | bytes accessed | tf_op | source)
XLA Modules:
  0.0 86.1 jit_solution(15691597685229132021)
XLA Ops:
  0.0 2.6 %shard_map.64 = (bf16[32,2,16,128]{3,2,1,0:T(8,128)(2,1)}, bf16[32,2,16,128]{3,2,1,0:T(8,128)(2,1)}, bf16[32,2,16,128]{3,2,1,0:T(8,128)(2,1)}, bf16[32,2,16,128]{3,2,1,0:T(8,128)(2,1)}) custom-call(bf16[128,2048]{1,0:T(8,128)(2,1)} %key_ref.1, bf16[128,2048]{1,0:T(8,128)(2,1)} %value_ref.1, bf16[128,128]{1,0:T(8,128)(2,1)} %filters_ref.1, s32[1,2048]{1,0:T(1,128)} %bitcast.52), custom_call_target="tpu_custom_call" | custom-call | tf_op jit(solution)/shard_map/pallas_call | solution.py:101
  2.6 7.3 %all-to-all-start = ((bf16[32,2,16,128]{3,2,1,0:T(8,128)(2,1)}), bf16[32,2,16,128]{3,2,1,0:T(8,128)(2,1)S(1)}, u32[]{:S(2)}, u32[]{:S(2)}) async-start(bf16[32,2,16,128]{3,2,1,0:T(8,128)(2,1)} %get-tuple-element.12), calls=%async_computation | async-start | bytes 524288 | tf_op jit(solution)/shard_map/all_to_all | solution.py:194
  10.3 0.1 fusion.76
  10.4 0.3 fusion.66
  10.7 0.3 broadcast_multiply_fusion
  11.0 9.6 %all-to-all-done = bf16[32,2,16,128]{3,2,1,0:T(8,128)(2,1)S(1)} async-done(((bf16[32,2,16,128]{3,2,1,0:T(8,128)(2,1)}), bf16[32,2,16,128]{3,2,1,0:T(8,128)(2,1)S(1)}, u32[]{:S(2)}, u32[]{:S(2)}) %all-to-all-start) | async-done | bytes 262176 | tf_op jit(solution)/shard_map/all_to_all | solution.py:194
  20.5 2.6 %all-to-all-start.1 = ((bf16[32,2,16,128]{3,2,1,0:T(8,128)(2,1)}), bf16[32,2,16,128]{3,2,1,0:T(8,128)(2,1)S(1)}, u32[]{:S(2)}, u32[]{:S(2)}) async-start(bf16[32,2,16,128]{3,2,1,0:T(8,128)(2,1)} %get-tuple-element.13), calls=%async_computation.1 | async-start | bytes 524288 | tf_op jit(solution)/shard_map/all_to_all | solution.py:194
  23.1 0.7 fusion.46
  23.9 0.4 multiply_add_fusion.3
  24.3 0.2 pad_maximum_fusion
  24.5 2.0 %fusion.6 = f32[64,32,256]{2,1,0:T(8,128)S(1)} fusion(f32[64,32,256]{2,0,1:T(8,128)S(1)} %pad_maximum_fusion, f32[128,128]{1,0:T(8,128)S(1)} %fusion.66, f32[128,128]{1,0:T(8,128)S(1)} %get-tuple-element.50, f32[128,128]{1,0:T(8,128)S(1)} %get-tuple-element.49), kind=kOutput, calls=%fused_computation.10 | convolution fusion | flops 805502976 | bytes 4390912 | tf_op jit(solution)/shard_map/kcb,bq->kcq/dot_general | solution.py:11
  26.6 0.1 multiply_subtract_fusion.11
  26.7 0.6 fusion.13
  27.5 0.7 fusion.8
  28.2 5.6 %all-to-all-done.1 = bf16[32,2,16,128]{3,2,1,0:T(8,128)(2,1)S(1)} async-done(((bf16[32,2,16,128]{3,2,1,0:T(8,128)(2,1)}), bf16[32,2,16,128]{3,2,1,0:T(8,128)(2,1)S(1)}, u32[]{:S(2)}, u32[]{:S(2)}) %all-to-all-start.1) | async-done | bytes 262176 | tf_op jit(solution)/shard_map/all_to_all | solution.py:194
  33.7 2.6 %all-to-all-start.2 = ((bf16[32,2,16,128]{3,2,1,0:T(8,128)(2,1)}), bf16[32,2,16,128]{3,2,1,0:T(8,128)(2,1)S(1)}, u32[]{:S(2)}, u32[]{:S(2)}) async-start(bf16[32,2,16,128]{3,2,1,0:T(8,128)(2,1)} %get-tuple-element.15), calls=%async_computation.2 | async-start | bytes 524288 | tf_op jit(solution)/shard_map/all_to_all | solution.py:194
  36.3 0.7 fusion.44
  37.1 0.4 multiply_add_fusion.2
  37.5 0.2 pad_maximum_fusion.1
  37.7 2.0 %fusion.4 = f32[64,32,256]{2,1,0:T(8,128)S(1)} fusion(f32[64,32,256]{2,0,1:T(8,128)S(1)} %pad_maximum_fusion.1, f32[128,128]{1,0:T(8,128)S(1)} %fusion.66, f32[128,128]{1,0:T(8,128)S(1)} %get-tuple-element.50, f32[128,128]{1,0:T(8,128)S(1)} %get-tuple-element.49), kind=kOutput, calls=%fused_computation.8 | convolution fusion | flops 805502976 | bytes 4390912 | tf_op jit(solution)/shard_map/kcb,bq->kcq/dot_general | solution.py:11
  39.7 0.1 multiply_subtract_fusion.9
  39.9 0.6 fusion.17
  40.7 0.7 fusion.9
  41.4 5.6 %all-to-all-done.2 = bf16[32,2,16,128]{3,2,1,0:T(8,128)(2,1)S(1)} async-done(((bf16[32,2,16,128]{3,2,1,0:T(8,128)(2,1)}), bf16[32,2,16,128]{3,2,1,0:T(8,128)(2,1)S(1)}, u32[]{:S(2)}, u32[]{:S(2)}) %all-to-all-start.2) | async-done | bytes 262176 | tf_op jit(solution)/shard_map/all_to_all | solution.py:194
  46.9 2.8 %all-to-all-start.3 = ((bf16[32,2,16,128]{3,2,1,0:T(8,128)(2,1)}), bf16[32,2,16,128]{3,2,1,0:T(8,128)(2,1)S(1)}, u32[]{:S(2)}, u32[]{:S(2)}) async-start(bf16[32,2,16,128]{3,2,1,0:T(8,128)(2,1)} %get-tuple-element.17), calls=%async_computation.3 | async-start | bytes 524288 | tf_op jit(solution)/shard_map/all_to_all | solution.py:194
  49.7 0.8 fusion.42
  50.5 0.4 multiply_add_fusion.1
  50.9 0.2 pad_maximum_fusion.2
  51.1 2.0 %fusion.2 = f32[64,32,256]{2,1,0:T(8,128)S(1)} fusion(f32[64,32,256]{2,0,1:T(8,128)S(1)} %pad_maximum_fusion.2, f32[128,128]{1,0:T(8,128)S(1)} %fusion.66, f32[128,128]{1,0:T(8,128)S(1)} %get-tuple-element.50, f32[128,128]{1,0:T(8,128)S(1)} %get-tuple-element.49), kind=kOutput, calls=%fused_computation.6 | convolution fusion | flops 805502976 | bytes 4390912 | tf_op jit(solution)/shard_map/kcb,bq->kcq/dot_general | solution.py:11
  53.1 0.1 multiply_subtract_fusion.7
  53.3 0.6 fusion.21
  54.0 0.7 fusion.10
  54.7 5.4 %all-to-all-done.3 = bf16[32,2,16,128]{3,2,1,0:T(8,128)(2,1)S(1)} async-done(((bf16[32,2,16,128]{3,2,1,0:T(8,128)(2,1)}), bf16[32,2,16,128]{3,2,1,0:T(8,128)(2,1)S(1)}, u32[]{:S(2)}, u32[]{:S(2)}) %all-to-all-start.3) | async-done | bytes 262176 | tf_op jit(solution)/shard_map/all_to_all | solution.py:194
  60.1 0.7 fusion.40
  60.9 0.4 multiply_add_fusion
  61.3 0.2 pad_maximum_fusion.3
  61.5 2.0 %fusion = f32[64,32,256]{2,1,0:T(8,128)S(1)} fusion(f32[64,32,256]{2,0,1:T(8,128)S(1)} %pad_maximum_fusion.3, f32[128,128]{1,0:T(8,128)S(1)} %fusion.66, f32[128,128]{1,0:T(8,128)S(1)} %get-tuple-element.50, f32[128,128]{1,0:T(8,128)S(1)} %get-tuple-element.49), kind=kOutput, calls=%fused_computation.4 | convolution fusion | flops 805502976 | bytes 4390912 | tf_op jit(solution)/shard_map/kcb,bq->kcq/dot_general | solution.py:11
  63.5 0.1 multiply_subtract_fusion.5
  63.7 0.6 fusion.25
  64.5 0.7 fusion.12
  65.3 1.0 %copy.49 = bf16[32,4,16,128]{3,2,1,0:T(8,128)(2,1)} copy(bf16[32,4,16,128]{3,0,2,1:T(8,128)(2,1)S(1)} %pad_maximum_fusion.8) | data formatting | bytes 1048576 | tf_op jit(solution)/shard_map/stack | solution.py:206
  66.3 2.7 %all-to-all-start.4 = ((bf16[32,4,16,128]{3,2,1,0:T(8,128)(2,1)}), bf16[32,4,16,128]{3,2,1,0:T(8,128)(2,1)S(1)}, u32[]{:S(2)}, u32[]{:S(2)}) async-start(bf16[32,4,16,128]{3,2,1,0:T(8,128)(2,1)} %copy.49), calls=%async_computation.4 | async-start | bytes 1048576 | tf_op jit(solution)/shard_map/all_to_all | solution.py:205
  69.0 0.3 copy.50
  69.3 0.3 copy.51
  69.6 0.3 copy.36
  69.9 14.7 %all-to-all-done.4 = bf16[32,4,16,128]{3,2,1,0:T(8,128)(2,1)S(1)} async-done(((bf16[32,4,16,128]{3,2,1,0:T(8,128)(2,1)}), bf16[32,4,16,128]{3,2,1,0:T(8,128)(2,1)S(1)}, u32[]{:S(2)}, u32[]{:S(2)}) %all-to-all-start.4) | async-done | bytes 524320 | tf_op jit(solution)/shard_map/all_to_all | solution.py:205
  84.6 0.5 fusion.31
  85.0 1.0 %copy.52 = bf16[128,2048]{1,0:T(8,128)(2,1)} copy(bf16[128,2048]{0,1:T(8,128)(2,1)S(1)} %fusion.31) | data formatting | bytes 1048576 | tf_op jit(solution)/shard_map/convert_element_type | solution.py:215
  (21 shorter events, 1.2 us)
Async XLA Ops:
  2.6 17.9 %all-to-all-start = ((bf16[32,2,16,128]{3,2,1,0:T(8,128)(2,1)}), bf16[32,2,16,128]{3,2,1,0:T(8,128)(2,1)S(1)}, u32[]{:S(2)}, u32[]{:S(2)}) async-start(bf16[32,2,16,128]{3,2,1,0:T(8,128)(2,1)} %get-tuple-element.12), calls=%async_computation | async-start | bytes 524288 | tf_op jit(solution)/shard_map/all_to_all | solution.py:194
  20.5 13.2 %all-to-all-start.1 = ((bf16[32,2,16,128]{3,2,1,0:T(8,128)(2,1)}), bf16[32,2,16,128]{3,2,1,0:T(8,128)(2,1)S(1)}, u32[]{:S(2)}, u32[]{:S(2)}) async-start(bf16[32,2,16,128]{3,2,1,0:T(8,128)(2,1)} %get-tuple-element.13), calls=%async_computation.1 | async-start | bytes 524288 | tf_op jit(solution)/shard_map/all_to_all | solution.py:194
  33.7 13.2 %all-to-all-start.2 = ((bf16[32,2,16,128]{3,2,1,0:T(8,128)(2,1)}), bf16[32,2,16,128]{3,2,1,0:T(8,128)(2,1)S(1)}, u32[]{:S(2)}, u32[]{:S(2)}) async-start(bf16[32,2,16,128]{3,2,1,0:T(8,128)(2,1)} %get-tuple-element.15), calls=%async_computation.2 | async-start | bytes 524288 | tf_op jit(solution)/shard_map/all_to_all | solution.py:194
  46.9 13.2 %all-to-all-start.3 = ((bf16[32,2,16,128]{3,2,1,0:T(8,128)(2,1)}), bf16[32,2,16,128]{3,2,1,0:T(8,128)(2,1)S(1)}, u32[]{:S(2)}, u32[]{:S(2)}) async-start(bf16[32,2,16,128]{3,2,1,0:T(8,128)(2,1)} %get-tuple-element.17), calls=%async_computation.3 | async-start | bytes 524288 | tf_op jit(solution)/shard_map/all_to_all | solution.py:194
  64.5 4.5 %copy-start = (bf16[128,2048]{1,0:T(8,128)(2,1)S(1)}, bf16[128,2048]{1,0:T(8,128)(2,1)}, u32[]{:S(2)}) copy-start(bf16[128,2048]{1,0:T(8,128)(2,1)} %key_ref.1) | copy-start | bytes 1572868
  65.2 4.1 %copy-start.1 = (bf16[128,2048]{1,0:T(8,128)(2,1)S(1)}, bf16[128,2048]{1,0:T(8,128)(2,1)}, u32[]{:S(2)}) copy-start(bf16[128,2048]{1,0:T(8,128)(2,1)} %value_ref.1) | copy-start | bytes 1572868
  65.3 4.3 %copy-start.2 = (bf16[128,2048]{1,0:T(8,128)(2,1)S(1)}, bf16[128,2048]{1,0:T(8,128)(2,1)}, u32[]{:S(2)}) copy-start(bf16[128,2048]{1,0:T(8,128)(2,1)} %param.6) | copy-start | bytes 1572868
  66.3 18.3 %copy-start.3 = (f32[2048]{0:T(1024)S(1)}, f32[2048]{0:T(1024)}, u32[]{:S(2)}) copy-start(f32[2048]{0:T(1024)} %param.11) | copy-start | bytes 24580
  66.3 18.3 %all-to-all-start.4 = ((bf16[32,4,16,128]{3,2,1,0:T(8,128)(2,1)}), bf16[32,4,16,128]{3,2,1,0:T(8,128)(2,1)S(1)}, u32[]{:S(2)}, u32[]{:S(2)}) async-start(bf16[32,4,16,128]{3,2,1,0:T(8,128)(2,1)} %copy.49), calls=%async_computation.4 | async-start | bytes 1048576 | tf_op jit(solution)/shard_map/all_to_all | solution.py:205

commit v11 on v10

--- a/solution.py
+++ b/solution.py
@@ -138,16 +138,17 @@
 def convolve_block(got, n_dev, row_count):
     own_width = got.shape[2]
     size_a = 2 * n_dev
+    kept = n_dev + 1
     padded = size_a * row_count
     stacked = got.reshape(n_dev, 2 * own_width, row_count).astype(jnp.float32)
-    first_cos, first_sin = dft_table(size_a, n_dev, size_a)
+    first_cos, first_sin = dft_table(kept, n_dev, size_a)
     first = contract("kn,ncb->kcb", jnp.concatenate([first_cos, -first_sin], axis=0), stacked)
     twiddle = angles_of(
-        jnp.arange(size_a, dtype=jnp.int32)[:, None]
+        jnp.arange(kept, dtype=jnp.int32)[:, None]
         * jnp.arange(row_count, dtype=jnp.int32)[None, :],
         padded,
     )[:, None, :]
-    real_part, imag_part = rotate(first[:size_a], first[size_a:], twiddle, -1)
+    real_part, imag_part = rotate(first[:kept], first[kept:], twiddle, -1)
     second_cos, second_sin = dft_table(row_count, row_count, row_count)
     prod = contract(
         "kcb,bq->kcq",
@@ -166,10 +167,12 @@
         complex_table(second_cos, second_sin, 1),
     )
     real_part, imag_part = rotate(prod[:, :, :row_count], prod[:, :, row_count:], twiddle, 1)
-    back_cos, back_sin = dft_table(n_dev, size_a, size_a)
+    back_cos, back_sin = dft_table(n_dev, kept, size_a)
+    index = jnp.arange(kept)
+    weight = jnp.where((index == 0) | (index == n_dev), 1.0, 2.0).astype(jnp.float32)[None, :]
     outcome = contract(
         "nk,kcb->ncb",
-        jnp.concatenate([back_cos, -back_sin], axis=1),
+        jnp.concatenate([back_cos * weight, -back_sin * weight], axis=1),
         jnp.concatenate([real_part, imag_part], axis=0),
     )
     return (outcome * (1.0 / padded)).astype(jnp.bfloat16)
@@ -180,7 +183,7 @@
     row_count = mixed.shape[0]
     channels = mixed.shape[1]
     own_width = channels // n_dev
-    pieces = 4 if own_width % 64 == 0 else (2 if own_width % 16 == 0 else 1)
+    pieces = 2 if own_width % 16 == 0 else 1
     piece_width = own_width // pieces
     if piece_width % 16 == 0:
         sent = prepare(key_in, value_in, filters, group_index, n_dev, pieces)

time: 86.6 us -> 70.8 us (0.82)
  matrix products: 16.2 us -> 8.08 us
  starting transfers between devices: 18 us -> 13.4 us
  other arithmetic: 5.15 us -> 3.2 us
  waiting for transfers between devices: 40.8 us -> 39.4 us
    dot_general x16 -> x8, matrix products: 16.2 us -> 8.08 us  [contract(): jnp.einsum(pattern, left_op, right_op, precision=lax.Precision.HIGH, pref...]
    all_to_all x4 -> x2, starting transfers between devices: 15.2 us -> 10.4 us  [by_channels(): lax.all_to_all(sent[piece], ('outer', 'inner'), split_axis=0, concat_axis...]
    add x4 -> x2, other arithmetic: 1.69 us -> 0.73 us  [rotate(): real_part * cosine + imag_part * sine_part]
    all_to_all x4 -> x2, waiting for transfers between devices: 26.1 us -> 25.2 us  [by_channels(): lax.all_to_all(sent[piece], ('outer', 'inner'), split_axis=0, concat_axis...]
  transfers between devices with their start and end apart: 5 -> 3, of which waited for: 5 -> 3; matrix products, arithmetic and copies ran while one was open for 19% -> 9% of each run, Pallas kernels for 0% -> 0%
where the time goes in v11:
time: 70.8 us; the launch traced here: 70.3 us
  waiting for transfers between devices  39.4 us (56%)
  starting transfers between devices  13.4 us (19%)
  matrix products  8.08 us (11%)
  local copies, waits for them, and re-layouts  3.29 us (5%)
  other arithmetic  3.2 us (5%)
  Pallas kernels  2.63 us (4%)
    all_to_all x2, waiting for transfers between devices, by_channels(): lax.all_to_all(sent[piece], ('outer', 'inner'), split_axis=0, concat_axis...  25.2 us
    all_to_all x1, waiting for transfers between devices, by_channels(): lax.all_to_all(jnp.stack(results, axis=1), ('outer', 'inner'), split_axis...  14.2 us
    all_to_all x2, starting transfers between devices, by_channels(): lax.all_to_all(sent[piece], ('outer', 'inner'), split_axis=0, concat_axis...  10.4 us
    dot_general x8, matrix products, contract(): jnp.einsum(pattern, left_op, right_op, precision=lax.Precision.HIGH, pref...  8.08 us
    all_to_all x1, starting transfers between devices, by_channels(): lax.all_to_all(jnp.stack(results, axis=1), ('outer', 'inner'), split_axis...  3.08 us
    pallas_call x1, Pallas kernels, prepare(): pl.pallas_call(prep_kernel, out_shape=tuple((jax.ShapeDtypeStruct((n_dev,...  2.63 us
  transfers between devices with their start and end apart: 3, of which 3 were waited for; matrix products, arithmetic and copies ran while one was open for 9% of the time, Pallas kernels for 0%

profile of v11, /device:TPU:0, one launch (start us, length us, event | category | flops | bytes accessed | tf_op | source)
XLA Modules:
  0.0 70.3 jit_solution(11395444326541670010)
XLA Ops:
  0.0 2.6 %shard_map.64 = (bf16[32,2,32,128]{3,2,1,0:T(8,128)(2,1)}, bf16[32,2,32,128]{3,2,1,0:T(8,128)(2,1)}) custom-call(bf16[128,2048]{1,0:T(8,128)(2,1)} %key_ref.1, bf16[128,2048]{1,0:T(8,128)(2,1)} %value_ref.1, bf16[128,128]{1,0:T(8,128)(2,1)} %filters_ref.1, s32[1,2048]{1,0:T(1,128)} %bitcast.36), custom_call_target="tpu_custom_call" | custom-call | tf_op jit(solution)/shard_map/pallas_call | solution.py:101
  2.6 7.3 %all-to-all-start = ((bf16[32,2,32,128]{3,2,1,0:T(8,128)(2,1)}), bf16[32,2,32,128]{3,2,1,0:T(8,128)(2,1)S(1)}, u32[]{:S(2)}, u32[]{:S(2)}) async-start(bf16[32,2,32,128]{3,2,1,0:T(8,128)(2,1)} %get-tuple-element.8), calls=%async_computation | async-start | bytes 1048576 | tf_op jit(solution)/shard_map/all_to_all | solution.py:197
  9.9 0.1 sine_negate_fusion
  10.0 0.1 fusion.60
  10.1 0.3 fusion.41
  10.4 0.3 broadcast_multiply_fusion
  10.7 0.1 cosine_multiply_fusion
  10.8 14.7 %all-to-all-done = bf16[32,2,32,128]{3,2,1,0:T(8,128)(2,1)S(1)} async-done(((bf16[32,2,32,128]{3,2,1,0:T(8,128)(2,1)}), bf16[32,2,32,128]{3,2,1,0:T(8,128)(2,1)S(1)}, u32[]{:S(2)}, u32[]{:S(2)}) %all-to-all-start) | async-done | bytes 524320 | tf_op jit(solution)/shard_map/all_to_all | solution.py:197
  25.5 3.1 %all-to-all-start.1 = ((bf16[32,2,32,128]{3,2,1,0:T(8,128)(2,1)}), bf16[32,2,32,128]{3,2,1,0:T(8,128)(2,1)S(1)}, u32[]{:S(2)}, u32[]{:S(2)}) async-start(bf16[32,2,32,128]{3,2,1,0:T(8,128)(2,1)} %get-tuple-element.9), calls=%async_computation.1 | async-start | bytes 1048576 | tf_op jit(solution)/shard_map/all_to_all | solution.py:197
  28.6 0.9 %fusion.24 = f32[66,64,128]{2,0,1:T(8,128)S(1)} fusion(bf16[32,64,128]{2,1,0:T(8,128)(2,1)S(1)} %bitcast.34, f32[33,32]{0,1:T(8,128)S(1)} %get-tuple-element.25, f32[33,32]{0,1:T(8,128)S(1)} %get-tuple-element.26), kind=kOutput, calls=%fused_computation.43 | convolution fusion | flops 103811136 | bytes 2695424 | tf_op jit(solution)/shard_map/kn,ncb->kcb/dot_general | solution.py:11
  29.5 0.4 multiply_add_fusion.1
  29.9 0.2 pad_maximum_fusion
  30.0 1.5 %fusion.2 = f32[33,64,256]{2,1,0:T(8,128)S(1)} fusion(f32[33,64,256]{2,0,1:T(8,128)S(1)} %pad_maximum_fusion, f32[128,128]{1,0:T(8,128)S(1)} %fusion.41, f32[128,128]{1,0:T(8,128)S(1)} %get-tuple-element.30, f32[128,128]{1,0:T(8,128)S(1)} %get-tuple-element.29), kind=kOutput, calls=%fused_computation.4 | convolution fusion | flops 830668800 | bytes 4521984 | tf_op jit(solution)/shard_map/kcb,bq->kcq/dot_general | solution.py:11
  31.6 0.2 multiply_subtract_fusion.5
  31.7 0.6 fusion.11
  32.3 0.2 multiply_subtract_fusion.4
  32.5 0.1 pad_maximum_fusion.2
  32.6 1.0 %fusion.4 = bf16[32,32,128]{2,0,1:T(8,128)(2,1)S(1)} fusion(f32[66,32,128]{2,1,0:T(8,128)S(1)} %pad_maximum_fusion.2, f32[32,33]{1,0:T(8,128)S(1)} %get-tuple-element.24, f32[32,33]{1,0:T(8,128)S(1)} %get-tuple-element.23), kind=kOutput, calls=%fused_computation.12 | convolution fusion | flops 52168768 | bytes 1351936 | tf_op jit(solution)/shard_map/nk,kcb->ncb/dot_general | solution.py:11
  33.6 10.5 %all-to-all-done.1 = bf16[32,2,32,128]{3,2,1,0:T(8,128)(2,1)S(1)} async-done(((bf16[32,2,32,128]{3,2,1,0:T(8,128)(2,1)}), bf16[32,2,32,128]{3,2,1,0:T(8,128)(2,1)S(1)}, u32[]{:S(2)}, u32[]{:S(2)}) %all-to-all-start.1) | async-done | bytes 524320 | tf_op jit(solution)/shard_map/all_to_all | solution.py:197
  44.1 0.9 %fusion.22 = f32[66,64,128]{2,0,1:T(8,128)S(1)} fusion(bf16[32,64,128]{2,1,0:T(8,128)(2,1)S(1)} %bitcast.33, f32[33,32]{0,1:T(8,128)S(1)} %get-tuple-element.25, f32[33,32]{0,1:T(8,128)S(1)} %get-tuple-element.26), kind=kOutput, calls=%fused_computation.41 | convolution fusion | flops 103811136 | bytes 2695424 | tf_op jit(solution)/shard_map/kn,ncb->kcb/dot_general | solution.py:11
  45.0 0.4 multiply_add_fusion
  45.4 0.2 pad_maximum_fusion.1
  45.6 1.5 %fusion = f32[33,64,256]{2,1,0:T(8,128)S(1)} fusion(f32[33,64,256]{2,0,1:T(8,128)S(1)} %pad_maximum_fusion.1, f32[128,128]{1,0:T(8,128)S(1)} %fusion.41, f32[128,128]{1,0:T(8,128)S(1)} %get-tuple-element.30, f32[128,128]{1,0:T(8,128)S(1)} %get-tuple-element.29), kind=kOutput, calls=%fused_computation.2 | convolution fusion | flops 830668800 | bytes 4521984 | tf_op jit(solution)/shard_map/kcb,bq->kcq/dot_general | solution.py:11
  47.1 0.2 multiply_subtract_fusion.3
  47.3 0.6 fusion.15
  47.9 0.2 multiply_subtract_fusion.2
  48.1 0.1 pad_maximum_fusion.3
  48.1 1.0 %fusion.8 = bf16[32,1,32,128]{3,0,2,1:T(8,128)(2,1)S(1)} fusion(f32[66,32,128]{2,1,0:T(8,128)S(1)} %pad_maximum_fusion.3, f32[32,33]{1,0:T(8,128)S(1)} %get-tuple-element.24, f32[32,33]{1,0:T(8,128)S(1)} %get-tuple-element.23), kind=kOutput, calls=%fused_computation.16 | convolution fusion | flops 52168768 | bytes 1351936 | tf_op jit(solution)/shard_map/nk,kcb->ncb/dot_general | solution.py:11
  49.1 0.1 pad_maximum_fusion.4
  49.2 0.0 copy-start
  49.2 1.0 %copy.31 = bf16[32,2,32,128]{3,2,1,0:T(8,128)(2,1)} copy(bf16[32,2,32,128]{3,0,2,1:T(8,128)(2,1)S(1)} %pad_maximum_fusion.4) | data formatting | bytes 1048576 | tf_op jit(solution)/shard_map/stack | solution.py:209
  50.2 0.0 copy-start.1
  50.2 3.1 %all-to-all-start.2 = ((bf16[32,2,32,128]{3,2,1,0:T(8,128)(2,1)}), bf16[32,2,32,128]{3,2,1,0:T(8,128)(2,1)S(1)}, u32[]{:S(2)}, u32[]{:S(2)}) async-start(bf16[32,2,32,128]{3,2,1,0:T(8,128)(2,1)} %copy.31), calls=%async_computation.2 | async-start | bytes 1048576 | tf_op jit(solution)/shard_map/all_to_all | solution.py:208
  53.3 0.0 copy-done
  53.3 0.0 copy-start.2
  53.3 0.3 copy.32
  53.6 0.0 copy-done.1
  53.6 0.0 copy-start.3
  53.6 0.3 copy.33
  53.9 0.5 copy-done.2
  54.4 0.3 copy.24
  54.6 14.2 %all-to-all-done.2 = bf16[32,2,32,128]{3,2,1,0:T(8,128)(2,1)S(1)} async-done(((bf16[32,2,32,128]{3,2,1,0:T(8,128)(2,1)}), bf16[32,2,32,128]{3,2,1,0:T(8,128)(2,1)S(1)}, u32[]{:S(2)}, u32[]{:S(2)}) %all-to-all-start.2) | async-done | bytes 524320 | tf_op jit(solution)/shard_map/all_to_all | solution.py:208
  68.9 0.0 copy-done.3
  68.9 0.5 fusion.21
  69.3 1.0 %copy.34 = bf16[128,2048]{1,0:T(8,128)(2,1)} copy(bf16[128,2048]{0,1:T(8,128)(2,1)S(1)} %fusion.21) | data formatting | bytes 1048576 | tf_op jit(solution)/shard_map/convert_element_type | solution.py:218
  (1 shorter events, 0.0 us)
Async XLA Ops:
  2.6 22.8 %all-to-all-start = ((bf16[32,2,32,128]{3,2,1,0:T(8,128)(2,1)}), bf16[32,2,32,128]{3,2,1,0:T(8,128)(2,1)S(1)}, u32[]{:S(2)}, u32[]{:S(2)}) async-start(bf16[32,2,32,128]{3,2,1,0:T(8,128)(2,1)} %get-tuple-element.8), calls=%async_computation | async-start | bytes 1048576 | tf_op jit(solution)/shard_map/all_to_all | solution.py:197
  25.5 18.6 %all-to-all-start.1 = ((bf16[32,2,32,128]{3,2,1,0:T(8,128)(2,1)}), bf16[32,2,32,128]{3,2,1,0:T(8,128)(2,1)S(1)}, u32[]{:S(2)}, u32[]{:S(2)}) async-start(bf16[32,2,32,128]{3,2,1,0:T(8,128)(2,1)} %get-tuple-element.9), calls=%async_computation.1 | async-start | bytes 1048576 | tf_op jit(solution)/shard_map/all_to_all | solution.py:197
  49.2 4.1 %copy-start = (bf16[128,2048]{1,0:T(8,128)(2,1)S(1)}, bf16[128,2048]{1,0:T(8,128)(2,1)}, u32[]{:S(2)}) copy-start(bf16[128,2048]{1,0:T(8,128)(2,1)} %key_ref.1) | copy-start | bytes 1572868
  50.2 3.4 %copy-start.1 = (bf16[128,2048]{1,0:T(8,128)(2,1)S(1)}, bf16[128,2048]{1,0:T(8,128)(2,1)}, u32[]{:S(2)}) copy-start(bf16[128,2048]{1,0:T(8,128)(2,1)} %value_ref.1) | copy-start | bytes 1572868
  50.2 18.6 %all-to-all-start.2 = ((bf16[32,2,32,128]{3,2,1,0:T(8,128)(2,1)}), bf16[32,2,32,128]{3,2,1,0:T(8,128)(2,1)S(1)}, u32[]{:S(2)}, u32[]{:S(2)}) async-start(bf16[32,2,32,128]{3,2,1,0:T(8,128)(2,1)} %copy.31), calls=%async_computation.2 | async-start | bytes 1048576 | tf_op jit(solution)/shard_map/all_to_all | solution.py:208
  53.3 1.0 %copy-start.2 = (bf16[128,2048]{1,0:T(8,128)(2,1)S(1)}, bf16[128,2048]{1,0:T(8,128)(2,1)}, u32[]{:S(2)}) copy-start(bf16[128,2048]{1,0:T(8,128)(2,1)} %param.6) | copy-start | bytes 1572868
  53.6 15.2 %copy-start.3 = (f32[2048]{0:T(1024)S(1)}, f32[2048]{0:T(1024)}, u32[]{:S(2)}) copy-start(f32[2048]{0:T(1024)} %param.11) | copy-start | bytes 24580

commit v12 on v11

--- a/solution.py
+++ b/solution.py
@@ -183,7 +183,7 @@
     row_count = mixed.shape[0]
     channels = mixed.shape[1]
     own_width = channels // n_dev
-    pieces = 2 if own_width % 16 == 0 else 1
+    pieces = 1
     piece_width = own_width // pieces
     if piece_width % 16 == 0:
         sent = prepare(key_in, value_in, filters, group_index, n_dev, pieces)

time: 70.8 us -> 67.8 us (0.958)
  starting transfers between devices: 13.4 us -> 10.9 us
    all_to_all x2 -> x1, starting transfers between devices: 10.4 us -> 7.3 us  [by_channels(): lax.all_to_all(sent[piece], ('outer', 'inner'), split_axis=0, concat_axis...]
    dot_general x8 -> x4, matrix products: 8.08 us -> 7.51 us  [contract(): jnp.einsum(pattern, left_op, right_op, precision=lax.Precision.HIGH, pref...]
    all_to_all x2 -> x1, waiting for transfers between devices: 25.2 us -> 25.4 us  [by_channels(): lax.all_to_all(sent[piece], ('outer', 'inner'), split_axis=0, concat_axis...]
  transfers between devices with their start and end apart: 3 -> 2, of which waited for: 3 -> 2; matrix products, arithmetic and copies ran while one was open for 9% -> 2% of each run, Pallas kernels for 0% -> 0%
where the time goes in v12:
time: 67.8 us; the launch traced here: 67.5 us
  waiting for transfers between devices  40.1 us (59%)
  starting transfers between devices  10.9 us (16%)
  matrix products  7.51 us (11%)
  other arithmetic  3.25 us (5%)
  local copies, waits for them, and re-layouts  2.84 us (4%)
  Pallas kernels  2.65 us (4%)
    all_to_all x1, waiting for transfers between devices, by_channels(): lax.all_to_all(sent[piece], ('outer', 'inner'), split_axis=0, concat_axis...  25.4 us
    all_to_all x1, waiting for transfers between devices, by_channels(): lax.all_to_all(jnp.stack(results, axis=1), ('outer', 'inner'), split_axis...  14.7 us
    dot_general x4, matrix products, contract(): jnp.einsum(pattern, left_op, right_op, precision=lax.Precision.HIGH, pref...  7.51 us
    all_to_all x1, starting transfers between devices, by_channels(): lax.all_to_all(sent[piece], ('outer', 'inner'), split_axis=0, concat_axis...  7.3 us
    all_to_all x1, starting transfers between devices, by_channels(): lax.all_to_all(jnp.stack(results, axis=1), ('outer', 'inner'), split_axis...  3.62 us
    pallas_call x1, Pallas kernels, prepare(): pl.pallas_call(prep_kernel, out_shape=tuple((jax.ShapeDtypeStruct((n_dev,...  2.65 us
  transfers between devices with their start and end apart: 2, of which 2 were waited for; matrix products, arithmetic and copies ran while one was open for 2% of the time, Pallas kernels for 0%

profile of v12, /device:TPU:0, one launch (start us, length us, event | category | flops | bytes accessed | tf_op | source)
XLA Modules:
  0.0 67.5 jit_solution(9012569442765587707)
XLA Ops:
  0.0 2.7 %shard_map.64 = bf16[32,2,64,128]{3,2,1,0:T(8,128)(2,1)} custom-call(bf16[128,2048]{1,0:T(8,128)(2,1)} %key_ref.1, bf16[128,2048]{1,0:T(8,128)(2,1)} %value_ref.1, bf16[128,128]{1,0:T(8,128)(2,1)} %filters_ref.1, s32[1,2048]{1,0:T(1,128)} %bitcast.30), custom_call_target="tpu_custom_call" | custom-call | tf_op jit(solution)/shard_map/pallas_call | solution.py:101
  2.7 7.3 %all-to-all-start = ((bf16[32,2,64,128]{3,2,1,0:T(8,128)(2,1)}), bf16[32,2,64,128]{3,2,1,0:T(8,128)(2,1)S(1)}, u32[]{:S(2)}, u32[]{:S(2)}) async-start(bf16[32,2,64,128]{3,2,1,0:T(8,128)(2,1)} %shard_map.64), calls=%async_computation | async-start | bytes 2097152 | tf_op jit(solution)/shard_map/all_to_all | solution.py:197
  10.0 0.1 sine_negate_fusion
  10.1 0.1 fusion.62
  10.2 0.3 fusion.39
  10.4 0.3 broadcast_multiply_fusion
  10.7 0.1 cosine_multiply_fusion
  10.8 25.4 %all-to-all-done = bf16[32,2,64,128]{3,2,1,0:T(8,128)(2,1)S(1)} async-done(((bf16[32,2,64,128]{3,2,1,0:T(8,128)(2,1)}), bf16[32,2,64,128]{3,2,1,0:T(8,128)(2,1)S(1)}, u32[]{:S(2)}, u32[]{:S(2)}) %all-to-all-start) | async-done | bytes 1048608 | tf_op jit(solution)/shard_map/all_to_all | solution.py:197
  36.2 1.6 %fusion.20 = f32[66,128,128]{2,0,1:T(8,128)S(1)} fusion(bf16[32,128,128]{2,1,0:T(8,128)(2,1)S(1)} %bitcast.29, f32[33,32]{0,1:T(8,128)S(1)} %get-tuple-element.13, f32[33,32]{0,1:T(8,128)S(1)} %get-tuple-element.14), kind=kOutput, calls=%fused_computation.23 | convolution fusion | flops 207620160 | bytes 5382400 | tf_op jit(solution)/shard_map/kn,ncb->kcb/dot_general | solution.py:11
  37.8 0.7 %multiply_add_fusion = (f32[33,128,128]{2,0,1:T(8,128)S(1)}, f32[33,128,128]{2,0,1:T(8,128)S(1)}) fusion(f32[66,128,128]{2,0,1:T(8,128)S(1)} %fusion.20, f32[33,128]{1,0:T(8,128)S(1)} %get-tuple-element.15, f32[33,128]{1,0:T(8,128)S(1)} %get-tuple-element.16), kind=kLoop, calls=%fused_computation.4 | loop fusion | flops 3244032 | bytes 8684544 | tf_op jit(solution)/shard_map/add | solution.py:38
  38.5 0.3 pad_maximum_fusion
  38.9 3.0 %fusion = f32[33,128,256]{2,1,0:T(8,128)S(1)} fusion(f32[33,128,256]{2,0,1:T(8,128)S(1)} %pad_maximum_fusion, f32[128,128]{1,0:T(8,128)S(1)} %fusion.39, f32[128,128]{1,0:T(8,128)S(1)} %get-tuple-element.18, f32[128,128]{1,0:T(8,128)S(1)} %get-tuple-element.17), kind=kOutput, calls=%fused_computation.1 | convolution fusion | flops 1661140992 | bytes 8847360 | tf_op jit(solution)/shard_map/kcb,bq->kcq/dot_general | solution.py:11
  41.9 0.3 multiply_subtract_fusion.2
  42.2 1.0 %fusion.4 = f32[33,64,256]{2,1,0:T(8,128)S(1)} fusion(f32[33,64,128]{2,1,0:T(8,128)S(1)} %get-tuple-element.8, f32[33,64,128]{2,1,0:T(8,128)S(1)} %get-tuple-element.7, f32[128,128]{1,0:T(8,128)S(1)} %fusion.39, f32[128,128]{1,0:T(8,128)S(1)} %get-tuple-element.17, f32[128,128]{1,0:T(8,128)S(1)} %get-tuple-element.18), kind=kOutput, calls=%fused_computation.7 | convolution fusion | flops 831209472 | bytes 4521984 | tf_op jit(solution)/shard_map/kcq,qb->kcb/dot_general | solution.py:11
  43.3 0.3 multiply_subtract_fusion.1
  43.6 0.2 pad_maximum_fusion.1
  43.9 0.0 copy-start
  43.9 1.9 %fusion.14 = bf16[32,1,64,128]{3,0,2,1:T(8,128)(2,1)S(1)} fusion(f32[66,64,128]{2,1,0:T(8,128)S(1)} %pad_maximum_fusion.1, f32[32,33]{1,0:T(8,128)S(1)} %get-tuple-element.12, f32[32,33]{1,0:T(8,128)S(1)} %get-tuple-element.11), kind=kOutput, calls=%fused_computation.14 | convolution fusion | flops 104335424 | bytes 2695424 | tf_op jit(solution)/shard_map/nk,kcb->ncb/dot_general | solution.py:11
  45.8 0.0 copy-start.1
  45.8 0.0 copy-start.2
  45.8 1.0 %copy.22 = bf16[32,1,64,128]{3,2,1,0:T(8,128)(2,1)} copy(bf16[32,1,64,128]{3,0,2,1:T(8,128)(2,1)S(1)} %fusion.14) | data formatting | bytes 1048576 | tf_op jit(solution)/shard_map/stack | solution.py:209
  46.8 0.0 copy-start.3
  46.8 3.6 %all-to-all-start.1 = ((bf16[32,1,64,128]{3,2,1,0:T(8,128)(2,1)}), bf16[32,1,64,128]{3,2,1,0:T(8,128)(2,1)S(1)}, u32[]{:S(2)}, u32[]{:S(2)}) async-start(bf16[32,1,64,128]{3,2,1,0:T(8,128)(2,1)} %copy.22), calls=%async_computation.1 | async-start | bytes 1048576 | tf_op jit(solution)/shard_map/all_to_all | solution.py:208
  50.4 0.0 copy-done
  50.4 0.3 copy.24
  50.7 0.0 copy-done.1
  50.7 0.3 copy.25
  51.0 0.0 copy-done.2
  51.0 0.3 copy.18
  51.3 14.7 %all-to-all-done.1 = bf16[32,1,64,128]{3,2,1,0:T(8,128)(2,1)S(1)} async-done(((bf16[32,1,64,128]{3,2,1,0:T(8,128)(2,1)}), bf16[32,1,64,128]{3,2,1,0:T(8,128)(2,1)S(1)}, u32[]{:S(2)}, u32[]{:S(2)}) %all-to-all-start.1) | async-done | bytes 524320 | tf_op jit(solution)/shard_map/all_to_all | solution.py:208
  66.0 0.0 copy-done.3
  66.0 0.5 fusion.19
  66.5 1.0 %copy.26 = bf16[128,2048]{1,0:T(8,128)(2,1)} copy(bf16[128,2048]{0,1:T(8,128)(2,1)S(1)} %fusion.19) | data formatting | bytes 1048576 | tf_op jit(solution)/shard_map/convert_element_type | solution.py:218
  (1 shorter events, 0.0 us)
Async XLA Ops:
  2.7 33.5 %all-to-all-start = ((bf16[32,2,64,128]{3,2,1,0:T(8,128)(2,1)}), bf16[32,2,64,128]{3,2,1,0:T(8,128)(2,1)S(1)}, u32[]{:S(2)}, u32[]{:S(2)}) async-start(bf16[32,2,64,128]{3,2,1,0:T(8,128)(2,1)} %shard_map.64), calls=%async_computation | async-start | bytes 2097152 | tf_op jit(solution)/shard_map/all_to_all | solution.py:197
  43.9 6.6 %copy-start = (bf16[128,2048]{1,0:T(8,128)(2,1)S(1)}, bf16[128,2048]{1,0:T(8,128)(2,1)}, u32[]{:S(2)}) copy-start(bf16[128,2048]{1,0:T(8,128)(2,1)} %key_ref.1) | copy-start | bytes 1572868
  45.8 4.9 %copy-start.1 = (bf16[128,2048]{1,0:T(8,128)(2,1)S(1)}, bf16[128,2048]{1,0:T(8,128)(2,1)}, u32[]{:S(2)}) copy-start(bf16[128,2048]{1,0:T(8,128)(2,1)} %value_ref.1) | copy-start | bytes 1572868
  45.8 5.2 %copy-start.2 = (bf16[128,2048]{1,0:T(8,128)(2,1)S(1)}, bf16[128,2048]{1,0:T(8,128)(2,1)}, u32[]{:S(2)}) copy-start(bf16[128,2048]{1,0:T(8,128)(2,1)} %param.6) | copy-start | bytes 1572868
  46.8 19.2 %copy-start.3 = (f32[2048]{0:T(1024)S(1)}, f32[2048]{0:T(1024)}, u32[]{:S(2)}) copy-start(f32[2048]{0:T(1024)} %param.11) | copy-start | bytes 24580
  46.8 19.2 %all-to-all-start.1 = ((bf16[32,1,64,128]{3,2,1,0:T(8,128)(2,1)}), bf16[32,1,64,128]{3,2,1,0:T(8,128)(2,1)S(1)}, u32[]{:S(2)}, u32[]{:S(2)}) async-start(bf16[32,1,64,128]{3,2,1,0:T(8,128)(2,1)} %copy.22), calls=%async_computation.1 | async-start | bytes 1048576 | tf_op jit(solution)/shard_map/all_to_all | solution.py:208

commit v13 on v12

--- a/solution.py
+++ b/solution.py
@@ -140,9 +140,14 @@
     size_a = 2 * n_dev
     kept = n_dev + 1
     padded = size_a * row_count
-    stacked = got.reshape(n_dev, 2 * own_width, row_count).astype(jnp.float32)
+    stacked = got.reshape(n_dev, 2 * own_width, row_count)
     first_cos, first_sin = dft_table(kept, n_dev, size_a)
-    first = contract("kn,ncb->kcb", jnp.concatenate([first_cos, -first_sin], axis=0), stacked)
+    first_table = jnp.concatenate([first_cos, -first_sin], axis=0)
+    table_high = first_table.astype(jnp.bfloat16)
+    table_low = (first_table - table_high.astype(jnp.float32)).astype(jnp.bfloat16)
+    first = jnp.einsum(
+        "kn,ncb->kcb", table_high, stacked, preferred_element_type=jnp.float32
+    ) + jnp.einsum("kn,ncb->kcb", table_low, stacked, preferred_element_type=jnp.float32)
     twiddle = angles_of(
         jnp.arange(kept, dtype=jnp.int32)[:, None]
         * jnp.arange(row_count, dtype=jnp.int32)[None, :],
@@ -176,6 +181,19 @@
         jnp.concatenate([real_part, imag_part], axis=0),
     )
     return (outcome * (1.0 / padded)).astype(jnp.bfloat16)
+
+
+def exchange(blocks, n_dev, me):
+    axes = ("outer", "inner")
+    arrived = [blocks[me][None]]
+    for shift in range(1, n_dev):
+        part = lax.dynamic_index_in_dim(blocks, (me + shift) % n_dev, axis=0)
+        arrived.append(
+            lax.ppermute(part, axes, perm=[(d, (d + shift) % n_dev) for d in range(n_dev)])
+        )
+    reversed_order = jnp.concatenate([arrived[0]] + arrived[:0:-1], axis=0)
+    doubled = jnp.concatenate([reversed_order, reversed_order], axis=0)
+    return lax.dynamic_slice_in_dim(doubled, (n_dev - me) % n_dev, n_dev, axis=0)
 
 
 def by_channels(mixed, key_in, value_in, filters, group_index):
@@ -205,9 +223,13 @@
             outcome, got = lax.optimization_barrier((outcome, got))
         outcome = convolve_block(got, n_dev, row_count)
         results.append(outcome)
-    returned = lax.all_to_all(
-        jnp.stack(results, axis=1), ("outer", "inner"), split_axis=0, concat_axis=0, tiled=True
-    )
+    me = lax.axis_index("outer") * lax.axis_size("inner") + lax.axis_index("inner")
+    if n_dev <= 32:
+        returned = exchange(jnp.stack(results, axis=1), n_dev, me)
+    else:
+        returned = lax.all_to_all(
+            jnp.stack(results, axis=1), ("outer", "inner"), split_axis=0, concat_axis=0, tiled=True
+        )
     return returned.reshape(channels, row_count)
 
 

time: 67.8 us -> 107 us (1.58)
  starting transfers between devices: 10.9 us -> 55.3 us
  waiting for transfers between devices: 40.1 us -> 32 us
  local copies, waits for them, and re-layouts: 2.84 us -> 4.24 us
  between operations: 0.19 us -> 1.26 us
    ppermute x0 -> x31, starting transfers between devices: none -> 48 us  [exchange(): lax.ppermute(part, axes, perm=[(d, (d + shift) % n_dev) for d in range(n_...]
    all_to_all x1 -> x0, waiting for transfers between devices: 14.7 us -> none  [by_channels(): lax.all_to_all(jnp.stack(results, axis=1), ('outer', 'inner'), split_axis...]
    ppermute x0 -> x31, waiting for transfers between devices: none -> 8.06 us  [exchange(): lax.ppermute(part, axes, perm=[(d, (d + shift) % n_dev) for d in range(n_...]
    all_to_all x1 -> x0, starting transfers between devices: 3.62 us -> none  [by_channels(): lax.all_to_all(jnp.stack(results, axis=1), ('outer', 'inner'), split_axis...]
    dot_general x0 -> x2, matrix products: none -> 2.08 us  [the longest x1 1.17 us: convolve_block(): jnp.einsum('kn,ncb->kcb', table_low, stacked, preferred_element_type=jnp....]
    dot_general x4 -> x3, matrix products: 7.51 us -> 5.91 us  [contract(): jnp.einsum(pattern, left_op, right_op, precision=lax.Precision.HIGH, pref...]
    all_to_all x1, waiting for transfers between devices: 25.4 us -> 23.9 us  [by_channels(): lax.all_to_all(sent[piece], ('outer', 'inner'), split_axis=0, concat_axis...]
  transfers between devices with their start and end apart: 2 -> 32, of which waited for: 2 -> 6; matrix products, arithmetic and copies ran while one was open for 2% -> 3% of each run, Pallas kernels for 0% -> 0%
where the time goes in v13:
time: 107 us
  starting transfers between devices  55.3 us (52%)
  waiting for transfers between devices  32 us (30%)
  matrix products  7.99 us (7%)
  local copies, waits for them, and re-layouts  4.24 us (4%)
  other arithmetic  3.26 us (3%)
  Pallas kernels  2.73 us (3%)
  between operations  1.26 us (1%)
    ppermute x31, starting transfers between devices, exchange(): lax.ppermute(part, axes, perm=[(d, (d + shift) % n_dev) for d in range(n_...  48 us
    all_to_all x1, waiting for transfers between devices, by_channels(): lax.all_to_all(sent[piece], ('outer', 'inner'), split_axis=0, concat_axis...  23.9 us
    ppermute x31, waiting for transfers between devices, exchange(): lax.ppermute(part, axes, perm=[(d, (d + shift) % n_dev) for d in range(n_...  8.06 us
    all_to_all x1, starting transfers between devices, by_channels(): lax.all_to_all(sent[piece], ('outer', 'inner'), split_axis=0, concat_axis...  7.3 us
    dot_general x3, matrix products, contract(): jnp.einsum(pattern, left_op, right_op, precision=lax.Precision.HIGH, pref...  5.91 us
    pallas_call x1, Pallas kernels, prepare(): pl.pallas_call(prep_kernel, out_shape=tuple((jax.ShapeDtypeStruct((n_dev,...  2.73 us
  transfers between devices with their start and end apart: 32, of which 6 were waited for; matrix products, arithmetic and copies ran while one was open for 3% of the time, Pallas kernels for 0%

profile of v13, /device:TPU:0, one launch (start us, length us, event | category | flops | bytes accessed | tf_op | source)
XLA Modules:
  0.0 106.8 jit_solution(11150468161743027056)
XLA Ops:
  0.0 2.7 %shard_map.64 = bf16[32,2,64,128]{3,2,1,0:T(8,128)(2,1)} custom-call(bf16[128,2048]{1,0:T(8,128)(2,1)} %key_ref.1, bf16[128,2048]{1,0:T(8,128)(2,1)} %value_ref.1, bf16[128,128]{1,0:T(8,128)(2,1)} %filters_ref.1, s32[1,2048]{1,0:T(1,128)} %bitcast.157), custom_call_target="tpu_custom_call" | custom-call | tf_op jit(solution)/shard_map/pallas_call | solution.py:101
  2.7 7.3 %all-to-all-start = ((bf16[32,2,64,128]{3,2,1,0:T(8,128)(2,1)}), bf16[32,2,64,128]{3,2,1,0:T(8,128)(2,1)S(1)}, u32[]{:S(2)}, u32[]{:S(2)}) async-start(bf16[32,2,64,128]{3,2,1,0:T(8,128)(2,1)} %shard_map.64), calls=%async_computation | async-start | bytes 2097152 | tf_op jit(solution)/shard_map/all_to_all | solution.py:215
  10.5 0.3 copy.76
  10.8 0.3 copy.77
  11.1 0.3 copy.71
  12.3 23.9 %all-to-all-done = bf16[32,2,64,128]{3,2,1,0:T(8,128)(2,1)S(1)} async-done(((bf16[32,2,64,128]{3,2,1,0:T(8,128)(2,1)}), bf16[32,2,64,128]{3,2,1,0:T(8,128)(2,1)S(1)}, u32[]{:S(2)}, u32[]{:S(2)}) %all-to-all-start) | async-done | bytes 1048608 | tf_op jit(solution)/shard_map/all_to_all | solution.py:215
  36.3 0.9 fusion.18
  37.2 1.2 %convolution_add_fusion = f32[66,128,128]{2,0,1:T(8,128)S(1)} fusion(f32[66,128,128]{2,0,1:T(8,128)S(1)} %fusion.18, bf16[32,128,128]{2,1,0:T(8,128)(2,1)S(1)} %bitcast.125, f32[33,32]{0,1:T(8,128)S(1)} %get-tuple-element.45, f32[33,32]{0,1:T(8,128)S(1)} %get-tuple-element.46), kind=kOutput, calls=%fused_computation.7 | convolution fusion | flops 70297920 | bytes 9707776 | tf_op jit(solution)/shard_map/kn,ncb->kcb/dot_general | solution.py:150
  38.4 0.7 multiply_add_fusion
  39.1 0.3 pad_maximum_fusion
  39.4 3.0 %fusion = f32[33,128,256]{2,1,0:T(8,128)S(1)} fusion(f32[33,128,256]{2,0,1:T(8,128)S(1)} %pad_maximum_fusion, f32[128,128]{1,0:T(8,128)S(1)} %fusion.37, f32[128,128]{1,0:T(8,128)S(1)} %get-tuple-element.50, f32[128,128]{1,0:T(8,128)S(1)} %get-tuple-element.49), kind=kOutput, calls=%fused_computation.1 | convolution fusion | flops 1661140992 | bytes 8847360 | tf_op jit(solution)/shard_map/kcb,bq->kcq/dot_general | solution.py:11
  42.4 0.3 multiply_subtract_fusion.2
  42.8 1.0 fusion.4
  43.8 0.3 multiply_subtract_fusion.1
  44.4 1.9 %fusion.11 = bf16[32,64,128]{2,0,1:T(8,128)(2,1)S(1)} fusion(f32[66,64,128]{2,1,0:T(8,128)S(1)} %pad_maximum_fusion.1, f32[32,33]{1,0:T(8,128)S(1)} %get-tuple-element.44, f32[32,33]{1,0:T(8,128)S(1)} %get-tuple-element.43), kind=kOutput, calls=%fused_computation.14 | convolution fusion | flops 104335424 | bytes 2695424 | tf_op jit(solution)/shard_map/nk,kcb->ncb/dot_general | solution.py:11
  46.3 0.6 constant_dynamic-slice_fusion.19
  47.0 3.0 %collective-permute-start = (bf16[1,1,64,128]{3,2,1,0:T(8,128)(2,1)S(1)}, bf16[1,1,64,128]{3,2,1,0:T(8,128)(2,1)S(1)}, u32[]{:S(2)}, u32[]{:S(2)}) collective-permute-start(bf16[1,1,64,128]{3,2,1,0:T(8,128)(2,1)S(1)} %bitcast.153), channel_id=1, source_target_pairs={{0,31},{1,0},{2,1},{3,2},{4,3},{5,4},{6,5},{7,6},{8,7},{9,8},{10,9... | collective-permute-start | bytes 49160 | tf_op jit(solution)/shard_map/ppermute | solution.py:192
  49.9 0.6 collective-permute-start.1
  50.6 0.6 collective-permute-start.3
  51.2 2.2 %collective-permute-start.4 = (bf16[1,1,64,128]{3,2,1,0:T(8,128)(2,1)S(1)}, bf16[1,1,64,128]{3,2,1,0:T(8,128)(2,1)S(1)}, u32[]{:S(2)}, u32[]{:S(2)}) collective-permute-start(bf16[1,1,64,128]{3,2,1,0:T(8,128)(2,1)S(1)} %bitcast.147), channel_id=1, source_target_pairs={{0,27},{1,28},{2,29},{3,30},{4,31},{5,0},{6,1},{7,2},{8,3},{9,4},{... | collective-permute-start | bytes 49160 | tf_op jit(solution)/shard_map/ppermute | solution.py:192
  53.4 1.0 constant_dynamic-slice_fusion.1
  54.8 2.7 %collective-permute-start.5 = (bf16[1,1,64,128]{3,2,1,0:T(8,128)(2,1)S(1)}, bf16[1,1,64,128]{3,2,1,0:T(8,128)(2,1)S(1)}, u32[]{:S(2)}, u32[]{:S(2)}) collective-permute-start(bf16[1,1,64,128]{3,2,1,0:T(8,128)(2,1)S(1)} %bitcast.156), channel_id=1, source_target_pairs={{0,26},{1,27},{2,28},{3,29},{4,30},{5,31},{6,0},{7,1},{8,2},{9,3},... | collective-permute-start | bytes 49160 | tf_op jit(solution)/shard_map/ppermute | solution.py:192
  57.6 1.2 %collective-permute-start.7 = (bf16[1,1,64,128]{3,2,1,0:T(8,128)(2,1)S(1)}, bf16[1,1,64,128]{3,2,1,0:T(8,128)(2,1)S(1)}, u32[]{:S(2)}, u32[]{:S(2)}) collective-permute-start(bf16[1,1,64,128]{3,2,1,0:T(8,128)(2,1)S(1)} %bitcast.154), channel_id=1, source_target_pairs={{0,24},{1,25},{2,26},{3,27},{4,28},{5,29},{6,30},{7,31},{8,0},{9,1... | collective-permute-start | bytes 49160 | tf_op jit(solution)/shard_map/ppermute | solution.py:192
  58.8 1.9 %collective-permute-start.8 = (bf16[1,1,64,128]{3,2,1,0:T(8,128)(2,1)S(1)}, bf16[1,1,64,128]{3,2,1,0:T(8,128)(2,1)S(1)}, u32[]{:S(2)}, u32[]{:S(2)}) collective-permute-start(bf16[1,1,64,128]{3,2,1,0:T(8,128)(2,1)S(1)} %bitcast.151), channel_id=1, source_target_pairs={{0,23},{1,24},{2,25},{3,26},{4,27},{5,28},{6,29},{7,30},{8,31},{9,... | collective-permute-start | bytes 49160 | tf_op jit(solution)/shard_map/ppermute | solution.py:192
  60.7 1.3 %collective-permute-start.9 = (bf16[1,1,64,128]{3,2,1,0:T(8,128)(2,1)S(1)}, bf16[1,1,64,128]{3,2,1,0:T(8,128)(2,1)S(1)}, u32[]{:S(2)}, u32[]{:S(2)}) collective-permute-start(bf16[1,1,64,128]{3,2,1,0:T(8,128)(2,1)S(1)} %bitcast.148), channel_id=1, source_target_pairs={{0,22},{1,23},{2,24},{3,25},{4,26},{5,27},{6,28},{7,29},{8,30},{9,... | collective-permute-start | bytes 49160 | tf_op jit(solution)/shard_map/ppermute | solution.py:192
  62.0 1.7 %collective-permute-start.10 = (bf16[1,1,64,128]{3,2,1,0:T(8,128)(2,1)S(1)}, bf16[1,1,64,128]{3,2,1,0:T(8,128)(2,1)S(1)}, u32[]{:S(2)}, u32[]{:S(2)}) collective-permute-start(bf16[1,1,64,128]{3,2,1,0:T(8,128)(2,1)S(1)} %bitcast.146), channel_id=1, source_target_pairs={{0,21},{1,22},{2,23},{3,24},{4,25},{5,26},{6,27},{7,28},{8,29},{9,... | collective-permute-start | bytes 49160 | tf_op jit(solution)/shard_map/ppermute | solution.py:192
  63.7 1.4 %collective-permute-start.11 = (bf16[1,1,64,128]{3,2,1,0:T(8,128)(2,1)S(1)}, bf16[1,1,64,128]{3,2,1,0:T(8,128)(2,1)S(1)}, u32[]{:S(2)}, u32[]{:S(2)}) collective-permute-start(bf16[1,1,64,128]{3,2,1,0:T(8,128)(2,1)S(1)} %bitcast.145), channel_id=1, source_target_pairs={{0,20},{1,21},{2,22},{3,23},{4,24},{5,25},{6,26},{7,27},{8,28},{9,... | collective-permute-start | bytes 49160 | tf_op jit(solution)/shard_map/ppermute | solution.py:192
  65.1 3.2 %collective-permute-start.12 = (bf16[1,1,64,128]{3,2,1,0:T(8,128)(2,1)S(1)}, bf16[1,1,64,128]{3,2,1,0:T(8,128)(2,1)S(1)}, u32[]{:S(2)}, u32[]{:S(2)}) collective-permute-start(bf16[1,1,64,128]{3,2,1,0:T(8,128)(2,1)S(1)} %bitcast.144), channel_id=1, source_target_pairs={{0,19},{1,20},{2,21},{3,22},{4,23},{5,24},{6,25},{7,26},{8,27},{9,... | collective-permute-start | bytes 49160 | tf_op jit(solution)/shard_map/ppermute | solution.py:192
  68.3 3.9 %collective-permute-start.13 = (bf16[1,1,64,128]{3,2,1,0:T(8,128)(2,1)S(1)}, bf16[1,1,64,128]{3,2,1,0:T(8,128)(2,1)S(1)}, u32[]{:S(2)}, u32[]{:S(2)}) collective-permute-start(bf16[1,1,64,128]{3,2,1,0:T(8,128)(2,1)S(1)} %bitcast.143), channel_id=1, source_target_pairs={{0,18},{1,19},{2,20},{3,21},{4,22},{5,23},{6,24},{7,25},{8,26},{9,... | collective-permute-start | bytes 49160 | tf_op jit(solution)/shard_map/ppermute | solution.py:192
  72.5 3.3 %collective-permute-start.16 = (bf16[1,1,64,128]{3,2,1,0:T(8,128)(2,1)S(1)}, bf16[1,1,64,128]{3,2,1,0:T(8,128)(2,1)S(1)}, u32[]{:S(2)}, u32[]{:S(2)}) collective-permute-start(bf16[1,1,64,128]{3,2,1,0:T(8,128)(2,1)S(1)} %bitcast.140), channel_id=1, source_target_pairs={{0,15},{1,16},{2,17},{3,18},{4,19},{5,20},{6,21},{7,22},{8,23},{9,... | collective-permute-start | bytes 49160 | tf_op jit(solution)/shard_map/ppermute | solution.py:192
  75.9 0.5 collective-permute-start.17
  76.4 1.0 collective-permute-start.18
  77.4 3.5 %collective-permute-start.19 = (bf16[1,1,64,128]{3,2,1,0:T(8,128)(2,1)S(1)}, bf16[1,1,64,128]{3,2,1,0:T(8,128)(2,1)S(1)}, u32[]{:S(2)}, u32[]{:S(2)}) collective-permute-start(bf16[1,1,64,128]{3,2,1,0:T(8,128)(2,1)S(1)} %bitcast.137), channel_id=1, source_target_pairs={{0,12},{1,13},{2,14},{3,15},{4,16},{5,17},{6,18},{7,19},{8,20},{9,... | collective-permute-start | bytes 49160 | tf_op jit(solution)/shard_map/ppermute | solution.py:192
  80.8 1.5 %collective-permute-start.20 = (bf16[1,1,64,128]{3,2,1,0:T(8,128)(2,1)S(1)}, bf16[1,1,64,128]{3,2,1,0:T(8,128)(2,1)S(1)}, u32[]{:S(2)}, u32[]{:S(2)}) collective-permute-start(bf16[1,1,64,128]{3,2,1,0:T(8,128)(2,1)S(1)} %bitcast.136), channel_id=1, source_target_pairs={{0,11},{1,12},{2,13},{3,14},{4,15},{5,16},{6,17},{7,18},{8,19},{9,... | collective-permute-start | bytes 49160 | tf_op jit(solution)/shard_map/ppermute | solution.py:192
  82.4 3.2 %collective-permute-start.21 = (bf16[1,1,64,128]{3,2,1,0:T(8,128)(2,1)S(1)}, bf16[1,1,64,128]{3,2,1,0:T(8,128)(2,1)S(1)}, u32[]{:S(2)}, u32[]{:S(2)}) collective-permute-start(bf16[1,1,64,128]{3,2,1,0:T(8,128)(2,1)S(1)} %bitcast.135), channel_id=1, source_target_pairs={{0,10},{1,11},{2,12},{3,13},{4,14},{5,15},{6,16},{7,17},{8,18},{9,... | collective-permute-start | bytes 49160 | tf_op jit(solution)/shard_map/ppermute | solution.py:192
  85.6 2.1 %collective-permute-start.23 = (bf16[1,1,64,128]{3,2,1,0:T(8,128)(2,1)S(1)}, bf16[1,1,64,128]{3,2,1,0:T(8,128)(2,1)S(1)}, u32[]{:S(2)}, u32[]{:S(2)}) collective-permute-start(bf16[1,1,64,128]{3,2,1,0:T(8,128)(2,1)S(1)} %bitcast.133), channel_id=1, source_target_pairs={{0,8},{1,9},{2,10},{3,11},{4,12},{5,13},{6,14},{7,15},{8,16},{9,17... | collective-permute-start | bytes 49160 | tf_op jit(solution)/shard_map/ppermute | solution.py:192
  87.7 3.9 %collective-permute-start.24 = (bf16[1,1,64,128]{3,2,1,0:T(8,128)(2,1)S(1)}, bf16[1,1,64,128]{3,2,1,0:T(8,128)(2,1)S(1)}, u32[]{:S(2)}, u32[]{:S(2)}) collective-permute-start(bf16[1,1,64,128]{3,2,1,0:T(8,128)(2,1)S(1)} %bitcast.132), channel_id=1, source_target_pairs={{0,7},{1,8},{2,9},{3,10},{4,11},{5,12},{6,13},{7,14},{8,15},{9,16}... | collective-permute-start | bytes 49160 | tf_op jit(solution)/shard_map/ppermute | solution.py:192
  91.6 1.1 %collective-permute-start.26 = (bf16[1,1,64,128]{3,2,1,0:T(8,128)(2,1)S(1)}, bf16[1,1,64,128]{3,2,1,0:T(8,128)(2,1)S(1)}, u32[]{:S(2)}, u32[]{:S(2)}) collective-permute-start(bf16[1,1,64,128]{3,2,1,0:T(8,128)(2,1)S(1)} %bitcast.130), channel_id=1, source_target_pairs={{0,5},{1,6},{2,7},{3,8},{4,9},{5,10},{6,11},{7,12},{8,13},{9,14},{... | collective-permute-start | bytes 49160 | tf_op jit(solution)/shard_map/ppermute | solution.py:192
  92.7 0.9 collective-permute-start.27
  93.6 0.7 collective-permute-start.28
  94.3 2.4 %collective-permute-start.29 = (bf16[1,1,64,128]{3,2,1,0:T(8,128)(2,1)S(1)}, bf16[1,1,64,128]{3,2,1,0:T(8,128)(2,1)S(1)}, u32[]{:S(2)}, u32[]{:S(2)}) collective-permute-start(bf16[1,1,64,128]{3,2,1,0:T(8,128)(2,1)S(1)} %bitcast.127), channel_id=1, source_target_pairs={{0,2},{1,3},{2,4},{3,5},{4,6},{5,7},{6,8},{7,9},{8,10},{9,11},{10,... | collective-permute-start | bytes 49160 | tf_op jit(solution)/shard_map/ppermute | solution.py:192
  96.7 1.3 %collective-permute-done.25 = bf16[1,1,64,128]{3,2,1,0:T(8,128)(2,1)S(1)} collective-permute-done((bf16[1,1,64,128]{3,2,1,0:T(8,128)(2,1)S(1)}, bf16[1,1,64,128]{3,2,1,0:T(8,128)(2,1)S(1)}, u32[]{:S(2)}, u32[]{:S(2)}) %collective-permute-start.25) | collective-permute-done | bytes 16416 | tf_op jit(solution)/shard_map/ppermute | solution.py:192
  98.1 1.1 %collective-permute-done.27 = bf16[1,1,64,128]{3,2,1,0:T(8,128)(2,1)S(1)} collective-permute-done((bf16[1,1,64,128]{3,2,1,0:T(8,128)(2,1)S(1)}, bf16[1,1,64,128]{3,2,1,0:T(8,128)(2,1)S(1)}, u32[]{:S(2)}, u32[]{:S(2)}) %collective-permute-start.27) | collective-permute-done | bytes 16416 | tf_op jit(solution)/shard_map/ppermute | solution.py:192
  99.2 0.8 collective-permute-done.28
  100.0 2.3 %collective-permute-done.29 = bf16[1,1,64,128]{3,2,1,0:T(8,128)(2,1)S(1)} collective-permute-done((bf16[1,1,64,128]{3,2,1,0:T(8,128)(2,1)S(1)}, bf16[1,1,64,128]{3,2,1,0:T(8,128)(2,1)S(1)}, u32[]{:S(2)}, u32[]{:S(2)}) %collective-permute-start.29) | collective-permute-done | bytes 16416 | tf_op jit(solution)/shard_map/ppermute | solution.py:192
  102.3 2.5 %collective-permute-done.30 = bf16[1,1,64,128]{3,2,1,0:T(8,128)(2,1)S(1)} collective-permute-done((bf16[1,1,64,128]{3,2,1,0:T(8,128)(2,1)S(1)}, bf16[1,1,64,128]{3,2,1,0:T(8,128)(2,1)S(1)}, u32[]{:S(2)}, u32[]{:S(2)}) %collective-permute-start.30) | collective-permute-done | bytes 16416 | tf_op jit(solution)/shard_map/ppermute | solution.py:192
  105.3 0.5 fusion.16
  105.8 1.0 copy.78
  (144 shorter events, 2.3 us)
Async XLA Ops:
  0.0 10.5 %copy-start = (bf16[128,2048]{1,0:T(8,128)(2,1)S(1)}, bf16[128,2048]{1,0:T(8,128)(2,1)}, u32[]{:S(2)}) copy-start(bf16[128,2048]{1,0:T(8,128)(2,1)} %key_ref.1) | copy-start | bytes 1572868
  2.7 8.0 %copy-start.1 = (bf16[128,2048]{1,0:T(8,128)(2,1)S(1)}, bf16[128,2048]{1,0:T(8,128)(2,1)}, u32[]{:S(2)}) copy-start(bf16[128,2048]{1,0:T(8,128)(2,1)} %value_ref.1) | copy-start | bytes 1572868
  2.7 8.3 %copy-start.2 = (bf16[128,2048]{1,0:T(8,128)(2,1)S(1)}, bf16[128,2048]{1,0:T(8,128)(2,1)}, u32[]{:S(2)}) copy-start(bf16[128,2048]{1,0:T(8,128)(2,1)} %param.6) | copy-start | bytes 1572868
  2.7 33.5 %all-to-all-start = ((bf16[32,2,64,128]{3,2,1,0:T(8,128)(2,1)}), bf16[32,2,64,128]{3,2,1,0:T(8,128)(2,1)S(1)}, u32[]{:S(2)}, u32[]{:S(2)}) async-start(bf16[32,2,64,128]{3,2,1,0:T(8,128)(2,1)} %shard_map.64), calls=%async_computation | async-start | bytes 2097152 | tf_op jit(solution)/shard_map/all_to_all | solution.py:215
  47.0 7.9 %collective-permute-start = (bf16[1,1,64,128]{3,2,1,0:T(8,128)(2,1)S(1)}, bf16[1,1,64,128]{3,2,1,0:T(8,128)(2,1)S(1)}, u32[]{:S(2)}, u32[]{:S(2)}) collective-permute-start(bf16[1,1,64,128]{3,2,1,0:T(8,128)(2,1)S(1)} %bitcast.153), channel_id=1, source_target_pairs={{0,31},{1,0},{2,1},{3,2},{4,3},{5,4},{6,5},{7,6},{8,7},{9,8},{10,9... | collective-permute-start | bytes 49160 | tf_op jit(solution)/shard_map/ppermute | solution.py:192
  49.9 7.7 %collective-permute-start.1 = (bf16[1,1,64,128]{3,2,1,0:T(8,128)(2,1)S(1)}, bf16[1,1,64,128]{3,2,1,0:T(8,128)(2,1)S(1)}, u32[]{:S(2)}, u32[]{:S(2)}) collective-permute-start(bf16[1,1,64,128]{3,2,1,0:T(8,128)(2,1)S(1)} %bitcast.152), channel_id=1, source_target_pairs={{0,30},{1,31},{2,0},{3,1},{4,2},{5,3},{6,4},{7,5},{8,6},{9,7},{10,... | collective-permute-start | bytes 49160 | tf_op jit(solution)/shard_map/ppermute | solution.py:192
  50.5 7.1 %collective-permute-start.2 = (bf16[1,1,64,128]{3,2,1,0:T(8,128)(2,1)S(1)}, bf16[1,1,64,128]{3,2,1,0:T(8,128)(2,1)S(1)}, u32[]{:S(2)}, u32[]{:S(2)}) collective-permute-start(bf16[1,1,64,128]{3,2,1,0:T(8,128)(2,1)S(1)} %bitcast.150), channel_id=1, source_target_pairs={{0,29},{1,30},{2,31},{3,0},{4,1},{5,2},{6,3},{7,4},{8,5},{9,6},{10... | collective-permute-start | bytes 49160 | tf_op jit(solution)/shard_map/ppermute | solution.py:192
  50.6 8.2 %collective-permute-start.3 = (bf16[1,1,64,128]{3,2,1,0:T(8,128)(2,1)S(1)}, bf16[1,1,64,128]{3,2,1,0:T(8,128)(2,1)S(1)}, u32[]{:S(2)}, u32[]{:S(2)}) collective-permute-start(bf16[1,1,64,128]{3,2,1,0:T(8,128)(2,1)S(1)} %bitcast.149), channel_id=1, source_target_pairs={{0,28},{1,29},{2,30},{3,31},{4,0},{5,1},{6,2},{7,3},{8,4},{9,5},{1... | collective-permute-start | bytes 49160 | tf_op jit(solution)/shard_map/ppermute | solution.py:192
  51.2 9.4 %collective-permute-start.4 = (bf16[1,1,64,128]{3,2,1,0:T(8,128)(2,1)S(1)}, bf16[1,1,64,128]{3,2,1,0:T(8,128)(2,1)S(1)}, u32[]{:S(2)}, u32[]{:S(2)}) collective-permute-start(bf16[1,1,64,128]{3,2,1,0:T(8,128)(2,1)S(1)} %bitcast.147), channel_id=1, source_target_pairs={{0,27},{1,28},{2,29},{3,30},{4,31},{5,0},{6,1},{7,2},{8,3},{9,4},{... | collective-permute-start | bytes 49160 | tf_op jit(solution)/shard_map/ppermute | solution.py:192
  54.5 50.7 %copy-start.3 = (f32[2048]{0:T(1024)S(1)}, f32[2048]{0:T(1024)}, u32[]{:S(2)}) copy-start(f32[2048]{0:T(1024)} %param.11) | copy-start | bytes 24580
  54.8 7.2 %collective-permute-start.5 = (bf16[1,1,64,128]{3,2,1,0:T(8,128)(2,1)S(1)}, bf16[1,1,64,128]{3,2,1,0:T(8,128)(2,1)S(1)}, u32[]{:S(2)}, u32[]{:S(2)}) collective-permute-start(bf16[1,1,64,128]{3,2,1,0:T(8,128)(2,1)S(1)} %bitcast.156), channel_id=1, source_target_pairs={{0,26},{1,27},{2,28},{3,29},{4,30},{5,31},{6,0},{7,1},{8,2},{9,3},... | collective-permute-start | bytes 49160 | tf_op jit(solution)/shard_map/ppermute | solution.py:192
  57.6 6.1 %collective-permute-start.6 = (bf16[1,1,64,128]{3,2,1,0:T(8,128)(2,1)S(1)}, bf16[1,1,64,128]{3,2,1,0:T(8,128)(2,1)S(1)}, u32[]{:S(2)}, u32[]{:S(2)}) collective-permute-start(bf16[1,1,64,128]{3,2,1,0:T(8,128)(2,1)S(1)} %bitcast.155), channel_id=1, source_target_pairs={{0,25},{1,26},{2,27},{3,28},{4,29},{5,30},{6,31},{7,0},{8,1},{9,2}... | collective-permute-start | bytes 49160 | tf_op jit(solution)/shard_map/ppermute | solution.py:192
  57.6 7.5 %collective-permute-start.7 = (bf16[1,1,64,128]{3,2,1,0:T(8,128)(2,1)S(1)}, bf16[1,1,64,128]{3,2,1,0:T(8,128)(2,1)S(1)}, u32[]{:S(2)}, u32[]{:S(2)}) collective-permute-start(bf16[1,1,64,128]{3,2,1,0:T(8,128)(2,1)S(1)} %bitcast.154), channel_id=1, source_target_pairs={{0,24},{1,25},{2,26},{3,27},{4,28},{5,29},{6,30},{7,31},{8,0},{9,1... | collective-permute-start | bytes 49160 | tf_op jit(solution)/shard_map/ppermute | solution.py:192
  58.8 9.5 %collective-permute-start.8 = (bf16[1,1,64,128]{3,2,1,0:T(8,128)(2,1)S(1)}, bf16[1,1,64,128]{3,2,1,0:T(8,128)(2,1)S(1)}, u32[]{:S(2)}, u32[]{:S(2)}) collective-permute-start(bf16[1,1,64,128]{3,2,1,0:T(8,128)(2,1)S(1)} %bitcast.151), channel_id=1, source_target_pairs={{0,23},{1,24},{2,25},{3,26},{4,27},{5,28},{6,29},{7,30},{8,31},{9,... | collective-permute-start | bytes 49160 | tf_op jit(solution)/shard_map/ppermute | solution.py:192
  60.7 11.5 %collective-permute-start.9 = (bf16[1,1,64,128]{3,2,1,0:T(8,128)(2,1)S(1)}, bf16[1,1,64,128]{3,2,1,0:T(8,128)(2,1)S(1)}, u32[]{:S(2)}, u32[]{:S(2)}) collective-permute-start(bf16[1,1,64,128]{3,2,1,0:T(8,128)(2,1)S(1)} %bitcast.148), channel_id=1, source_target_pairs={{0,22},{1,23},{2,24},{3,25},{4,26},{5,27},{6,28},{7,29},{8,30},{9,... | collective-permute-start | bytes 49160 | tf_op jit(solution)/shard_map/ppermute | solution.py:192
  62.0 10.2 %collective-permute-start.10 = (bf16[1,1,64,128]{3,2,1,0:T(8,128)(2,1)S(1)}, bf16[1,1,64,128]{3,2,1,0:T(8,128)(2,1)S(1)}, u32[]{:S(2)}, u32[]{:S(2)}) collective-permute-start(bf16[1,1,64,128]{3,2,1,0:T(8,128)(2,1)S(1)} %bitcast.146), channel_id=1, source_target_pairs={{0,21},{1,22},{2,23},{3,24},{4,25},{5,26},{6,27},{7,28},{8,29},{9,... | collective-permute-start | bytes 49160 | tf_op jit(solution)/shard_map/ppermute | solution.py:192
  63.7 8.8 %collective-permute-start.11 = (bf16[1,1,64,128]{3,2,1,0:T(8,128)(2,1)S(1)}, bf16[1,1,64,128]{3,2,1,0:T(8,128)(2,1)S(1)}, u32[]{:S(2)}, u32[]{:S(2)}) collective-permute-start(bf16[1,1,64,128]{3,2,1,0:T(8,128)(2,1)S(1)} %bitcast.145), channel_id=1, source_target_pairs={{0,20},{1,21},{2,22},{3,23},{4,24},{5,25},{6,26},{7,27},{8,28},{9,... | collective-permute-start | bytes 49160 | tf_op jit(solution)/shard_map/ppermute | solution.py:192
  65.1 10.8 %collective-permute-start.12 = (bf16[1,1,64,128]{3,2,1,0:T(8,128)(2,1)S(1)}, bf16[1,1,64,128]{3,2,1,0:T(8,128)(2,1)S(1)}, u32[]{:S(2)}, u32[]{:S(2)}) collective-permute-start(bf16[1,1,64,128]{3,2,1,0:T(8,128)(2,1)S(1)} %bitcast.144), channel_id=1, source_target_pairs={{0,19},{1,20},{2,21},{3,22},{4,23},{5,24},{6,25},{7,26},{8,27},{9,... | collective-permute-start | bytes 49160 | tf_op jit(solution)/shard_map/ppermute | solution.py:192
  68.3 8.1 %collective-permute-start.13 = (bf16[1,1,64,128]{3,2,1,0:T(8,128)(2,1)S(1)}, bf16[1,1,64,128]{3,2,1,0:T(8,128)(2,1)S(1)}, u32[]{:S(2)}, u32[]{:S(2)}) collective-permute-start(bf16[1,1,64,128]{3,2,1,0:T(8,128)(2,1)S(1)} %bitcast.143), channel_id=1, source_target_pairs={{0,18},{1,19},{2,20},{3,21},{4,22},{5,23},{6,24},{7,25},{8,26},{9,... | collective-permute-start | bytes 49160 | tf_op jit(solution)/shard_map/ppermute | solution.py:192
  72.2 5.1 %collective-permute-start.14 = (bf16[1,1,64,128]{3,2,1,0:T(8,128)(2,1)S(1)}, bf16[1,1,64,128]{3,2,1,0:T(8,128)(2,1)S(1)}, u32[]{:S(2)}, u32[]{:S(2)}) collective-permute-start(bf16[1,1,64,128]{3,2,1,0:T(8,128)(2,1)S(1)} %bitcast.142), channel_id=1, source_target_pairs={{0,17},{1,18},{2,19},{3,20},{4,21},{5,22},{6,23},{7,24},{8,25},{9,... | collective-permute-start | bytes 49160 | tf_op jit(solution)/shard_map/ppermute | solution.py:192
  72.2 8.6 %collective-permute-start.15 = (bf16[1,1,64,128]{3,2,1,0:T(8,128)(2,1)S(1)}, bf16[1,1,64,128]{3,2,1,0:T(8,128)(2,1)S(1)}, u32[]{:S(2)}, u32[]{:S(2)}) collective-permute-start(bf16[1,1,64,128]{3,2,1,0:T(8,128)(2,1)S(1)} %bitcast.141), channel_id=1, source_target_pairs={{0,16},{1,17},{2,18},{3,19},{4,20},{5,21},{6,22},{7,23},{8,24},{9,... | collective-permute-start | bytes 49160 | tf_op jit(solution)/shard_map/ppermute | solution.py:192
  72.5 9.9 %collective-permute-start.16 = (bf16[1,1,64,128]{3,2,1,0:T(8,128)(2,1)S(1)}, bf16[1,1,64,128]{3,2,1,0:T(8,128)(2,1)S(1)}, u32[]{:S(2)}, u32[]{:S(2)}) collective-permute-start(bf16[1,1,64,128]{3,2,1,0:T(8,128)(2,1)S(1)} %bitcast.140), channel_id=1, source_target_pairs={{0,15},{1,16},{2,17},{3,18},{4,19},{5,20},{6,21},{7,22},{8,23},{9,... | collective-permute-start | bytes 49160 | tf_op jit(solution)/shard_map/ppermute | solution.py:192
  75.9 9.7 %collective-permute-start.17 = (bf16[1,1,64,128]{3,2,1,0:T(8,128)(2,1)S(1)}, bf16[1,1,64,128]{3,2,1,0:T(8,128)(2,1)S(1)}, u32[]{:S(2)}, u32[]{:S(2)}) collective-permute-start(bf16[1,1,64,128]{3,2,1,0:T(8,128)(2,1)S(1)} %bitcast.139), channel_id=1, source_target_pairs={{0,14},{1,15},{2,16},{3,17},{4,18},{5,19},{6,20},{7,21},{8,22},{9,... | collective-permute-start | bytes 49160 | tf_op jit(solution)/shard_map/ppermute | solution.py:192
  76.4 9.2 %collective-permute-start.18 = (bf16[1,1,64,128]{3,2,1,0:T(8,128)(2,1)S(1)}, bf16[1,1,64,128]{3,2,1,0:T(8,128)(2,1)S(1)}, u32[]{:S(2)}, u32[]{:S(2)}) collective-permute-start(bf16[1,1,64,128]{3,2,1,0:T(8,128)(2,1)S(1)} %bitcast.138), channel_id=1, source_target_pairs={{0,13},{1,14},{2,15},{3,16},{4,17},{5,18},{6,19},{7,20},{8,21},{9,... | collective-permute-start | bytes 49160 | tf_op jit(solution)/shard_map/ppermute | solution.py:192
  77.4 10.3 %collective-permute-start.19 = (bf16[1,1,64,128]{3,2,1,0:T(8,128)(2,1)S(1)}, bf16[1,1,64,128]{3,2,1,0:T(8,128)(2,1)S(1)}, u32[]{:S(2)}, u32[]{:S(2)}) collective-permute-start(bf16[1,1,64,128]{3,2,1,0:T(8,128)(2,1)S(1)} %bitcast.137), channel_id=1, source_target_pairs={{0,12},{1,13},{2,14},{3,15},{4,16},{5,17},{6,18},{7,19},{8,20},{9,... | collective-permute-start | bytes 49160 | tf_op jit(solution)/shard_map/ppermute | solution.py:192
  80.8 10.7 %collective-permute-start.20 = (bf16[1,1,64,128]{3,2,1,0:T(8,128)(2,1)S(1)}, bf16[1,1,64,128]{3,2,1,0:T(8,128)(2,1)S(1)}, u32[]{:S(2)}, u32[]{:S(2)}) collective-permute-start(bf16[1,1,64,128]{3,2,1,0:T(8,128)(2,1)S(1)} %bitcast.136), channel_id=1, source_target_pairs={{0,11},{1,12},{2,13},{3,14},{4,15},{5,16},{6,17},{7,18},{8,19},{9,... | collective-permute-start | bytes 49160 | tf_op jit(solution)/shard_map/ppermute | solution.py:192
  82.4 9.2 %collective-permute-start.21 = (bf16[1,1,64,128]{3,2,1,0:T(8,128)(2,1)S(1)}, bf16[1,1,64,128]{3,2,1,0:T(8,128)(2,1)S(1)}, u32[]{:S(2)}, u32[]{:S(2)}) collective-permute-start(bf16[1,1,64,128]{3,2,1,0:T(8,128)(2,1)S(1)} %bitcast.135), channel_id=1, source_target_pairs={{0,10},{1,11},{2,12},{3,13},{4,14},{5,15},{6,16},{7,17},{8,18},{9,... | collective-permute-start | bytes 49160 | tf_op jit(solution)/shard_map/ppermute | solution.py:192
  85.6 7.2 %collective-permute-start.22 = (bf16[1,1,64,128]{3,2,1,0:T(8,128)(2,1)S(1)}, bf16[1,1,64,128]{3,2,1,0:T(8,128)(2,1)S(1)}, u32[]{:S(2)}, u32[]{:S(2)}) collective-permute-start(bf16[1,1,64,128]{3,2,1,0:T(8,128)(2,1)S(1)} %bitcast.134), channel_id=1, source_target_pairs={{0,9},{1,10},{2,11},{3,12},{4,13},{5,14},{6,15},{7,16},{8,17},{9,1... | collective-permute-start | bytes 49160 | tf_op jit(solution)/shard_map/ppermute | solution.py:192
  85.6 8.0 %collective-permute-start.23 = (bf16[1,1,64,128]{3,2,1,0:T(8,128)(2,1)S(1)}, bf16[1,1,64,128]{3,2,1,0:T(8,128)(2,1)S(1)}, u32[]{:S(2)}, u32[]{:S(2)}) collective-permute-start(bf16[1,1,64,128]{3,2,1,0:T(8,128)(2,1)S(1)} %bitcast.133), channel_id=1, source_target_pairs={{0,8},{1,9},{2,10},{3,11},{4,12},{5,13},{6,14},{7,15},{8,16},{9,17... | collective-permute-start | bytes 49160 | tf_op jit(solution)/shard_map/ppermute | solution.py:192
  87.7 6.6 %collective-permute-start.24 = (bf16[1,1,64,128]{3,2,1,0:T(8,128)(2,1)S(1)}, bf16[1,1,64,128]{3,2,1,0:T(8,128)(2,1)S(1)}, u32[]{:S(2)}, u32[]{:S(2)}) collective-permute-start(bf16[1,1,64,128]{3,2,1,0:T(8,128)(2,1)S(1)} %bitcast.132), channel_id=1, source_target_pairs={{0,7},{1,8},{2,9},{3,10},{4,11},{5,12},{6,13},{7,14},{8,15},{9,16}... | collective-permute-start | bytes 49160 | tf_op jit(solution)/shard_map/ppermute | solution.py:192
  91.6 6.4 %collective-permute-start.25 = (bf16[1,1,64,128]{3,2,1,0:T(8,128)(2,1)S(1)}, bf16[1,1,64,128]{3,2,1,0:T(8,128)(2,1)S(1)}, u32[]{:S(2)}, u32[]{:S(2)}) collective-permute-start(bf16[1,1,64,128]{3,2,1,0:T(8,128)(2,1)S(1)} %bitcast.131), channel_id=1, source_target_pairs={{0,6},{1,7},{2,8},{3,9},{4,10},{5,11},{6,12},{7,13},{8,14},{9,15},... | collective-permute-start | bytes 49160 | tf_op jit(solution)/shard_map/ppermute | solution.py:192
  91.6 6.4 %collective-permute-start.26 = (bf16[1,1,64,128]{3,2,1,0:T(8,128)(2,1)S(1)}, bf16[1,1,64,128]{3,2,1,0:T(8,128)(2,1)S(1)}, u32[]{:S(2)}, u32[]{:S(2)}) collective-permute-start(bf16[1,1,64,128]{3,2,1,0:T(8,128)(2,1)S(1)} %bitcast.130), channel_id=1, source_target_pairs={{0,5},{1,6},{2,7},{3,8},{4,9},{5,10},{6,11},{7,12},{8,13},{9,14},{... | collective-permute-start | bytes 49160 | tf_op jit(solution)/shard_map/ppermute | solution.py:192
  92.7 6.4 %collective-permute-start.27 = (bf16[1,1,64,128]{3,2,1,0:T(8,128)(2,1)S(1)}, bf16[1,1,64,128]{3,2,1,0:T(8,128)(2,1)S(1)}, u32[]{:S(2)}, u32[]{:S(2)}) collective-permute-start(bf16[1,1,64,128]{3,2,1,0:T(8,128)(2,1)S(1)} %bitcast.129), channel_id=1, source_target_pairs={{0,4},{1,5},{2,6},{3,7},{4,8},{5,9},{6,10},{7,11},{8,12},{9,13},{1... | collective-permute-start | bytes 49160 | tf_op jit(solution)/shard_map/ppermute | solution.py:192
  93.6 6.4 %collective-permute-start.28 = (bf16[1,1,64,128]{3,2,1,0:T(8,128)(2,1)S(1)}, bf16[1,1,64,128]{3,2,1,0:T(8,128)(2,1)S(1)}, u32[]{:S(2)}, u32[]{:S(2)}) collective-permute-start(bf16[1,1,64,128]{3,2,1,0:T(8,128)(2,1)S(1)} %bitcast.128), channel_id=1, source_target_pairs={{0,3},{1,4},{2,5},{3,6},{4,7},{5,8},{6,9},{7,10},{8,11},{9,12},{10... | collective-permute-start | bytes 49160 | tf_op jit(solution)/shard_map/ppermute | solution.py:192
  94.3 8.0 %collective-permute-start.29 = (bf16[1,1,64,128]{3,2,1,0:T(8,128)(2,1)S(1)}, bf16[1,1,64,128]{3,2,1,0:T(8,128)(2,1)S(1)}, u32[]{:S(2)}, u32[]{:S(2)}) collective-permute-start(bf16[1,1,64,128]{3,2,1,0:T(8,128)(2,1)S(1)} %bitcast.127), channel_id=1, source_target_pairs={{0,2},{1,3},{2,4},{3,5},{4,6},{5,7},{6,8},{7,9},{8,10},{9,11},{10,... | collective-permute-start | bytes 49160 | tf_op jit(solution)/shard_map/ppermute | solution.py:192
  98.0 6.8 %collective-permute-start.30 = (bf16[1,1,64,128]{3,2,1,0:T(8,128)(2,1)S(1)}, bf16[1,1,64,128]{3,2,1,0:T(8,128)(2,1)S(1)}, u32[]{:S(2)}, u32[]{:S(2)}) collective-permute-start(bf16[1,1,64,128]{3,2,1,0:T(8,128)(2,1)S(1)} %bitcast.126), channel_id=1, source_target_pairs={{0,1},{1,2},{2,3},{3,4},{4,5},{5,6},{6,7},{7,8},{8,9},{9,10},{10,1... | collective-permute-start | bytes 49160 | tf_op jit(solution)/shard_map/ppermute | solution.py:192

commit v14 on v12

--- a/solution.py
+++ b/solution.py
@@ -84,10 +84,8 @@
     channels = index_ref.shape[1]
     onehot_t = (
         lax.broadcasted_iota(jnp.int32, (groups, channels), 0) == index_ref[...]
-    ).astype(jnp.float32)
-    picked = jnp.dot(
-        filters_ref[...].astype(jnp.float32), onehot_t, preferred_element_type=jnp.float32
-    ).T
+    ).astype(jnp.bfloat16)
+    picked = jnp.dot(filters_ref[...], onehot_t, preferred_element_type=jnp.float32).T
     for dest in range(n_dev):
         for piece in range(pieces):
             low = (dest * pieces + piece) * piece_width

time: 67.8 us -> 67.8 us (level)
  no operation moved by 1% of the time
where the time goes in v14:
time: 67.8 us; the launch traced here: 67.5 us
  waiting for transfers between devices  40.1 us (59%)
  starting transfers between devices  10.9 us (16%)
  matrix products  7.51 us (11%)
  other arithmetic  3.25 us (5%)
  local copies, waits for them, and re-layouts  2.84 us (4%)
  Pallas kernels  2.66 us (4%)
    all_to_all x1, waiting for transfers between devices, by_channels(): lax.all_to_all(sent[piece], ('outer', 'inner'), split_axis=0, concat_axis...  25.4 us
    all_to_all x1, waiting for transfers between devices, by_channels(): lax.all_to_all(jnp.stack(results, axis=1), ('outer', 'inner'), split_axis...  14.7 us
    dot_general x4, matrix products, contract(): jnp.einsum(pattern, left_op, right_op, precision=lax.Precision.HIGH, pref...  7.51 us
    all_to_all x1, starting transfers between devices, by_channels(): lax.all_to_all(sent[piece], ('outer', 'inner'), split_axis=0, concat_axis...  7.3 us
    all_to_all x1, starting transfers between devices, by_channels(): lax.all_to_all(jnp.stack(results, axis=1), ('outer', 'inner'), split_axis...  3.62 us
    pallas_call x1, Pallas kernels, prepare(): pl.pallas_call(prep_kernel, out_shape=tuple((jax.ShapeDtypeStruct((n_dev,...  2.66 us
  transfers between devices with their start and end apart: 2, of which 2 were waited for; matrix products, arithmetic and copies ran while one was open for 2% of the time, Pallas kernels for 0%

profile of v14, /device:TPU:0, one launch (start us, length us, event | category | flops | bytes accessed | tf_op | source)
XLA Modules:
  0.0 67.5 jit_solution(1927136317099098372)
XLA Ops:
  0.0 2.7 %shard_map.64 = bf16[32,2,64,128]{3,2,1,0:T(8,128)(2,1)} custom-call(bf16[128,2048]{1,0:T(8,128)(2,1)} %key_ref.1, bf16[128,2048]{1,0:T(8,128)(2,1)} %value_ref.1, bf16[128,128]{1,0:T(8,128)(2,1)} %filters_ref.1, s32[1,2048]{1,0:T(1,128)} %bitcast.30), custom_call_target="tpu_custom_call" | custom-call | tf_op jit(solution)/shard_map/pallas_call | solution.py:99
  2.7 7.3 %all-to-all-start = ((bf16[32,2,64,128]{3,2,1,0:T(8,128)(2,1)}), bf16[32,2,64,128]{3,2,1,0:T(8,128)(2,1)S(1)}, u32[]{:S(2)}, u32[]{:S(2)}) async-start(bf16[32,2,64,128]{3,2,1,0:T(8,128)(2,1)} %shard_map.64), calls=%async_computation | async-start | bytes 2097152 | tf_op jit(solution)/shard_map/all_to_all | solution.py:195
  10.0 0.1 sine_negate_fusion
  10.1 0.1 fusion.62
  10.2 0.3 fusion.39
  10.4 0.3 broadcast_multiply_fusion
  10.7 0.1 cosine_multiply_fusion
  10.8 25.4 %all-to-all-done = bf16[32,2,64,128]{3,2,1,0:T(8,128)(2,1)S(1)} async-done(((bf16[32,2,64,128]{3,2,1,0:T(8,128)(2,1)}), bf16[32,2,64,128]{3,2,1,0:T(8,128)(2,1)S(1)}, u32[]{:S(2)}, u32[]{:S(2)}) %all-to-all-start) | async-done | bytes 1048608 | tf_op jit(solution)/shard_map/all_to_all | solution.py:195
  36.2 1.6 %fusion.20 = f32[66,128,128]{2,0,1:T(8,128)S(1)} fusion(bf16[32,128,128]{2,1,0:T(8,128)(2,1)S(1)} %bitcast.29, f32[33,32]{0,1:T(8,128)S(1)} %get-tuple-element.13, f32[33,32]{0,1:T(8,128)S(1)} %get-tuple-element.14), kind=kOutput, calls=%fused_computation.23 | convolution fusion | flops 207620160 | bytes 5382400 | tf_op jit(solution)/shard_map/kn,ncb->kcb/dot_general | solution.py:11
  37.8 0.7 %multiply_add_fusion = (f32[33,128,128]{2,0,1:T(8,128)S(1)}, f32[33,128,128]{2,0,1:T(8,128)S(1)}) fusion(f32[66,128,128]{2,0,1:T(8,128)S(1)} %fusion.20, f32[33,128]{1,0:T(8,128)S(1)} %get-tuple-element.15, f32[33,128]{1,0:T(8,128)S(1)} %get-tuple-element.16), kind=kLoop, calls=%fused_computation.4 | loop fusion | flops 3244032 | bytes 8684544 | tf_op jit(solution)/shard_map/add | solution.py:38
  38.5 0.3 pad_maximum_fusion
  38.9 3.0 %fusion = f32[33,128,256]{2,1,0:T(8,128)S(1)} fusion(f32[33,128,256]{2,0,1:T(8,128)S(1)} %pad_maximum_fusion, f32[128,128]{1,0:T(8,128)S(1)} %fusion.39, f32[128,128]{1,0:T(8,128)S(1)} %get-tuple-element.18, f32[128,128]{1,0:T(8,128)S(1)} %get-tuple-element.17), kind=kOutput, calls=%fused_computation.1 | convolution fusion | flops 1661140992 | bytes 8847360 | tf_op jit(solution)/shard_map/kcb,bq->kcq/dot_general | solution.py:11
  41.9 0.3 multiply_subtract_fusion.2
  42.2 1.0 %fusion.4 = f32[33,64,256]{2,1,0:T(8,128)S(1)} fusion(f32[33,64,128]{2,1,0:T(8,128)S(1)} %get-tuple-element.8, f32[33,64,128]{2,1,0:T(8,128)S(1)} %get-tuple-element.7, f32[128,128]{1,0:T(8,128)S(1)} %fusion.39, f32[128,128]{1,0:T(8,128)S(1)} %get-tuple-element.17, f32[128,128]{1,0:T(8,128)S(1)} %get-tuple-element.18), kind=kOutput, calls=%fused_computation.7 | convolution fusion | flops 831209472 | bytes 4521984 | tf_op jit(solution)/shard_map/kcq,qb->kcb/dot_general | solution.py:11
  43.3 0.3 multiply_subtract_fusion.1
  43.6 0.2 pad_maximum_fusion.1
  43.9 0.0 copy-start
  43.9 1.9 %fusion.14 = bf16[32,1,64,128]{3,0,2,1:T(8,128)(2,1)S(1)} fusion(f32[66,64,128]{2,1,0:T(8,128)S(1)} %pad_maximum_fusion.1, f32[32,33]{1,0:T(8,128)S(1)} %get-tuple-element.12, f32[32,33]{1,0:T(8,128)S(1)} %get-tuple-element.11), kind=kOutput, calls=%fused_computation.14 | convolution fusion | flops 104335424 | bytes 2695424 | tf_op jit(solution)/shard_map/nk,kcb->ncb/dot_general | solution.py:11
  45.8 0.0 copy-start.1
  45.8 0.0 copy-start.2
  45.8 1.0 %copy.22 = bf16[32,1,64,128]{3,2,1,0:T(8,128)(2,1)} copy(bf16[32,1,64,128]{3,0,2,1:T(8,128)(2,1)S(1)} %fusion.14) | data formatting | bytes 1048576 | tf_op jit(solution)/shard_map/stack | solution.py:207
  46.8 0.0 copy-start.3
  46.8 3.6 %all-to-all-start.1 = ((bf16[32,1,64,128]{3,2,1,0:T(8,128)(2,1)}), bf16[32,1,64,128]{3,2,1,0:T(8,128)(2,1)S(1)}, u32[]{:S(2)}, u32[]{:S(2)}) async-start(bf16[32,1,64,128]{3,2,1,0:T(8,128)(2,1)} %copy.22), calls=%async_computation.1 | async-start | bytes 1048576 | tf_op jit(solution)/shard_map/all_to_all | solution.py:206
  50.4 0.0 copy-done
  50.4 0.3 copy.24
  50.7 0.0 copy-done.1
  50.7 0.3 copy.25
  51.0 0.0 copy-done.2
  51.0 0.3 copy.18
  51.3 14.7 %all-to-all-done.1 = bf16[32,1,64,128]{3,2,1,0:T(8,128)(2,1)S(1)} async-done(((bf16[32,1,64,128]{3,2,1,0:T(8,128)(2,1)}), bf16[32,1,64,128]{3,2,1,0:T(8,128)(2,1)S(1)}, u32[]{:S(2)}, u32[]{:S(2)}) %all-to-all-start.1) | async-done | bytes 524320 | tf_op jit(solution)/shard_map/all_to_all | solution.py:206
  66.0 0.0 copy-done.3
  66.0 0.5 fusion.19
  66.5 1.0 %copy.26 = bf16[128,2048]{1,0:T(8,128)(2,1)} copy(bf16[128,2048]{0,1:T(8,128)(2,1)S(1)} %fusion.19) | data formatting | bytes 1048576 | tf_op jit(solution)/shard_map/convert_element_type | solution.py:216
  (1 shorter events, 0.0 us)
Async XLA Ops:
  2.7 33.5 %all-to-all-start = ((bf16[32,2,64,128]{3,2,1,0:T(8,128)(2,1)}), bf16[32,2,64,128]{3,2,1,0:T(8,128)(2,1)S(1)}, u32[]{:S(2)}, u32[]{:S(2)}) async-start(bf16[32,2,64,128]{3,2,1,0:T(8,128)(2,1)} %shard_map.64), calls=%async_computation | async-start | bytes 2097152 | tf_op jit(solution)/shard_map/all_to_all | solution.py:195
  43.9 6.6 %copy-start = (bf16[128,2048]{1,0:T(8,128)(2,1)S(1)}, bf16[128,2048]{1,0:T(8,128)(2,1)}, u32[]{:S(2)}) copy-start(bf16[128,2048]{1,0:T(8,128)(2,1)} %key_ref.1) | copy-start | bytes 1572868
  45.8 4.9 %copy-start.1 = (bf16[128,2048]{1,0:T(8,128)(2,1)S(1)}, bf16[128,2048]{1,0:T(8,128)(2,1)}, u32[]{:S(2)}) copy-start(bf16[128,2048]{1,0:T(8,128)(2,1)} %value_ref.1) | copy-start | bytes 1572868
  45.8 5.2 %copy-start.2 = (bf16[128,2048]{1,0:T(8,128)(2,1)S(1)}, bf16[128,2048]{1,0:T(8,128)(2,1)}, u32[]{:S(2)}) copy-start(bf16[128,2048]{1,0:T(8,128)(2,1)} %param.6) | copy-start | bytes 1572868
  46.8 19.2 %copy-start.3 = (f32[2048]{0:T(1024)S(1)}, f32[2048]{0:T(1024)}, u32[]{:S(2)}) copy-start(f32[2048]{0:T(1024)} %param.11) | copy-start | bytes 24580
  46.8 19.2 %all-to-all-start.1 = ((bf16[32,1,64,128]{3,2,1,0:T(8,128)(2,1)}), bf16[32,1,64,128]{3,2,1,0:T(8,128)(2,1)S(1)}, u32[]{:S(2)}, u32[]{:S(2)}) async-start(bf16[32,1,64,128]{3,2,1,0:T(8,128)(2,1)} %copy.22), calls=%async_computation.1 | async-start | bytes 1048576 | tf_op jit(solution)/shard_map/all_to_all | solution.py:206

commit v15 on v14

--- a/solution.py
+++ b/solution.py
@@ -133,14 +133,16 @@
     )
 
 
-def convolve_block(got, n_dev, row_count):
+def convolve_block(got, n_dev, row_count, order):
     own_width = got.shape[2]
     size_a = 2 * n_dev
     kept = n_dev + 1
     padded = size_a * row_count
     stacked = got.reshape(n_dev, 2 * own_width, row_count).astype(jnp.float32)
     first_cos, first_sin = dft_table(kept, n_dev, size_a)
-    first = contract("kn,ncb->kcb", jnp.concatenate([first_cos, -first_sin], axis=0), stacked)
+    first = contract(
+        "kn,ncb->kcb", jnp.concatenate([first_cos, -first_sin], axis=0)[:, order], stacked
+    )
     twiddle = angles_of(
         jnp.arange(kept, dtype=jnp.int32)[:, None]
         * jnp.arange(row_count, dtype=jnp.int32)[None, :],
@@ -170,7 +172,7 @@
     weight = jnp.where((index == 0) | (index == n_dev), 1.0, 2.0).astype(jnp.float32)[None, :]
     outcome = contract(
         "nk,kcb->ncb",
-        jnp.concatenate([back_cos * weight, -back_sin * weight], axis=1),
+        jnp.concatenate([back_cos * weight, -back_sin * weight], axis=1)[order],
         jnp.concatenate([real_part, imag_part], axis=0),
     )
     return (outcome * (1.0 / padded)).astype(jnp.bfloat16)
@@ -191,8 +193,10 @@
             2, n_dev, pieces, piece_width, row_count
         )
         sent = sent.transpose(2, 1, 0, 3, 4)
+    axes = ("inner", "outer")
+    order = jnp.arange(n_dev).reshape(lax.axis_size("outer"), lax.axis_size("inner")).T.reshape(-1)
     arrived = [
-        lax.all_to_all(sent[piece], ("outer", "inner"), split_axis=0, concat_axis=0, tiled=True)
+        lax.all_to_all(sent[piece], axes, split_axis=0, concat_axis=0, tiled=True)
         for piece in range(pieces)
     ]
     results = []
@@ -201,10 +205,10 @@
         got = arrived[piece]
         if outcome is not None:
             outcome, got = lax.optimization_barrier((outcome, got))
-        outcome = convolve_block(got, n_dev, row_count)
+        outcome = convolve_block(got, n_dev, row_count, order)
         results.append(outcome)
     returned = lax.all_to_all(
-        jnp.stack(results, axis=1), ("outer", "inner"), split_axis=0, concat_axis=0, tiled=True
+        jnp.stack(results, axis=1), axes, split_axis=0, concat_axis=0, tiled=True
     )
     return returned.reshape(channels, row_count)
 

time: 67.8 us -> 69 us (1.018)
  local copies, waits for them, and re-layouts: 2.84 us -> 4.08 us
  starting transfers between devices: 10.9 us -> 10 us
  waiting for transfers between devices: 40.1 us -> 40.8 us
    gather x0 -> x2, local copies, waits for them, and re-layouts: none -> 1.16 us  [the longest x1 0.58 us: convolve_block(): jnp.concatenate([first_cos, -first_sin], axis=0)[:, order]]
    all_to_all x2, starting transfers between devices: 10.9 us -> 10 us  [the longest x1 7.3 us: by_channels(): lax.all_to_all(sent[piece], axes, split_axis=0, concat_axis=0, tiled=True)]
    all_to_all x2, waiting for transfers between devices: 40.1 us -> 40.8 us  [the longest x1 25.3 us: by_channels(): lax.all_to_all(sent[piece], axes, split_axis=0, concat_axis=0, tiled=True)]
  transfers between devices with their start and end apart: 2 -> 2, of which waited for: 2 -> 2; matrix products, arithmetic and copies ran while one was open for 2% -> 4% of each run, Pallas kernels for 0% -> 0%
where the time goes in v15:
time: 69 us; the launch traced here: 68.7 us
  waiting for transfers between devices  40.8 us (59%)
  starting transfers between devices  10 us (14%)
  matrix products  7.44 us (11%)
  local copies, waits for them, and re-layouts  4.08 us (6%)
  other arithmetic  3.43 us (5%)
  Pallas kernels  2.66 us (4%)
    all_to_all x1, waiting for transfers between devices, by_channels(): lax.all_to_all(sent[piece], axes, split_axis=0, concat_axis=0, tiled=True)  25.3 us
    all_to_all x1, waiting for transfers between devices, by_channels(): lax.all_to_all(jnp.stack(results, axis=1), axes, split_axis=0, concat_axi...  15.5 us
    dot_general x4, matrix products, contract(): jnp.einsum(pattern, left_op, right_op, precision=lax.Precision.HIGH, pref...  7.44 us
    all_to_all x1, starting transfers between devices, by_channels(): lax.all_to_all(sent[piece], axes, split_axis=0, concat_axis=0, tiled=True)  7.3 us
    all_to_all x1, starting transfers between devices, by_channels(): lax.all_to_all(jnp.stack(results, axis=1), axes, split_axis=0, concat_axi...  2.74 us
    pallas_call x1, Pallas kernels, prepare(): pl.pallas_call(prep_kernel, out_shape=tuple((jax.ShapeDtypeStruct((n_dev,...  2.66 us
  transfers between devices with their start and end apart: 2, of which 2 were waited for; matrix products, arithmetic and copies ran while one was open for 4% of the time, Pallas kernels for 0%

profile of v15, /device:TPU:0, one launch (start us, length us, event | category | flops | bytes accessed | tf_op | source)
XLA Modules:
  0.0 68.7 jit_solution(1903131653468649084)
XLA Ops:
  0.0 2.7 %shard_map.64 = bf16[32,2,64,128]{3,2,1,0:T(8,128)(2,1)} custom-call(bf16[128,2048]{1,0:T(8,128)(2,1)} %key_ref.1, bf16[128,2048]{1,0:T(8,128)(2,1)} %value_ref.1, bf16[128,128]{1,0:T(8,128)(2,1)} %filters_ref.1, s32[1,2048]{1,0:T(1,128)} %bitcast.32), custom_call_target="tpu_custom_call" | custom-call | tf_op jit(solution)/shard_map/pallas_call | solution.py:99
  2.7 7.3 %all-to-all-start = ((bf16[32,2,64,128]{3,2,1,0:T(8,128)(2,1)}), bf16[32,2,64,128]{3,2,1,0:T(8,128)(2,1)S(1)}, u32[]{:S(2)}, u32[]{:S(2)}) async-start(bf16[32,2,64,128]{3,2,1,0:T(8,128)(2,1)} %shard_map.64), calls=%async_computation | async-start | bytes 2097152 | tf_op jit(solution)/shard_map/all_to_all | solution.py:199
  10.0 0.1 reshape.107
  10.1 0.1 sine_negate_fusion
  10.2 0.1 pad_maximum_fusion.9
  10.2 0.6 gather_fusion.1
  10.8 0.1 cosine_multiply_fusion
  10.9 0.1 pad_maximum_fusion.8
  11.0 0.6 gather_fusion
  11.6 0.1 fusion.60
  11.7 0.3 fusion.39
  11.9 0.3 broadcast_multiply_fusion
  12.2 25.3 %all-to-all-done = bf16[32,2,64,128]{3,2,1,0:T(8,128)(2,1)S(1)} async-done(((bf16[32,2,64,128]{3,2,1,0:T(8,128)(2,1)}), bf16[32,2,64,128]{3,2,1,0:T(8,128)(2,1)S(1)}, u32[]{:S(2)}, u32[]{:S(2)}) %all-to-all-start) | async-done | bytes 1048608 | tf_op jit(solution)/shard_map/all_to_all | solution.py:199
  37.6 1.5 %fusion.20 = f32[66,128,128]{2,0,1:T(8,128)S(1)} fusion(bf16[32,128,128]{2,1,0:T(8,128)(2,1)S(1)} %bitcast.31, f32[32,66]{1,0:T(8,128)S(1)} %gather_fusion.1), kind=kOutput, calls=%fused_computation.25 | convolution fusion | flops 207618048 | bytes 5382400 | tf_op jit(solution)/shard_map/kn,ncb->kcb/dot_general | solution.py:11
  39.1 0.7 %multiply_add_fusion = (f32[33,128,128]{2,0,1:T(8,128)S(1)}, f32[33,128,128]{2,0,1:T(8,128)S(1)}) fusion(f32[66,128,128]{2,0,1:T(8,128)S(1)} %fusion.20, f32[33,128]{1,0:T(8,128)S(1)} %get-tuple-element.15, f32[33,128]{1,0:T(8,128)S(1)} %get-tuple-element.16), kind=kLoop, calls=%fused_computation.6 | loop fusion | flops 3244032 | bytes 8684544 | tf_op jit(solution)/shard_map/add | solution.py:38
  39.8 0.3 pad_maximum_fusion
  40.2 3.0 %fusion = f32[33,128,256]{2,1,0:T(8,128)S(1)} fusion(f32[33,128,256]{2,0,1:T(8,128)S(1)} %pad_maximum_fusion, f32[128,128]{1,0:T(8,128)S(1)} %fusion.39, f32[128,128]{1,0:T(8,128)S(1)} %get-tuple-element.18, f32[128,128]{1,0:T(8,128)S(1)} %get-tuple-element.17), kind=kOutput, calls=%fused_computation.3 | convolution fusion | flops 1661140992 | bytes 8847360 | tf_op jit(solution)/shard_map/kcb,bq->kcq/dot_general | solution.py:11
  43.1 0.3 multiply_subtract_fusion.2
  43.5 1.1 %fusion.4 = f32[33,64,256]{2,1,0:T(8,128)S(1)} fusion(f32[33,64,128]{2,1,0:T(8,128)S(1)} %get-tuple-element.8, f32[33,64,128]{2,1,0:T(8,128)S(1)} %get-tuple-element.7, f32[128,128]{1,0:T(8,128)S(1)} %fusion.39, f32[128,128]{1,0:T(8,128)S(1)} %get-tuple-element.17, f32[128,128]{1,0:T(8,128)S(1)} %get-tuple-element.18), kind=kOutput, calls=%fused_computation.9 | convolution fusion | flops 831209472 | bytes 4521984 | tf_op jit(solution)/shard_map/kcq,qb->kcb/dot_general | solution.py:11
  44.6 0.3 multiply_subtract_fusion.1
  44.9 0.2 pad_maximum_fusion.1
  45.2 0.0 copy-start
  45.2 1.9 %fusion.14 = bf16[32,1,64,128]{3,0,2,1:T(8,128)(2,1)S(1)} fusion(f32[66,64,128]{2,1,0:T(8,128)S(1)} %pad_maximum_fusion.1, f32[32,66]{1,0:T(8,128)S(1)} %gather_fusion), kind=kOutput, calls=%fused_computation.16 | convolution fusion | flops 104333312 | bytes 2695424 | tf_op jit(solution)/shard_map/nk,kcb->ncb/dot_general | solution.py:11
  47.1 0.0 copy-start.1
  47.1 0.0 copy-start.2
  47.1 1.0 %copy.22 = bf16[32,1,64,128]{3,2,1,0:T(8,128)(2,1)} copy(bf16[32,1,64,128]{3,0,2,1:T(8,128)(2,1)S(1)} %fusion.14) | data formatting | bytes 1048576 | tf_op jit(solution)/shard_map/stack | solution.py:211
  48.1 0.0 copy-start.3
  48.1 2.7 %all-to-all-start.1 = ((bf16[32,1,64,128]{3,2,1,0:T(8,128)(2,1)}), bf16[32,1,64,128]{3,2,1,0:T(8,128)(2,1)S(1)}, u32[]{:S(2)}, u32[]{:S(2)}) async-start(bf16[32,1,64,128]{3,2,1,0:T(8,128)(2,1)} %copy.22), calls=%async_computation.1 | async-start | bytes 1048576 | tf_op jit(solution)/shard_map/all_to_all | solution.py:210
  50.8 0.0 copy-done
  50.8 0.3 copy.24
  51.1 0.0 copy-done.1
  51.1 0.3 copy.25
  51.4 0.0 copy-done.2
  51.4 0.3 copy.18
  51.7 15.5 %all-to-all-done.1 = bf16[32,1,64,128]{3,2,1,0:T(8,128)(2,1)S(1)} async-done(((bf16[32,1,64,128]{3,2,1,0:T(8,128)(2,1)}), bf16[32,1,64,128]{3,2,1,0:T(8,128)(2,1)S(1)}, u32[]{:S(2)}, u32[]{:S(2)}) %all-to-all-start.1) | async-done | bytes 524320 | tf_op jit(solution)/shard_map/all_to_all | solution.py:210
  67.2 0.0 copy-done.3
  67.2 0.5 fusion.19
  67.7 1.0 %copy.26 = bf16[128,2048]{1,0:T(8,128)(2,1)} copy(bf16[128,2048]{0,1:T(8,128)(2,1)S(1)} %fusion.19) | data formatting | bytes 1048576 | tf_op jit(solution)/shard_map/convert_element_type | solution.py:220
  (4 shorter events, 0.0 us)
Async XLA Ops:
  2.7 34.9 %all-to-all-start = ((bf16[32,2,64,128]{3,2,1,0:T(8,128)(2,1)}), bf16[32,2,64,128]{3,2,1,0:T(8,128)(2,1)S(1)}, u32[]{:S(2)}, u32[]{:S(2)}) async-start(bf16[32,2,64,128]{3,2,1,0:T(8,128)(2,1)} %shard_map.64), calls=%async_computation | async-start | bytes 2097152 | tf_op jit(solution)/shard_map/all_to_all | solution.py:199
  45.2 5.7 %copy-start = (bf16[128,2048]{1,0:T(8,128)(2,1)S(1)}, bf16[128,2048]{1,0:T(8,128)(2,1)}, u32[]{:S(2)}) copy-start(bf16[128,2048]{1,0:T(8,128)(2,1)} %key_ref.1) | copy-start | bytes 1572868
  47.1 4.1 %copy-start.1 = (bf16[128,2048]{1,0:T(8,128)(2,1)S(1)}, bf16[128,2048]{1,0:T(8,128)(2,1)}, u32[]{:S(2)}) copy-start(bf16[128,2048]{1,0:T(8,128)(2,1)} %value_ref.1) | copy-start | bytes 1572868
  47.1 4.3 %copy-start.2 = (bf16[128,2048]{1,0:T(8,128)(2,1)S(1)}, bf16[128,2048]{1,0:T(8,128)(2,1)}, u32[]{:S(2)}) copy-start(bf16[128,2048]{1,0:T(8,128)(2,1)} %param.6) | copy-start | bytes 1572868
  48.1 19.1 %copy-start.3 = (f32[2048]{0:T(1024)S(1)}, f32[2048]{0:T(1024)}, u32[]{:S(2)}) copy-start(f32[2048]{0:T(1024)} %param.11) | copy-start | bytes 24580
  48.1 19.1 %all-to-all-start.1 = ((bf16[32,1,64,128]{3,2,1,0:T(8,128)(2,1)}), bf16[32,1,64,128]{3,2,1,0:T(8,128)(2,1)S(1)}, u32[]{:S(2)}, u32[]{:S(2)}) async-start(bf16[32,1,64,128]{3,2,1,0:T(8,128)(2,1)} %copy.22), calls=%async_computation.1 | async-start | bytes 1048576 | tf_op jit(solution)/shard_map/all_to_all | solution.py:210

commit v16 on v14

--- a/solution.py
+++ b/solution.py
@@ -138,9 +138,17 @@
     size_a = 2 * n_dev
     kept = n_dev + 1
     padded = size_a * row_count
-    stacked = got.reshape(n_dev, 2 * own_width, row_count).astype(jnp.float32)
+    stacked = got.reshape(n_dev, 2 * own_width, row_count)
     first_cos, first_sin = dft_table(kept, n_dev, size_a)
-    first = contract("kn,ncb->kcb", jnp.concatenate([first_cos, -first_sin], axis=0), stacked)
+    first_table = jnp.concatenate([first_cos, -first_sin], axis=0)
+    table_high = first_table.astype(jnp.bfloat16)
+    table_low = (first_table - table_high.astype(jnp.float32)).astype(jnp.bfloat16)
+    first = jnp.einsum(
+        "kn,ncb->kcb",
+        jnp.concatenate([table_high, table_low], axis=1),
+        jnp.concatenate([stacked, stacked], axis=0),
+        preferred_element_type=jnp.float32,
+    )
     twiddle = angles_of(
         jnp.arange(kept, dtype=jnp.int32)[:, None]
         * jnp.arange(row_count, dtype=jnp.int32)[None, :],

time: 67.8 us -> 67.6 us (level)
  matrix products: 7.51 us -> 6.7 us
  local copies, waits for them, and re-layouts: 2.84 us -> 3.52 us
    dot_general x4 -> x3, matrix products: 7.51 us -> 5.91 us  [contract(): jnp.einsum(pattern, left_op, right_op, precision=lax.Precision.HIGH, pref...]
    dot_general x0 -> x1, matrix products: none -> 0.79 us  [convolve_block(): jnp.einsum('kn,ncb->kcb', jnp.concatenate([table_high, table_low], axis=1...]
    reshape x0 -> x1, local copies, waits for them, and re-layouts: none -> 0.68 us  [convolve_block(): stacked = got.reshape(n_dev, 2 * own_width, row_count)]
  transfers between devices with their start and end apart: 2 -> 2, of which waited for: 2 -> 2; matrix products, arithmetic and copies ran while one was open for 2% -> 3% of each run, Pallas kernels for 0% -> 0%
where the time goes in v16:
time: 67.6 us; the launch traced here: 67.3 us
  waiting for transfers between devices  39.9 us (59%)
  starting transfers between devices  10.9 us (16%)
  matrix products  6.7 us (10%)
  local copies, waits for them, and re-layouts  3.52 us (5%)
  other arithmetic  3.41 us (5%)
  Pallas kernels  2.66 us (4%)
    all_to_all x1, waiting for transfers between devices, by_channels(): lax.all_to_all(sent[piece], ('outer', 'inner'), split_axis=0, concat_axis...  25.3 us
    all_to_all x1, waiting for transfers between devices, by_channels(): lax.all_to_all(jnp.stack(results, axis=1), ('outer', 'inner'), split_axis...  14.7 us
    all_to_all x1, starting transfers between devices, by_channels(): lax.all_to_all(sent[piece], ('outer', 'inner'), split_axis=0, concat_axis...  7.3 us
    dot_general x3, matrix products, contract(): jnp.einsum(pattern, left_op, right_op, precision=lax.Precision.HIGH, pref...  5.91 us
    all_to_all x1, starting transfers between devices, by_channels(): lax.all_to_all(jnp.stack(results, axis=1), ('outer', 'inner'), split_axis...  3.62 us
    pallas_call x1, Pallas kernels, prepare(): pl.pallas_call(prep_kernel, out_shape=tuple((jax.ShapeDtypeStruct((n_dev,...  2.66 us
  transfers between devices with their start and end apart: 2, of which 2 were waited for; matrix products, arithmetic and copies ran while one was open for 3% of the time, Pallas kernels for 0%

profile of v16, /device:TPU:0, one launch (start us, length us, event | category | flops | bytes accessed | tf_op | source)
XLA Modules:
  0.0 67.3 jit_solution(1411397814198780968)
XLA Ops:
  0.0 2.7 %shard_map.64 = bf16[32,2,64,128]{3,2,1,0:T(8,128)(2,1)} custom-call(bf16[128,2048]{1,0:T(8,128)(2,1)} %key_ref.1, bf16[128,2048]{1,0:T(8,128)(2,1)} %value_ref.1, bf16[128,128]{1,0:T(8,128)(2,1)} %filters_ref.1, s32[1,2048]{1,0:T(1,128)} %bitcast.30), custom_call_target="tpu_custom_call" | custom-call | tf_op jit(solution)/shard_map/pallas_call | solution.py:99
  2.7 7.3 %all-to-all-start = ((bf16[32,2,64,128]{3,2,1,0:T(8,128)(2,1)}), bf16[32,2,64,128]{3,2,1,0:T(8,128)(2,1)S(1)}, u32[]{:S(2)}, u32[]{:S(2)}) async-start(bf16[32,2,64,128]{3,2,1,0:T(8,128)(2,1)} %shard_map.64), calls=%async_computation | async-start | bytes 2097152 | tf_op jit(solution)/shard_map/all_to_all | solution.py:203
  10.0 0.1 sine_negate_fusion
  10.1 0.1 fusion.67
  10.1 0.1 subtract_convert_fusion
  10.2 0.1 fusion.64
  10.3 0.3 fusion.41
  10.6 0.3 broadcast_multiply_fusion
  10.9 0.1 cosine_multiply_fusion
  10.9 25.3 %all-to-all-done = bf16[32,2,64,128]{3,2,1,0:T(8,128)(2,1)S(1)} async-done(((bf16[32,2,64,128]{3,2,1,0:T(8,128)(2,1)}), bf16[32,2,64,128]{3,2,1,0:T(8,128)(2,1)S(1)}, u32[]{:S(2)}, u32[]{:S(2)}) %all-to-all-start) | async-done | bytes 1048608 | tf_op jit(solution)/shard_map/all_to_all | solution.py:203
  36.2 0.7 %copy.21 = bf16[32,128,128]{2,0,1:T(8,128)(2,1)S(1)} copy(bf16[32,128,128]{2,1,0:T(8,128)(2,1)S(1)} %bitcast.29) | data formatting | bytes 2097152 | tf_op jit(solution)/shard_map/reshape | solution.py:141
  36.9 0.8 %fusion.8 = f32[66,128,128]{2,0,1:T(8,128)S(1)} fusion(bf16[32,128,128]{2,0,1:T(8,128)(2,1)S(1)} %copy.21, bf16[66,32]{0,1:T(8,128)(2,1)S(1)} %subtract_convert_fusion, bf16[66,32]{0,1:T(8,128)(2,1)S(1)} %fusion.67), kind=kOutput, calls=%fused_computation.12 | convolution fusion | flops 142623232 | bytes 5382400 | tf_op jit(solution)/shard_map/kn,ncb->kcb/dot_general | solution.py:146
  37.7 0.7 %multiply_add_fusion = (f32[33,128,128]{2,0,1:T(8,128)S(1)}, f32[33,128,128]{2,0,1:T(8,128)S(1)}) fusion(f32[66,128,128]{2,0,1:T(8,128)S(1)} %fusion.8, f32[33,128]{1,0:T(8,128)S(1)} %get-tuple-element.15, f32[33,128]{1,0:T(8,128)S(1)} %get-tuple-element.16), kind=kLoop, calls=%fused_computation.4 | loop fusion | flops 3244032 | bytes 8684544 | tf_op jit(solution)/shard_map/add | solution.py:38
  38.4 0.3 pad_maximum_fusion
  38.8 3.0 %fusion = f32[33,128,256]{2,1,0:T(8,128)S(1)} fusion(f32[33,128,256]{2,0,1:T(8,128)S(1)} %pad_maximum_fusion, f32[128,128]{1,0:T(8,128)S(1)} %fusion.41, f32[128,128]{1,0:T(8,128)S(1)} %get-tuple-element.18, f32[128,128]{1,0:T(8,128)S(1)} %get-tuple-element.17), kind=kOutput, calls=%fused_computation.1 | convolution fusion | flops 1661140992 | bytes 8847360 | tf_op jit(solution)/shard_map/kcb,bq->kcq/dot_general | solution.py:11
  41.7 0.3 multiply_subtract_fusion.2
  42.1 1.0 %fusion.4 = f32[33,64,256]{2,1,0:T(8,128)S(1)} fusion(f32[33,64,128]{2,1,0:T(8,128)S(1)} %get-tuple-element.8, f32[33,64,128]{2,1,0:T(8,128)S(1)} %get-tuple-element.7, f32[128,128]{1,0:T(8,128)S(1)} %fusion.41, f32[128,128]{1,0:T(8,128)S(1)} %get-tuple-element.17, f32[128,128]{1,0:T(8,128)S(1)} %get-tuple-element.18), kind=kOutput, calls=%fused_computation.7 | convolution fusion | flops 831209472 | bytes 4521984 | tf_op jit(solution)/shard_map/kcq,qb->kcb/dot_general | solution.py:11
  43.1 0.3 multiply_subtract_fusion.1
  43.5 0.2 pad_maximum_fusion.1
  43.7 0.0 copy-start
  43.7 1.9 %fusion.18 = bf16[32,1,64,128]{3,0,2,1:T(8,128)(2,1)S(1)} fusion(f32[66,64,128]{2,1,0:T(8,128)S(1)} %pad_maximum_fusion.1, f32[32,33]{1,0:T(8,128)S(1)} %get-tuple-element.12, f32[32,33]{1,0:T(8,128)S(1)} %get-tuple-element.11), kind=kOutput, calls=%fused_computation.18 | convolution fusion | flops 104335424 | bytes 2695424 | tf_op jit(solution)/shard_map/nk,kcb->ncb/dot_general | solution.py:11
  45.6 0.0 copy-start.1
  45.7 0.0 copy-start.2
  45.7 1.0 %copy.25 = bf16[32,1,64,128]{3,2,1,0:T(8,128)(2,1)} copy(bf16[32,1,64,128]{3,0,2,1:T(8,128)(2,1)S(1)} %fusion.18) | data formatting | bytes 1048576 | tf_op jit(solution)/shard_map/stack | solution.py:215
  46.7 0.0 copy-start.3
  46.7 3.6 %all-to-all-start.1 = ((bf16[32,1,64,128]{3,2,1,0:T(8,128)(2,1)}), bf16[32,1,64,128]{3,2,1,0:T(8,128)(2,1)S(1)}, u32[]{:S(2)}, u32[]{:S(2)}) async-start(bf16[32,1,64,128]{3,2,1,0:T(8,128)(2,1)} %copy.25), calls=%async_computation.1 | async-start | bytes 1048576 | tf_op jit(solution)/shard_map/all_to_all | solution.py:214
  50.3 0.0 copy-done
  50.3 0.3 copy.27
  50.6 0.0 copy-done.1
  50.6 0.3 copy.28
  50.9 0.0 copy-done.2
  50.9 0.3 copy.20
  51.2 14.7 %all-to-all-done.1 = bf16[32,1,64,128]{3,2,1,0:T(8,128)(2,1)S(1)} async-done(((bf16[32,1,64,128]{3,2,1,0:T(8,128)(2,1)}), bf16[32,1,64,128]{3,2,1,0:T(8,128)(2,1)S(1)}, u32[]{:S(2)}, u32[]{:S(2)}) %all-to-all-start.1) | async-done | bytes 524320 | tf_op jit(solution)/shard_map/all_to_all | solution.py:214
  65.8 0.0 copy-done.3
  65.8 0.5 fusion.23
  66.3 1.0 %copy.29 = bf16[128,2048]{1,0:T(8,128)(2,1)} copy(bf16[128,2048]{0,1:T(8,128)(2,1)S(1)} %fusion.23) | data formatting | bytes 1048576 | tf_op jit(solution)/shard_map/convert_element_type | solution.py:224
  (1 shorter events, 0.0 us)
Async XLA Ops:
  2.7 33.5 %all-to-all-start = ((bf16[32,2,64,128]{3,2,1,0:T(8,128)(2,1)}), bf16[32,2,64,128]{3,2,1,0:T(8,128)(2,1)S(1)}, u32[]{:S(2)}, u32[]{:S(2)}) async-start(bf16[32,2,64,128]{3,2,1,0:T(8,128)(2,1)} %shard_map.64), calls=%async_computation | async-start | bytes 2097152 | tf_op jit(solution)/shard_map/all_to_all | solution.py:203
  43.7 6.6 %copy-start = (bf16[128,2048]{1,0:T(8,128)(2,1)S(1)}, bf16[128,2048]{1,0:T(8,128)(2,1)}, u32[]{:S(2)}) copy-start(bf16[128,2048]{1,0:T(8,128)(2,1)} %key_ref.1) | copy-start | bytes 1572868
  45.6 4.9 %copy-start.1 = (bf16[128,2048]{1,0:T(8,128)(2,1)S(1)}, bf16[128,2048]{1,0:T(8,128)(2,1)}, u32[]{:S(2)}) copy-start(bf16[128,2048]{1,0:T(8,128)(2,1)} %value_ref.1) | copy-start | bytes 1572868
  45.7 5.2 %copy-start.2 = (bf16[128,2048]{1,0:T(8,128)(2,1)S(1)}, bf16[128,2048]{1,0:T(8,128)(2,1)}, u32[]{:S(2)}) copy-start(bf16[128,2048]{1,0:T(8,128)(2,1)} %param.6) | copy-start | bytes 1572868
  46.7 19.2 %copy-start.3 = (f32[2048]{0:T(1024)S(1)}, f32[2048]{0:T(1024)}, u32[]{:S(2)}) copy-start(f32[2048]{0:T(1024)} %param.11) | copy-start | bytes 24580
  46.7 19.2 %all-to-all-start.1 = ((bf16[32,1,64,128]{3,2,1,0:T(8,128)(2,1)}), bf16[32,1,64,128]{3,2,1,0:T(8,128)(2,1)S(1)}, u32[]{:S(2)}, u32[]{:S(2)}) async-start(bf16[32,1,64,128]{3,2,1,0:T(8,128)(2,1)} %copy.25), calls=%async_computation.1 | async-start | bytes 1048576 | tf_op jit(solution)/shard_map/all_to_all | solution.py:214

commit v17 on v14

--- a/solution.py
+++ b/solution.py
@@ -121,6 +121,17 @@
         finish_kernel,
         out_shape=jax.ShapeDtypeStruct(query.shape, jnp.bfloat16),
     )(returned, query, key_in, value_in, skip_gain.reshape(1, -1))
+
+
+def flip_kernel(in_ref, out_ref):
+    out_ref[...] = in_ref[...].astype(jnp.float32).T
+
+
+def flip(block):
+    return pl.pallas_call(
+        flip_kernel,
+        out_shape=jax.ShapeDtypeStruct((block.shape[1], block.shape[0]), jnp.float32),
+    )(block)
 
 
 def complex_table(cos_part, sin_part, direction):
@@ -211,7 +222,7 @@
 
 def on_device(query, key_in, value_in, filters, group_index, skip_gain):
     mixed = (key_in.astype(jnp.float32) * value_in.astype(jnp.float32)).astype(jnp.bfloat16)
-    convolved = by_channels(mixed, key_in, value_in, filters, group_index).T.astype(jnp.float32)
+    convolved = flip(by_channels(mixed, key_in, value_in, filters, group_index))
     mixed_wide = mixed.astype(jnp.float32)
     return (query.astype(jnp.float32) * (convolved + skip_gain[None, :] * mixed_wide)).astype(
         jnp.bfloat16

time: 67.8 us -> 70 us (1.032)
  blocking collectives: 0 us -> 19.1 us
  waiting for transfers between devices: 40.1 us -> 25.4 us
  starting transfers between devices: 10.9 us -> 7.3 us
  local copies, waits for them, and re-layouts: 2.84 us -> 0.23 us
  Pallas kernels: 2.66 us -> 4.87 us
  other arithmetic: 3.25 us -> 5.09 us
    all_to_all x0 -> x1, blocking collectives: none -> 19.1 us  [by_channels(): lax.all_to_all(jnp.stack(results, axis=1), ('outer', 'inner'), split_axis...]
    all_to_all x1 -> x0, waiting for transfers between devices: 14.7 us -> none  [by_channels(): lax.all_to_all(jnp.stack(results, axis=1), ('outer', 'inner'), split_axis...]
    all_to_all x1 -> x0, starting transfers between devices: 3.62 us -> none  [by_channels(): lax.all_to_all(jnp.stack(results, axis=1), ('outer', 'inner'), split_axis...]
    pallas_call x0 -> x1, Pallas kernels: none -> 2.22 us  [flip(): pl.pallas_call(flip_kernel, out_shape=jax.ShapeDtypeStruct((block.shape[1...]
    convert_element_type x1, other arithmetic: 0.47 us -> 2.31 us  [on_device(): (query.astype(jnp.float32) * (convolved + skip_gain[None, :] * mixed_wide...]
    convert_element_type x1 -> x0, local copies, waits for them, and re-layouts: 1.01 us -> none  [on_device(): (query.astype(jnp.float32) * (convolved + skip_gain[None, :] * mixed_wide...]
    unnamed x11 -> x8, local copies, waits for them, and re-layouts: 0.83 us -> 0.03 us
    another operation x1, local copies, waits for them, and re-layouts: 1 us -> 0.21 us  [by_channels(): jnp.stack(results, axis=1)]
  transfers between devices with their start and end apart: 2 -> 1, of which waited for: 2 -> 1; matrix products, arithmetic and copies ran while one was open for 2% -> 1% of each run, Pallas kernels for 0% -> 0%
where the time goes in v17:
time: 70 us; the launch traced here: 69.6 us
  waiting for transfers between devices  25.4 us (36%)
  blocking collectives  19.1 us (27%)
  matrix products  7.51 us (11%)
  starting transfers between devices  7.3 us (10%)
  other arithmetic  5.09 us (7%)
  Pallas kernels  4.87 us (7%)
    all_to_all x1, waiting for transfers between devices, by_channels(): lax.all_to_all(sent[piece], ('outer', 'inner'), split_axis=0, concat_axis...  25.4 us
    all_to_all x1, blocking collectives, by_channels(): lax.all_to_all(jnp.stack(results, axis=1), ('outer', 'inner'), split_axis...  19.1 us
    dot_general x4, matrix products, contract(): jnp.einsum(pattern, left_op, right_op, precision=lax.Precision.HIGH, pref...  7.51 us
    all_to_all x1, starting transfers between devices, by_channels(): lax.all_to_all(sent[piece], ('outer', 'inner'), split_axis=0, concat_axis...  7.3 us
    pallas_call x1, Pallas kernels, prepare(): pl.pallas_call(prep_kernel, out_shape=tuple((jax.ShapeDtypeStruct((n_dev,...  2.65 us
    convert_element_type x1, other arithmetic, on_device(): (query.astype(jnp.float32) * (convolved + skip_gain[None, :] * mixed_wide...  2.31 us
    pallas_call x1, Pallas kernels, flip(): pl.pallas_call(flip_kernel, out_shape=jax.ShapeDtypeStruct((block.shape[1...  2.22 us
  transfers between devices with their start and end apart: 1, of which 1 were waited for; matrix products, arithmetic and copies ran while one was open for 1% of the time, Pallas kernels for 0%

profile of v17, /device:TPU:0, one launch (start us, length us, event | category | flops | bytes accessed | tf_op | source)
XLA Modules:
  0.0 69.6 jit_solution(790953488176285538)
XLA Ops:
  0.0 2.6 %shard_map.64 = bf16[32,2,64,128]{3,2,1,0:T(8,128)(2,1)} custom-call(bf16[128,2048]{1,0:T(8,128)(2,1)} %key_ref.1, bf16[128,2048]{1,0:T(8,128)(2,1)} %value_ref.1, bf16[128,128]{1,0:T(8,128)(2,1)} %filters_ref.1, s32[1,2048]{1,0:T(1,128)} %bitcast.19), custom_call_target="tpu_custom_call" | custom-call | tf_op jit(solution)/shard_map/pallas_call | solution.py:99
  2.6 7.3 %all-to-all-start = ((bf16[32,2,64,128]{3,2,1,0:T(8,128)(2,1)}), bf16[32,2,64,128]{3,2,1,0:T(8,128)(2,1)S(1)}, u32[]{:S(2)}, u32[]{:S(2)}) async-start(bf16[32,2,64,128]{3,2,1,0:T(8,128)(2,1)} %shard_map.64), calls=%async_computation | async-start | bytes 2097152 | tf_op jit(solution)/shard_map/all_to_all | solution.py:206
  10.0 0.1 sine_negate_fusion
  10.1 0.1 fusion.59
  10.2 0.3 fusion.36
  10.4 0.3 broadcast_multiply_fusion
  10.7 0.1 cosine_multiply_fusion
  10.8 25.4 %all-to-all-done = bf16[32,2,64,128]{3,2,1,0:T(8,128)(2,1)S(1)} async-done(((bf16[32,2,64,128]{3,2,1,0:T(8,128)(2,1)}), bf16[32,2,64,128]{3,2,1,0:T(8,128)(2,1)S(1)}, u32[]{:S(2)}, u32[]{:S(2)}) %all-to-all-start) | async-done | bytes 1048608 | tf_op jit(solution)/shard_map/all_to_all | solution.py:206
  36.2 1.6 %fusion.17 = f32[66,128,128]{2,0,1:T(8,128)S(1)} fusion(bf16[32,128,128]{2,1,0:T(8,128)(2,1)S(1)} %bitcast.17, f32[33,32]{0,1:T(8,128)S(1)} %get-tuple-element.13, f32[33,32]{0,1:T(8,128)S(1)} %get-tuple-element.14), kind=kOutput, calls=%fused_computation.19 | convolution fusion | flops 207620160 | bytes 5382400 | tf_op jit(solution)/shard_map/kn,ncb->kcb/dot_general | solution.py:11
  37.8 0.7 %multiply_add_fusion = (f32[33,128,128]{2,0,1:T(8,128)S(1)}, f32[33,128,128]{2,0,1:T(8,128)S(1)}) fusion(f32[66,128,128]{2,0,1:T(8,128)S(1)} %fusion.17, f32[33,128]{1,0:T(8,128)S(1)} %get-tuple-element.15, f32[33,128]{1,0:T(8,128)S(1)} %get-tuple-element.16), kind=kLoop, calls=%fused_computation.4 | loop fusion | flops 3244032 | bytes 8684544 | tf_op jit(solution)/shard_map/add | solution.py:38
  38.5 0.3 pad_maximum_fusion
  38.9 3.0 %fusion = f32[33,128,256]{2,1,0:T(8,128)S(1)} fusion(f32[33,128,256]{2,0,1:T(8,128)S(1)} %pad_maximum_fusion, f32[128,128]{1,0:T(8,128)S(1)} %fusion.36, f32[128,128]{1,0:T(8,128)S(1)} %get-tuple-element.18, f32[128,128]{1,0:T(8,128)S(1)} %get-tuple-element.17), kind=kOutput, calls=%fused_computation.1 | convolution fusion | flops 1661140992 | bytes 8847360 | tf_op jit(solution)/shard_map/kcb,bq->kcq/dot_general | solution.py:11
  41.9 0.3 multiply_subtract_fusion.2
  42.2 1.0 %fusion.4 = f32[33,64,256]{2,1,0:T(8,128)S(1)} fusion(f32[33,64,128]{2,1,0:T(8,128)S(1)} %get-tuple-element.8, f32[33,64,128]{2,1,0:T(8,128)S(1)} %get-tuple-element.7, f32[128,128]{1,0:T(8,128)S(1)} %fusion.36, f32[128,128]{1,0:T(8,128)S(1)} %get-tuple-element.17, f32[128,128]{1,0:T(8,128)S(1)} %get-tuple-element.18), kind=kOutput, calls=%fused_computation.7 | convolution fusion | flops 831209472 | bytes 4521984 | tf_op jit(solution)/shard_map/kcq,qb->kcb/dot_general | solution.py:11
  43.2 0.3 multiply_subtract_fusion.1
  43.6 0.2 pad_maximum_fusion.1
  43.9 1.9 %fusion.14 = bf16[32,1,64,128]{3,0,2,1:T(8,128)(2,1)S(1)} fusion(f32[66,64,128]{2,1,0:T(8,128)S(1)} %pad_maximum_fusion.1, f32[32,33]{1,0:T(8,128)S(1)} %get-tuple-element.12, f32[32,33]{1,0:T(8,128)S(1)} %get-tuple-element.11), kind=kOutput, calls=%fused_computation.14 | convolution fusion | flops 104335424 | bytes 2695424 | tf_op jit(solution)/shard_map/nk,kcb->ncb/dot_general | solution.py:11
  45.7 0.0 copy-start
  45.8 0.0 copy-start.1
  45.8 0.0 copy-start.2
  45.8 0.0 copy-start.3
  45.8 0.2 copy.14
  46.0 19.1 %all_to_all.10 = bf16[32,1,64,128]{3,2,1,0:T(8,128)(2,1)} all-to-all(bf16[32,1,64,128]{3,2,1,0:T(8,128)(2,1)S(1)} %copy.14), channel_id=1, replica_groups=mesh['outer'=8,'inner'=4] {'outer','inner'}, dimensions={0} | all-to-all | bytes 1048576 | tf_op jit(solution)/shard_map/all_to_all | solution.py:217
  65.1 2.2 %shard_map.65 = f32[128,2048]{1,0:T(8,128)} custom-call(bf16[2048,128]{1,0:T(8,128)(2,1)} %bitcast.18), custom_call_target="tpu_custom_call" | custom-call | tf_op jit(solution)/shard_map/pallas_call | solution.py:131
  67.3 0.0 copy-done
  67.3 0.0 copy-done.1
  67.3 0.0 copy-done.2
  67.3 0.0 copy-done.3
  67.3 2.3 %multiply_convert_fusion = bf16[128,2048]{1,0:T(8,128)(2,1)} fusion(f32[128,2048]{1,0:T(8,128)} %shard_map.65, bf16[128,2048]{1,0:T(8,128)(2,1)S(1)} %copy-done.2, bf16[128,2048]{1,0:T(8,128)(2,1)S(1)} %copy-done.1, bf16[128,2048]{1,0:T(8,128)(2,1)S(1)} %copy-done, f32[2048]{0:T(1024)S(1)} %copy-done.3), kind=kLoop, calls=%fused_computation.21 | loop fusion | flops 2621440 | bytes 3153920 | tf_op jit(solution)/shard_map/convert_element_type | solution.py:227
  (1 shorter events, 0.0 us)
Async XLA Ops:
  2.6 33.5 %all-to-all-start = ((bf16[32,2,64,128]{3,2,1,0:T(8,128)(2,1)}), bf16[32,2,64,128]{3,2,1,0:T(8,128)(2,1)S(1)}, u32[]{:S(2)}, u32[]{:S(2)}) async-start(bf16[32,2,64,128]{3,2,1,0:T(8,128)(2,1)} %shard_map.64), calls=%async_computation | async-start | bytes 2097152 | tf_op jit(solution)/shard_map/all_to_all | solution.py:206
  45.7 21.6 %copy-start = (bf16[128,2048]{1,0:T(8,128)(2,1)S(1)}, bf16[128,2048]{1,0:T(8,128)(2,1)}, u32[]{:S(2)}) copy-start(bf16[128,2048]{1,0:T(8,128)(2,1)} %key_ref.1) | copy-start | bytes 1572868
  45.8 21.6 %copy-start.1 = (bf16[128,2048]{1,0:T(8,128)(2,1)S(1)}, bf16[128,2048]{1,0:T(8,128)(2,1)}, u32[]{:S(2)}) copy-start(bf16[128,2048]{1,0:T(8,128)(2,1)} %value_ref.1) | copy-start | bytes 1572868
  45.8 21.5 %copy-start.2 = (bf16[128,2048]{1,0:T(8,128)(2,1)S(1)}, bf16[128,2048]{1,0:T(8,128)(2,1)}, u32[]{:S(2)}) copy-start(bf16[128,2048]{1,0:T(8,128)(2,1)} %param.6) | copy-start | bytes 1572868
  45.8 21.5 %copy-start.3 = (f32[2048]{0:T(1024)S(1)}, f32[2048]{0:T(1024)}, u32[]{:S(2)}) copy-start(f32[2048]{0:T(1024)} %param.11) | copy-start | bytes 24580

commit v18 on v14

--- a/solution.py
+++ b/solution.py
@@ -79,13 +79,15 @@
     mixed = (key_ref[...].astype(jnp.float32) * value_ref[...].astype(jnp.float32)).astype(
         jnp.bfloat16
     )
-    mixed_t = mixed.astype(jnp.float32).T
+    mixed_t = mixed.T
     groups = filters_ref.shape[1]
     channels = index_ref.shape[1]
     onehot_t = (
         lax.broadcasted_iota(jnp.int32, (groups, channels), 0) == index_ref[...]
     ).astype(jnp.bfloat16)
-    picked = jnp.dot(filters_ref[...], onehot_t, preferred_element_type=jnp.float32).T
+    picked = jnp.dot(filters_ref[...], onehot_t, preferred_element_type=jnp.float32).astype(
+        jnp.bfloat16
+    ).T
     for dest in range(n_dev):
         for piece in range(pieces):
             low = (dest * pieces + piece) * piece_width

time: 67.8 us -> 67.7 us (level)
  no operation moved by 1% of the time
where the time goes in v18:
time: 67.7 us; the launch traced here: 67.4 us
  waiting for transfers between devices  40.1 us (59%)
  starting transfers between devices  10.9 us (16%)
  matrix products  7.51 us (11%)
  other arithmetic  3.25 us (5%)
  local copies, waits for them, and re-layouts  2.84 us (4%)
  Pallas kernels  2.58 us (4%)
    all_to_all x1, waiting for transfers between devices, by_channels(): lax.all_to_all(sent[piece], ('outer', 'inner'), split_axis=0, concat_axis...  25.4 us
    all_to_all x1, waiting for transfers between devices, by_channels(): lax.all_to_all(jnp.stack(results, axis=1), ('outer', 'inner'), split_axis...  14.7 us
    dot_general x4, matrix products, contract(): jnp.einsum(pattern, left_op, right_op, precision=lax.Precision.HIGH, pref...  7.51 us
    all_to_all x1, starting transfers between devices, by_channels(): lax.all_to_all(sent[piece], ('outer', 'inner'), split_axis=0, concat_axis...  7.29 us
    all_to_all x1, starting transfers between devices, by_channels(): lax.all_to_all(jnp.stack(results, axis=1), ('outer', 'inner'), split_axis...  3.62 us
    pallas_call x1, Pallas kernels, prepare(): pl.pallas_call(prep_kernel, out_shape=tuple((jax.ShapeDtypeStruct((n_dev,...  2.58 us
  transfers between devices with their start and end apart: 2, of which 2 were waited for; matrix products, arithmetic and copies ran while one was open for 2% of the time, Pallas kernels for 0%

profile of v18, /device:TPU:0, one launch (start us, length us, event | category | flops | bytes accessed | tf_op | source)
XLA Modules:
  0.0 67.4 jit_solution(10597824759190743013)
XLA Ops:
  0.0 2.6 %shard_map.64 = bf16[32,2,64,128]{3,2,1,0:T(8,128)(2,1)} custom-call(bf16[128,2048]{1,0:T(8,128)(2,1)} %key_ref.1, bf16[128,2048]{1,0:T(8,128)(2,1)} %value_ref.1, bf16[128,128]{1,0:T(8,128)(2,1)} %filters_ref.1, s32[1,2048]{1,0:T(1,128)} %bitcast.30), custom_call_target="tpu_custom_call" | custom-call | tf_op jit(solution)/shard_map/pallas_call | solution.py:101
  2.6 7.3 %all-to-all-start = ((bf16[32,2,64,128]{3,2,1,0:T(8,128)(2,1)}), bf16[32,2,64,128]{3,2,1,0:T(8,128)(2,1)S(1)}, u32[]{:S(2)}, u32[]{:S(2)}) async-start(bf16[32,2,64,128]{3,2,1,0:T(8,128)(2,1)} %shard_map.64), calls=%async_computation | async-start | bytes 2097152 | tf_op jit(solution)/shard_map/all_to_all | solution.py:197
  9.9 0.1 sine_negate_fusion
  10.0 0.1 fusion.62
  10.1 0.3 fusion.39
  10.3 0.3 broadcast_multiply_fusion
  10.6 0.1 cosine_multiply_fusion
  10.7 25.4 %all-to-all-done = bf16[32,2,64,128]{3,2,1,0:T(8,128)(2,1)S(1)} async-done(((bf16[32,2,64,128]{3,2,1,0:T(8,128)(2,1)}), bf16[32,2,64,128]{3,2,1,0:T(8,128)(2,1)S(1)}, u32[]{:S(2)}, u32[]{:S(2)}) %all-to-all-start) | async-done | bytes 1048608 | tf_op jit(solution)/shard_map/all_to_all | solution.py:197
  36.1 1.6 %fusion.20 = f32[66,128,128]{2,0,1:T(8,128)S(1)} fusion(bf16[32,128,128]{2,1,0:T(8,128)(2,1)S(1)} %bitcast.29, f32[33,32]{0,1:T(8,128)S(1)} %get-tuple-element.13, f32[33,32]{0,1:T(8,128)S(1)} %get-tuple-element.14), kind=kOutput, calls=%fused_computation.23 | convolution fusion | flops 207620160 | bytes 5382400 | tf_op jit(solution)/shard_map/kn,ncb->kcb/dot_general | solution.py:11
  37.7 0.7 %multiply_add_fusion = (f32[33,128,128]{2,0,1:T(8,128)S(1)}, f32[33,128,128]{2,0,1:T(8,128)S(1)}) fusion(f32[66,128,128]{2,0,1:T(8,128)S(1)} %fusion.20, f32[33,128]{1,0:T(8,128)S(1)} %get-tuple-element.15, f32[33,128]{1,0:T(8,128)S(1)} %get-tuple-element.16), kind=kLoop, calls=%fused_computation.4 | loop fusion | flops 3244032 | bytes 8684544 | tf_op jit(solution)/shard_map/add | solution.py:38
  38.5 0.3 pad_maximum_fusion
  38.8 3.0 %fusion = f32[33,128,256]{2,1,0:T(8,128)S(1)} fusion(f32[33,128,256]{2,0,1:T(8,128)S(1)} %pad_maximum_fusion, f32[128,128]{1,0:T(8,128)S(1)} %fusion.39, f32[128,128]{1,0:T(8,128)S(1)} %get-tuple-element.18, f32[128,128]{1,0:T(8,128)S(1)} %get-tuple-element.17), kind=kOutput, calls=%fused_computation.1 | convolution fusion | flops 1661140992 | bytes 8847360 | tf_op jit(solution)/shard_map/kcb,bq->kcq/dot_general | solution.py:11
  41.8 0.3 multiply_subtract_fusion.2
  42.1 1.0 %fusion.4 = f32[33,64,256]{2,1,0:T(8,128)S(1)} fusion(f32[33,64,128]{2,1,0:T(8,128)S(1)} %get-tuple-element.8, f32[33,64,128]{2,1,0:T(8,128)S(1)} %get-tuple-element.7, f32[128,128]{1,0:T(8,128)S(1)} %fusion.39, f32[128,128]{1,0:T(8,128)S(1)} %get-tuple-element.17, f32[128,128]{1,0:T(8,128)S(1)} %get-tuple-element.18), kind=kOutput, calls=%fused_computation.7 | convolution fusion | flops 831209472 | bytes 4521984 | tf_op jit(solution)/shard_map/kcq,qb->kcb/dot_general | solution.py:11
  43.2 0.3 multiply_subtract_fusion.1
  43.5 0.2 pad_maximum_fusion.1
  43.8 0.0 copy-start
  43.8 1.9 %fusion.14 = bf16[32,1,64,128]{3,0,2,1:T(8,128)(2,1)S(1)} fusion(f32[66,64,128]{2,1,0:T(8,128)S(1)} %pad_maximum_fusion.1, f32[32,33]{1,0:T(8,128)S(1)} %get-tuple-element.12, f32[32,33]{1,0:T(8,128)S(1)} %get-tuple-element.11), kind=kOutput, calls=%fused_computation.14 | convolution fusion | flops 104335424 | bytes 2695424 | tf_op jit(solution)/shard_map/nk,kcb->ncb/dot_general | solution.py:11
  45.7 0.0 copy-start.1
  45.7 0.0 copy-start.2
  45.7 1.0 %copy.22 = bf16[32,1,64,128]{3,2,1,0:T(8,128)(2,1)} copy(bf16[32,1,64,128]{3,0,2,1:T(8,128)(2,1)S(1)} %fusion.14) | data formatting | bytes 1048576 | tf_op jit(solution)/shard_map/stack | solution.py:209
  46.7 0.0 copy-start.3
  46.7 3.6 %all-to-all-start.1 = ((bf16[32,1,64,128]{3,2,1,0:T(8,128)(2,1)}), bf16[32,1,64,128]{3,2,1,0:T(8,128)(2,1)S(1)}, u32[]{:S(2)}, u32[]{:S(2)}) async-start(bf16[32,1,64,128]{3,2,1,0:T(8,128)(2,1)} %copy.22), calls=%async_computation.1 | async-start | bytes 1048576 | tf_op jit(solution)/shard_map/all_to_all | solution.py:208
  50.3 0.0 copy-done
  50.4 0.3 copy.24
  50.6 0.0 copy-done.1
  50.6 0.3 copy.25
  50.9 0.0 copy-done.2
  50.9 0.3 copy.18
  51.2 14.7 %all-to-all-done.1 = bf16[32,1,64,128]{3,2,1,0:T(8,128)(2,1)S(1)} async-done(((bf16[32,1,64,128]{3,2,1,0:T(8,128)(2,1)}), bf16[32,1,64,128]{3,2,1,0:T(8,128)(2,1)S(1)}, u32[]{:S(2)}, u32[]{:S(2)}) %all-to-all-start.1) | async-done | bytes 524320 | tf_op jit(solution)/shard_map/all_to_all | solution.py:208
  65.9 0.0 copy-done.3
  65.9 0.5 fusion.19
  66.4 1.0 %copy.26 = bf16[128,2048]{1,0:T(8,128)(2,1)} copy(bf16[128,2048]{0,1:T(8,128)(2,1)S(1)} %fusion.19) | data formatting | bytes 1048576 | tf_op jit(solution)/shard_map/convert_element_type | solution.py:218
  (1 shorter events, 0.0 us)
Async XLA Ops:
  2.6 33.5 %all-to-all-start = ((bf16[32,2,64,128]{3,2,1,0:T(8,128)(2,1)}), bf16[32,2,64,128]{3,2,1,0:T(8,128)(2,1)S(1)}, u32[]{:S(2)}, u32[]{:S(2)}) async-start(bf16[32,2,64,128]{3,2,1,0:T(8,128)(2,1)} %shard_map.64), calls=%async_computation | async-start | bytes 2097152 | tf_op jit(solution)/shard_map/all_to_all | solution.py:197
  43.8 6.6 %copy-start = (bf16[128,2048]{1,0:T(8,128)(2,1)S(1)}, bf16[128,2048]{1,0:T(8,128)(2,1)}, u32[]{:S(2)}) copy-start(bf16[128,2048]{1,0:T(8,128)(2,1)} %key_ref.1) | copy-start | bytes 1572868
  45.7 4.9 %copy-start.1 = (bf16[128,2048]{1,0:T(8,128)(2,1)S(1)}, bf16[128,2048]{1,0:T(8,128)(2,1)}, u32[]{:S(2)}) copy-start(bf16[128,2048]{1,0:T(8,128)(2,1)} %value_ref.1) | copy-start | bytes 1572868
  45.7 5.2 %copy-start.2 = (bf16[128,2048]{1,0:T(8,128)(2,1)S(1)}, bf16[128,2048]{1,0:T(8,128)(2,1)}, u32[]{:S(2)}) copy-start(bf16[128,2048]{1,0:T(8,128)(2,1)} %param.6) | copy-start | bytes 1572868
  46.7 19.2 %copy-start.3 = (f32[2048]{0:T(1024)S(1)}, f32[2048]{0:T(1024)}, u32[]{:S(2)}) copy-start(f32[2048]{0:T(1024)} %param.11) | copy-start | bytes 24580
  46.7 19.2 %all-to-all-start.1 = ((bf16[32,1,64,128]{3,2,1,0:T(8,128)(2,1)}), bf16[32,1,64,128]{3,2,1,0:T(8,128)(2,1)S(1)}, u32[]{:S(2)}, u32[]{:S(2)}) async-start(bf16[32,1,64,128]{3,2,1,0:T(8,128)(2,1)} %copy.22), calls=%async_computation.1 | async-start | bytes 1048576 | tf_op jit(solution)/shard_map/all_to_all | solution.py:208

commit v19 on v14

--- a/solution.py
+++ b/solution.py
@@ -146,13 +146,17 @@
         * jnp.arange(row_count, dtype=jnp.int32)[None, :],
         padded,
     )[:, None, :]
-    real_part, imag_part = rotate(first[:kept], first[kept:], twiddle, -1)
+    real_part = first[:kept]
+    imag_part = first[kept:]
+    cosine = jnp.cos(twiddle)
+    sine_part = jnp.sin(twiddle)
+    rotated = jnp.concatenate([real_part, imag_part], axis=2) * jnp.concatenate(
+        [cosine, cosine], axis=2
+    ) + jnp.concatenate([imag_part, real_part], axis=2) * jnp.concatenate(
+        [sine_part, -sine_part], axis=2
+    )
     second_cos, second_sin = dft_table(row_count, row_count, row_count)
-    prod = contract(
-        "kcb,bq->kcq",
-        jnp.concatenate([real_part, imag_part], axis=2),
-        complex_table(second_cos, second_sin, -1),
-    )
+    prod = contract("kcb,bq->kcq", rotated, complex_table(second_cos, second_sin, -1))
     data_real = prod[:, :own_width, :row_count]
     data_imag = prod[:, :own_width, row_count:]
     filter_real = prod[:, own_width:, :row_count]

time: 67.8 us -> 67.7 us (level)
  transfers between devices with their start and end apart: 2 -> 2, of which waited for: 2 -> 2; matrix products, arithmetic and copies ran while one was open for 2% -> 3% of each run, Pallas kernels for 0% -> 0%
where the time goes in v19:
time: 67.7 us; the launch traced here: 67.3 us
  waiting for transfers between devices  39.9 us (59%)
  starting transfers between devices  10.9 us (16%)
  matrix products  7.36 us (11%)
  local copies, waits for them, and re-layouts  3.24 us (5%)
  other arithmetic  3.08 us (5%)
  Pallas kernels  2.65 us (4%)
    all_to_all x1, waiting for transfers between devices, by_channels(): lax.all_to_all(sent[piece], ('outer', 'inner'), split_axis=0, concat_axis...  25.2 us
    all_to_all x1, waiting for transfers between devices, by_channels(): lax.all_to_all(jnp.stack(results, axis=1), ('outer', 'inner'), split_axis...  14.7 us
    dot_general x4, matrix products, contract(): jnp.einsum(pattern, left_op, right_op, precision=lax.Precision.HIGH, pref...  7.36 us
    all_to_all x1, starting transfers between devices, by_channels(): lax.all_to_all(sent[piece], ('outer', 'inner'), split_axis=0, concat_axis...  7.3 us
    all_to_all x1, starting transfers between devices, by_channels(): lax.all_to_all(jnp.stack(results, axis=1), ('outer', 'inner'), split_axis...  3.62 us
    pallas_call x1, Pallas kernels, prepare(): pl.pallas_call(prep_kernel, out_shape=tuple((jax.ShapeDtypeStruct((n_dev,...  2.65 us
  transfers between devices with their start and end apart: 2, of which 2 were waited for; matrix products, arithmetic and copies ran while one was open for 3% of the time, Pallas kernels for 0%

profile of v19, /device:TPU:0, one launch (start us, length us, event | category | flops | bytes accessed | tf_op | source)
XLA Modules:
  0.0 67.3 jit_solution(7062123991919134402)
XLA Ops:
  0.0 2.7 %shard_map.64 = bf16[32,2,64,128]{3,2,1,0:T(8,128)(2,1)} custom-call(bf16[128,2048]{1,0:T(8,128)(2,1)} %key_ref.1, bf16[128,2048]{1,0:T(8,128)(2,1)} %value_ref.1, bf16[128,128]{1,0:T(8,128)(2,1)} %filters_ref.1, s32[1,2048]{1,0:T(1,128)} %bitcast.34), custom_call_target="tpu_custom_call" | custom-call | tf_op jit(solution)/shard_map/pallas_call | solution.py:99
  2.7 7.3 %all-to-all-start = ((bf16[32,2,64,128]{3,2,1,0:T(8,128)(2,1)}), bf16[32,2,64,128]{3,2,1,0:T(8,128)(2,1)S(1)}, u32[]{:S(2)}, u32[]{:S(2)}) async-start(bf16[32,2,64,128]{3,2,1,0:T(8,128)(2,1)} %shard_map.64), calls=%async_computation | async-start | bytes 2097152 | tf_op jit(solution)/shard_map/all_to_all | solution.py:199
  10.0 0.1 fusion.72
  10.1 0.1 sine_negate_fusion
  10.2 0.1 fusion.71
  10.3 0.1 fusion.69
  10.4 0.3 fusion.40
  10.7 0.3 broadcast_multiply_fusion
  10.9 0.1 cosine_multiply_fusion
  11.0 25.2 %all-to-all-done = bf16[32,2,64,128]{3,2,1,0:T(8,128)(2,1)S(1)} async-done(((bf16[32,2,64,128]{3,2,1,0:T(8,128)(2,1)}), bf16[32,2,64,128]{3,2,1,0:T(8,128)(2,1)S(1)}, u32[]{:S(2)}, u32[]{:S(2)}) %all-to-all-start) | async-done | bytes 1048608 | tf_op jit(solution)/shard_map/all_to_all | solution.py:199
  36.2 1.6 %fusion.21 = f32[66,128,128]{2,0,1:T(8,128)S(1)} fusion(bf16[32,128,128]{2,1,0:T(8,128)(2,1)S(1)} %bitcast.33, f32[33,32]{0,1:T(8,128)S(1)} %get-tuple-element.13, f32[33,32]{0,1:T(8,128)S(1)} %get-tuple-element.14), kind=kOutput, calls=%fused_computation.23 | convolution fusion | flops 207620160 | bytes 5382400 | tf_op jit(solution)/shard_map/kn,ncb->kcb/dot_general | solution.py:11
  37.8 0.4 fusion.79
  38.2 0.7 %fusion = f32[33,128,256]{2,0,1:T(8,128)S(1)} fusion(f32[33,128,128]{2,0,1:T(8,128)S(1)} %get-tuple-element.6, f32[33,128,128]{2,0,1:T(8,128)S(1)} %get-tuple-element.5, f32[33,256]{1,0:T(8,128)S(1)} %maximum_bitcast_fusion.1, f32[33,256]{1,0:T(8,128)S(1)} %maximum_bitcast_fusion), kind=kLoop, calls=%fused_computation.1 | loop fusion | flops 5406720 | bytes 8718336 | tf_op jit(solution)/shard_map/add | solution.py:153
  38.9 2.9 %fusion.1 = f32[33,128,256]{2,1,0:T(8,128)S(1)} fusion(f32[33,128,256]{2,0,1:T(8,128)S(1)} %fusion, f32[128,128]{1,0:T(8,128)S(1)} %fusion.40, f32[128,128]{1,0:T(8,128)S(1)} %get-tuple-element.18, f32[128,128]{1,0:T(8,128)S(1)} %get-tuple-element.17), kind=kOutput, calls=%fused_computation.3 | convolution fusion | flops 1661140992 | bytes 8847360 | tf_op jit(solution)/shard_map/kcb,bq->kcq/dot_general | solution.py:11
  41.8 0.3 multiply_subtract_fusion.1
  42.1 1.0 %fusion.5 = f32[33,64,256]{2,1,0:T(8,128)S(1)} fusion(f32[33,64,128]{2,1,0:T(8,128)S(1)} %get-tuple-element.8, f32[33,64,128]{2,1,0:T(8,128)S(1)} %get-tuple-element.7, f32[128,128]{1,0:T(8,128)S(1)} %fusion.40, f32[128,128]{1,0:T(8,128)S(1)} %get-tuple-element.17, f32[128,128]{1,0:T(8,128)S(1)} %get-tuple-element.18), kind=kOutput, calls=%fused_computation.7 | convolution fusion | flops 831209472 | bytes 4521984 | tf_op jit(solution)/shard_map/kcq,qb->kcb/dot_general | solution.py:11
  43.1 0.3 multiply_subtract_fusion
  43.5 0.2 pad_maximum_fusion
  43.7 0.0 copy-start
  43.7 1.9 %fusion.15 = bf16[32,1,64,128]{3,0,2,1:T(8,128)(2,1)S(1)} fusion(f32[66,64,128]{2,1,0:T(8,128)S(1)} %pad_maximum_fusion, f32[32,33]{1,0:T(8,128)S(1)} %get-tuple-element.12, f32[32,33]{1,0:T(8,128)S(1)} %get-tuple-element.11), kind=kOutput, calls=%fused_computation.14 | convolution fusion | flops 104335424 | bytes 2695424 | tf_op jit(solution)/shard_map/nk,kcb->ncb/dot_general | solution.py:11
  45.6 0.0 copy-start.1
  45.7 0.0 copy-start.2
  45.7 1.0 %copy.22 = bf16[32,1,64,128]{3,2,1,0:T(8,128)(2,1)} copy(bf16[32,1,64,128]{3,0,2,1:T(8,128)(2,1)S(1)} %fusion.15) | data formatting | bytes 1048576 | tf_op jit(solution)/shard_map/stack | solution.py:211
  46.7 0.0 copy-start.3
  46.7 3.6 %all-to-all-start.1 = ((bf16[32,1,64,128]{3,2,1,0:T(8,128)(2,1)}), bf16[32,1,64,128]{3,2,1,0:T(8,128)(2,1)S(1)}, u32[]{:S(2)}, u32[]{:S(2)}) async-start(bf16[32,1,64,128]{3,2,1,0:T(8,128)(2,1)} %copy.22), calls=%async_computation.1 | async-start | bytes 1048576 | tf_op jit(solution)/shard_map/all_to_all | solution.py:210
  50.3 0.0 copy-done
  50.3 0.3 copy.24
  50.6 0.0 copy-done.1
  50.6 0.3 copy.25
  50.9 0.0 copy-done.2
  50.9 0.3 copy.18
  51.2 14.7 %all-to-all-done.1 = bf16[32,1,64,128]{3,2,1,0:T(8,128)(2,1)S(1)} async-done(((bf16[32,1,64,128]{3,2,1,0:T(8,128)(2,1)}), bf16[32,1,64,128]{3,2,1,0:T(8,128)(2,1)S(1)}, u32[]{:S(2)}, u32[]{:S(2)}) %all-to-all-start.1) | async-done | bytes 524320 | tf_op jit(solution)/shard_map/all_to_all | solution.py:210
  65.8 0.0 copy-done.3
  65.8 0.5 fusion.20
  66.3 1.0 %copy.26 = bf16[128,2048]{1,0:T(8,128)(2,1)} copy(bf16[128,2048]{0,1:T(8,128)(2,1)S(1)} %fusion.20) | data formatting | bytes 1048576 | tf_op jit(solution)/shard_map/convert_element_type | solution.py:220
  (3 shorter events, 0.0 us)
Async XLA Ops:
  2.7 33.5 %all-to-all-start = ((bf16[32,2,64,128]{3,2,1,0:T(8,128)(2,1)}), bf16[32,2,64,128]{3,2,1,0:T(8,128)(2,1)S(1)}, u32[]{:S(2)}, u32[]{:S(2)}) async-start(bf16[32,2,64,128]{3,2,1,0:T(8,128)(2,1)} %shard_map.64), calls=%async_computation | async-start | bytes 2097152 | tf_op jit(solution)/shard_map/all_to_all | solution.py:199
  43.7 6.6 %copy-start = (bf16[128,2048]{1,0:T(8,128)(2,1)S(1)}, bf16[128,2048]{1,0:T(8,128)(2,1)}, u32[]{:S(2)}) copy-start(bf16[128,2048]{1,0:T(8,128)(2,1)} %key_ref.1) | copy-start | bytes 1572868
  45.6 4.9 %copy-start.1 = (bf16[128,2048]{1,0:T(8,128)(2,1)S(1)}, bf16[128,2048]{1,0:T(8,128)(2,1)}, u32[]{:S(2)}) copy-start(bf16[128,2048]{1,0:T(8,128)(2,1)} %value_ref.1) | copy-start | bytes 1572868
  45.7 5.2 %copy-start.2 = (bf16[128,2048]{1,0:T(8,128)(2,1)S(1)}, bf16[128,2048]{1,0:T(8,128)(2,1)}, u32[]{:S(2)}) copy-start(bf16[128,2048]{1,0:T(8,128)(2,1)} %param.6) | copy-start | bytes 1572868
  46.7 19.2 %copy-start.3 = (f32[2048]{0:T(1024)S(1)}, f32[2048]{0:T(1024)}, u32[]{:S(2)}) copy-start(f32[2048]{0:T(1024)} %param.11) | copy-start | bytes 24580
  46.7 19.2 %all-to-all-start.1 = ((bf16[32,1,64,128]{3,2,1,0:T(8,128)(2,1)}), bf16[32,1,64,128]{3,2,1,0:T(8,128)(2,1)S(1)}, u32[]{:S(2)}, u32[]{:S(2)}) async-start(bf16[32,1,64,128]{3,2,1,0:T(8,128)(2,1)} %copy.22), calls=%async_computation.1 | async-start | bytes 1048576 | tf_op jit(solution)/shard_map/all_to_all | solution.py:210

commit v20 on v14

--- a/solution.py
+++ b/solution.py
@@ -164,14 +164,22 @@
         jnp.concatenate([spec_real, spec_imag], axis=2),
         complex_table(second_cos, second_sin, 1),
     )
-    real_part, imag_part = rotate(prod[:, :, :row_count], prod[:, :, row_count:], twiddle, 1)
+    real_part = prod[:, :, :row_count]
+    imag_part = prod[:, :, row_count:]
+    cosine = jnp.cos(twiddle)
+    sine_part = jnp.sin(twiddle)
+    stacked_back = jnp.concatenate([real_part, imag_part], axis=0) * jnp.concatenate(
+        [cosine, cosine], axis=0
+    ) + jnp.concatenate([imag_part, real_part], axis=0) * jnp.concatenate(
+        [-sine_part, sine_part], axis=0
+    )
     back_cos, back_sin = dft_table(n_dev, kept, size_a)
     index = jnp.arange(kept)
     weight = jnp.where((index == 0) | (index == n_dev), 1.0, 2.0).astype(jnp.float32)[None, :]
     outcome = contract(
         "nk,kcb->ncb",
         jnp.concatenate([back_cos * weight, -back_sin * weight], axis=1),
-        jnp.concatenate([real_part, imag_part], axis=0),
+        stacked_back,
     )
     return (outcome * (1.0 / padded)).astype(jnp.bfloat16)
 

time: 67.8 us -> 68.1 us (level)
  transfers between devices with their start and end apart: 2 -> 2, of which waited for: 2 -> 2; matrix products, arithmetic and copies ran while one was open for 2% -> 3% of each run, Pallas kernels for 0% -> 0%
where the time goes in v20:
time: 68.1 us; the launch traced here: 67.8 us
  waiting for transfers between devices  39.9 us (59%)
  starting transfers between devices  10.9 us (16%)
  matrix products  7.51 us (11%)
  other arithmetic  3.48 us (5%)
  local copies, waits for them, and re-layouts  3.12 us (5%)
  Pallas kernels  2.65 us (4%)
    all_to_all x1, waiting for transfers between devices, by_channels(): lax.all_to_all(sent[piece], ('outer', 'inner'), split_axis=0, concat_axis...  25.2 us
    all_to_all x1, waiting for transfers between devices, by_channels(): lax.all_to_all(jnp.stack(results, axis=1), ('outer', 'inner'), split_axis...  14.7 us
    dot_general x4, matrix products, contract(): jnp.einsum(pattern, left_op, right_op, precision=lax.Precision.HIGH, pref...  7.51 us
    all_to_all x1, starting transfers between devices, by_channels(): lax.all_to_all(sent[piece], ('outer', 'inner'), split_axis=0, concat_axis...  7.3 us
    all_to_all x1, starting transfers between devices, by_channels(): lax.all_to_all(jnp.stack(results, axis=1), ('outer', 'inner'), split_axis...  3.62 us
    pallas_call x1, Pallas kernels, prepare(): pl.pallas_call(prep_kernel, out_shape=tuple((jax.ShapeDtypeStruct((n_dev,...  2.65 us
  transfers between devices with their start and end apart: 2, of which 2 were waited for; matrix products, arithmetic and copies ran while one was open for 3% of the time, Pallas kernels for 0%

profile of v20, /device:TPU:0, one launch (start us, length us, event | category | flops | bytes accessed | tf_op | source)
XLA Modules:
  0.0 67.8 jit_solution(1149672063797234545)
XLA Ops:
  0.0 2.7 %shard_map.64 = bf16[32,2,64,128]{3,2,1,0:T(8,128)(2,1)} custom-call(bf16[128,2048]{1,0:T(8,128)(2,1)} %key_ref.1, bf16[128,2048]{1,0:T(8,128)(2,1)} %value_ref.1, bf16[128,128]{1,0:T(8,128)(2,1)} %filters_ref.1, s32[1,2048]{1,0:T(1,128)} %bitcast.34), custom_call_target="tpu_custom_call" | custom-call | tf_op jit(solution)/shard_map/pallas_call | solution.py:99
  2.7 7.3 %all-to-all-start = ((bf16[32,2,64,128]{3,2,1,0:T(8,128)(2,1)}), bf16[32,2,64,128]{3,2,1,0:T(8,128)(2,1)S(1)}, u32[]{:S(2)}, u32[]{:S(2)}) async-start(bf16[32,2,64,128]{3,2,1,0:T(8,128)(2,1)} %shard_map.64), calls=%async_computation | async-start | bytes 2097152 | tf_op jit(solution)/shard_map/all_to_all | solution.py:203
  10.0 0.1 fusion.70
  10.1 0.1 sine_negate_fusion
  10.2 0.1 fusion.69
  10.3 0.1 fusion.71
  10.4 0.3 fusion.40
  10.7 0.3 broadcast_multiply_fusion
  10.9 0.1 cosine_multiply_fusion
  11.0 25.2 %all-to-all-done = bf16[32,2,64,128]{3,2,1,0:T(8,128)(2,1)S(1)} async-done(((bf16[32,2,64,128]{3,2,1,0:T(8,128)(2,1)}), bf16[32,2,64,128]{3,2,1,0:T(8,128)(2,1)S(1)}, u32[]{:S(2)}, u32[]{:S(2)}) %all-to-all-start) | async-done | bytes 1048608 | tf_op jit(solution)/shard_map/all_to_all | solution.py:203
  36.2 1.6 %fusion.21 = f32[66,128,128]{2,0,1:T(8,128)S(1)} fusion(bf16[32,128,128]{2,1,0:T(8,128)(2,1)S(1)} %bitcast.33, f32[33,32]{0,1:T(8,128)S(1)} %get-tuple-element.13, f32[33,32]{0,1:T(8,128)S(1)} %get-tuple-element.14), kind=kOutput, calls=%fused_computation.23 | convolution fusion | flops 207620160 | bytes 5382400 | tf_op jit(solution)/shard_map/kn,ncb->kcb/dot_general | solution.py:11
  37.8 0.7 %multiply_add_fusion = (f32[33,128,128]{2,0,1:T(8,128)S(1)}, f32[33,128,128]{2,0,1:T(8,128)S(1)}) fusion(f32[66,128,128]{2,0,1:T(8,128)S(1)} %fusion.21, f32[33,128]{1,0:T(8,128)S(1)} %get-tuple-element.15, f32[33,128]{1,0:T(8,128)S(1)} %get-tuple-element.16), kind=kLoop, calls=%fused_computation.4 | loop fusion | flops 3244032 | bytes 8684544 | tf_op jit(solution)/shard_map/add | solution.py:38
  38.5 0.3 pad_maximum_fusion
  38.9 3.0 %fusion = f32[33,128,256]{2,1,0:T(8,128)S(1)} fusion(f32[33,128,256]{2,0,1:T(8,128)S(1)} %pad_maximum_fusion, f32[128,128]{1,0:T(8,128)S(1)} %fusion.40, f32[128,128]{1,0:T(8,128)S(1)} %get-tuple-element.18, f32[128,128]{1,0:T(8,128)S(1)} %get-tuple-element.17), kind=kOutput, calls=%fused_computation.1 | convolution fusion | flops 1661140992 | bytes 8847360 | tf_op jit(solution)/shard_map/kcb,bq->kcq/dot_general | solution.py:11
  41.9 0.3 multiply_subtract_fusion.1
  42.2 1.0 %fusion.4 = f32[33,64,256]{2,1,0:T(8,128)S(1)} fusion(f32[33,64,128]{2,1,0:T(8,128)S(1)} %get-tuple-element.8, f32[33,64,128]{2,1,0:T(8,128)S(1)} %get-tuple-element.7, f32[128,128]{1,0:T(8,128)S(1)} %fusion.40, f32[128,128]{1,0:T(8,128)S(1)} %get-tuple-element.17, f32[128,128]{1,0:T(8,128)S(1)} %get-tuple-element.18), kind=kOutput, calls=%fused_computation.7 | convolution fusion | flops 831209472 | bytes 4521984 | tf_op jit(solution)/shard_map/kcq,qb->kcb/dot_general | solution.py:11
  43.3 0.3 fusion.79
  43.5 0.6 fusion.8
  44.2 0.0 copy-start
  44.2 1.9 %fusion.15 = bf16[32,1,64,128]{3,0,2,1:T(8,128)(2,1)S(1)} fusion(f32[66,64,128]{2,1,0:T(8,128)S(1)} %fusion.8, f32[32,33]{1,0:T(8,128)S(1)} %get-tuple-element.12, f32[32,33]{1,0:T(8,128)S(1)} %get-tuple-element.11), kind=kOutput, calls=%fused_computation.16 | convolution fusion | flops 104335424 | bytes 2695424 | tf_op jit(solution)/shard_map/nk,kcb->ncb/dot_general | solution.py:11
  46.1 0.0 copy-start.1
  46.1 0.0 copy-start.2
  46.1 1.0 %copy.22 = bf16[32,1,64,128]{3,2,1,0:T(8,128)(2,1)} copy(bf16[32,1,64,128]{3,0,2,1:T(8,128)(2,1)S(1)} %fusion.15) | data formatting | bytes 1048576 | tf_op jit(solution)/shard_map/stack | solution.py:215
  47.1 0.0 copy-start.3
  47.1 3.6 %all-to-all-start.1 = ((bf16[32,1,64,128]{3,2,1,0:T(8,128)(2,1)}), bf16[32,1,64,128]{3,2,1,0:T(8,128)(2,1)S(1)}, u32[]{:S(2)}, u32[]{:S(2)}) async-start(bf16[32,1,64,128]{3,2,1,0:T(8,128)(2,1)} %copy.22), calls=%async_computation.1 | async-start | bytes 1048576 | tf_op jit(solution)/shard_map/all_to_all | solution.py:214
  50.7 0.0 copy-done
  50.7 0.3 copy.24
  51.0 0.0 copy-done.1
  51.0 0.3 copy.25
  51.3 0.0 copy-done.2
  51.3 0.3 copy.18
  51.6 14.7 %all-to-all-done.1 = bf16[32,1,64,128]{3,2,1,0:T(8,128)(2,1)S(1)} async-done(((bf16[32,1,64,128]{3,2,1,0:T(8,128)(2,1)}), bf16[32,1,64,128]{3,2,1,0:T(8,128)(2,1)S(1)}, u32[]{:S(2)}, u32[]{:S(2)}) %all-to-all-start.1) | async-done | bytes 524320 | tf_op jit(solution)/shard_map/all_to_all | solution.py:214
  66.3 0.0 copy-done.3
  66.3 0.5 fusion.20
  66.8 1.0 %copy.26 = bf16[128,2048]{1,0:T(8,128)(2,1)} copy(bf16[128,2048]{0,1:T(8,128)(2,1)S(1)} %fusion.20) | data formatting | bytes 1048576 | tf_op jit(solution)/shard_map/convert_element_type | solution.py:224
  (3 shorter events, 0.0 us)
Async XLA Ops:
  2.7 33.5 %all-to-all-start = ((bf16[32,2,64,128]{3,2,1,0:T(8,128)(2,1)}), bf16[32,2,64,128]{3,2,1,0:T(8,128)(2,1)S(1)}, u32[]{:S(2)}, u32[]{:S(2)}) async-start(bf16[32,2,64,128]{3,2,1,0:T(8,128)(2,1)} %shard_map.64), calls=%async_computation | async-start | bytes 2097152 | tf_op jit(solution)/shard_map/all_to_all | solution.py:203
  44.2 6.6 %copy-start = (bf16[128,2048]{1,0:T(8,128)(2,1)S(1)}, bf16[128,2048]{1,0:T(8,128)(2,1)}, u32[]{:S(2)}) copy-start(bf16[128,2048]{1,0:T(8,128)(2,1)} %key_ref.1) | copy-start | bytes 1572868
  46.1 4.9 %copy-start.1 = (bf16[128,2048]{1,0:T(8,128)(2,1)S(1)}, bf16[128,2048]{1,0:T(8,128)(2,1)}, u32[]{:S(2)}) copy-start(bf16[128,2048]{1,0:T(8,128)(2,1)} %value_ref.1) | copy-start | bytes 1572868
  46.1 5.2 %copy-start.2 = (bf16[128,2048]{1,0:T(8,128)(2,1)S(1)}, bf16[128,2048]{1,0:T(8,128)(2,1)}, u32[]{:S(2)}) copy-start(bf16[128,2048]{1,0:T(8,128)(2,1)} %param.6) | copy-start | bytes 1572868
  47.1 19.2 %copy-start.3 = (f32[2048]{0:T(1024)S(1)}, f32[2048]{0:T(1024)}, u32[]{:S(2)}) copy-start(f32[2048]{0:T(1024)} %param.11) | copy-start | bytes 24580
  47.1 19.2 %all-to-all-start.1 = ((bf16[32,1,64,128]{3,2,1,0:T(8,128)(2,1)}), bf16[32,1,64,128]{3,2,1,0:T(8,128)(2,1)S(1)}, u32[]{:S(2)}, u32[]{:S(2)}) async-start(bf16[32,1,64,128]{3,2,1,0:T(8,128)(2,1)} %copy.22), calls=%async_computation.1 | async-start | bytes 1048576 | tf_op jit(solution)/shard_map/all_to_all | solution.py:214

commit v21 on v14

--- a/solution.py
+++ b/solution.py
@@ -170,10 +170,10 @@
     weight = jnp.where((index == 0) | (index == n_dev), 1.0, 2.0).astype(jnp.float32)[None, :]
     outcome = contract(
         "nk,kcb->ncb",
-        jnp.concatenate([back_cos * weight, -back_sin * weight], axis=1),
+        jnp.concatenate([back_cos * weight, -back_sin * weight], axis=1) * (1.0 / padded),
         jnp.concatenate([real_part, imag_part], axis=0),
     )
-    return (outcome * (1.0 / padded)).astype(jnp.bfloat16)
+    return outcome.astype(jnp.bfloat16)
 
 
 def by_channels(mixed, key_in, value_in, filters, group_index):

time: 67.8 us -> 67.8 us (level)
  no operation moved by 1% of the time
where the time goes in v21:
time: 67.8 us; the launch traced here: 67.5 us
  waiting for transfers between devices  40.1 us (59%)
  starting transfers between devices  10.9 us (16%)
  matrix products  7.5 us (11%)
  other arithmetic  3.25 us (5%)
  local copies, waits for them, and re-layouts  2.84 us (4%)
  Pallas kernels  2.66 us (4%)
    all_to_all x1, waiting for transfers between devices, by_channels(): lax.all_to_all(sent[piece], ('outer', 'inner'), split_axis=0, concat_axis...  25.4 us
    all_to_all x1, waiting for transfers between devices, by_channels(): lax.all_to_all(jnp.stack(results, axis=1), ('outer', 'inner'), split_axis...  14.7 us
    dot_general x4, matrix products, contract(): jnp.einsum(pattern, left_op, right_op, precision=lax.Precision.HIGH, pref...  7.5 us
    all_to_all x1, starting transfers between devices, by_channels(): lax.all_to_all(sent[piece], ('outer', 'inner'), split_axis=0, concat_axis...  7.3 us
    all_to_all x1, starting transfers between devices, by_channels(): lax.all_to_all(jnp.stack(results, axis=1), ('outer', 'inner'), split_axis...  3.62 us
    pallas_call x1, Pallas kernels, prepare(): pl.pallas_call(prep_kernel, out_shape=tuple((jax.ShapeDtypeStruct((n_dev,...  2.66 us
  transfers between devices with their start and end apart: 2, of which 2 were waited for; matrix products, arithmetic and copies ran while one was open for 2% of the time, Pallas kernels for 0%

profile of v21, /device:TPU:0, one launch (start us, length us, event | category | flops | bytes accessed | tf_op | source)
XLA Modules:
  0.0 67.5 jit_solution(7650558428041912297)
XLA Ops:
  0.0 2.7 %shard_map.64 = bf16[32,2,64,128]{3,2,1,0:T(8,128)(2,1)} custom-call(bf16[128,2048]{1,0:T(8,128)(2,1)} %key_ref.1, bf16[128,2048]{1,0:T(8,128)(2,1)} %value_ref.1, bf16[128,128]{1,0:T(8,128)(2,1)} %filters_ref.1, s32[1,2048]{1,0:T(1,128)} %bitcast.30), custom_call_target="tpu_custom_call" | custom-call | tf_op jit(solution)/shard_map/pallas_call | solution.py:99
  2.7 7.3 %all-to-all-start = ((bf16[32,2,64,128]{3,2,1,0:T(8,128)(2,1)}), bf16[32,2,64,128]{3,2,1,0:T(8,128)(2,1)S(1)}, u32[]{:S(2)}, u32[]{:S(2)}) async-start(bf16[32,2,64,128]{3,2,1,0:T(8,128)(2,1)} %shard_map.64), calls=%async_computation | async-start | bytes 2097152 | tf_op jit(solution)/shard_map/all_to_all | solution.py:195
  10.0 0.1 sine_negate_fusion
  10.1 0.1 fusion.61
  10.2 0.3 fusion.36
  10.4 0.3 broadcast_multiply_fusion
  10.7 0.1 cosine_multiply_fusion
  10.8 25.4 %all-to-all-done = bf16[32,2,64,128]{3,2,1,0:T(8,128)(2,1)S(1)} async-done(((bf16[32,2,64,128]{3,2,1,0:T(8,128)(2,1)}), bf16[32,2,64,128]{3,2,1,0:T(8,128)(2,1)S(1)}, u32[]{:S(2)}, u32[]{:S(2)}) %all-to-all-start) | async-done | bytes 1048608 | tf_op jit(solution)/shard_map/all_to_all | solution.py:195
  36.2 1.6 %fusion.17 = f32[66,128,128]{2,0,1:T(8,128)S(1)} fusion(bf16[32,128,128]{2,1,0:T(8,128)(2,1)S(1)} %bitcast.29, f32[33,32]{0,1:T(8,128)S(1)} %get-tuple-element.13, f32[33,32]{0,1:T(8,128)S(1)} %get-tuple-element.14), kind=kOutput, calls=%fused_computation.22 | convolution fusion | flops 207620160 | bytes 5382400 | tf_op jit(solution)/shard_map/kn,ncb->kcb/dot_general | solution.py:11
  37.8 0.7 %multiply_add_fusion = (f32[33,128,128]{2,0,1:T(8,128)S(1)}, f32[33,128,128]{2,0,1:T(8,128)S(1)}) fusion(f32[66,128,128]{2,0,1:T(8,128)S(1)} %fusion.17, f32[33,128]{1,0:T(8,128)S(1)} %get-tuple-element.15, f32[33,128]{1,0:T(8,128)S(1)} %get-tuple-element.16), kind=kLoop, calls=%fused_computation.4 | loop fusion | flops 3244032 | bytes 8684544 | tf_op jit(solution)/shard_map/add | solution.py:38
  38.5 0.3 pad_maximum_fusion
  38.9 3.0 %fusion = f32[33,128,256]{2,1,0:T(8,128)S(1)} fusion(f32[33,128,256]{2,0,1:T(8,128)S(1)} %pad_maximum_fusion, f32[128,128]{1,0:T(8,128)S(1)} %fusion.36, f32[128,128]{1,0:T(8,128)S(1)} %get-tuple-element.18, f32[128,128]{1,0:T(8,128)S(1)} %get-tuple-element.17), kind=kOutput, calls=%fused_computation.1 | convolution fusion | flops 1661140992 | bytes 8847360 | tf_op jit(solution)/shard_map/kcb,bq->kcq/dot_general | solution.py:11
  41.9 0.3 multiply_subtract_fusion.2
  42.2 1.0 %fusion.4 = f32[33,64,256]{2,1,0:T(8,128)S(1)} fusion(f32[33,64,128]{2,1,0:T(8,128)S(1)} %get-tuple-element.8, f32[33,64,128]{2,1,0:T(8,128)S(1)} %get-tuple-element.7, f32[128,128]{1,0:T(8,128)S(1)} %fusion.36, f32[128,128]{1,0:T(8,128)S(1)} %get-tuple-element.17, f32[128,128]{1,0:T(8,128)S(1)} %get-tuple-element.18), kind=kOutput, calls=%fused_computation.7 | convolution fusion | flops 831209472 | bytes 4521984 | tf_op jit(solution)/shard_map/kcq,qb->kcb/dot_general | solution.py:11
  43.3 0.3 multiply_subtract_fusion.1
  43.6 0.2 pad_maximum_fusion.1
  43.9 0.0 copy-start
  43.9 1.9 %fusion.11 = bf16[32,1,64,128]{3,0,2,1:T(8,128)(2,1)S(1)} fusion(f32[66,64,128]{2,1,0:T(8,128)S(1)} %pad_maximum_fusion.1, f32[32,33]{1,0:T(8,128)S(1)} %get-tuple-element.12, f32[32,33]{1,0:T(8,128)S(1)} %get-tuple-element.11), kind=kOutput, calls=%fused_computation.13 | convolution fusion | flops 104075392 | bytes 2695424 | tf_op jit(solution)/shard_map/nk,kcb->ncb/dot_general | solution.py:11
  45.8 0.0 copy-start.1
  45.8 0.0 copy-start.2
  45.8 1.0 %copy.22 = bf16[32,1,64,128]{3,2,1,0:T(8,128)(2,1)} copy(bf16[32,1,64,128]{3,0,2,1:T(8,128)(2,1)S(1)} %fusion.11) | data formatting | bytes 1048576 | tf_op jit(solution)/shard_map/stack | solution.py:207
  46.8 0.0 copy-start.3
  46.8 3.6 %all-to-all-start.1 = ((bf16[32,1,64,128]{3,2,1,0:T(8,128)(2,1)}), bf16[32,1,64,128]{3,2,1,0:T(8,128)(2,1)S(1)}, u32[]{:S(2)}, u32[]{:S(2)}) async-start(bf16[32,1,64,128]{3,2,1,0:T(8,128)(2,1)} %copy.22), calls=%async_computation.1 | async-start | bytes 1048576 | tf_op jit(solution)/shard_map/all_to_all | solution.py:206
  50.4 0.0 copy-done
  50.4 0.3 copy.24
  50.7 0.0 copy-done.1
  50.7 0.3 copy.25
  51.0 0.0 copy-done.2
  51.0 0.3 copy.18
  51.3 14.7 %all-to-all-done.1 = bf16[32,1,64,128]{3,2,1,0:T(8,128)(2,1)S(1)} async-done(((bf16[32,1,64,128]{3,2,1,0:T(8,128)(2,1)}), bf16[32,1,64,128]{3,2,1,0:T(8,128)(2,1)S(1)}, u32[]{:S(2)}, u32[]{:S(2)}) %all-to-all-start.1) | async-done | bytes 524320 | tf_op jit(solution)/shard_map/all_to_all | solution.py:206
  66.0 0.0 copy-done.3
  66.0 0.5 fusion.16
  66.5 1.0 %copy.26 = bf16[128,2048]{1,0:T(8,128)(2,1)} copy(bf16[128,2048]{0,1:T(8,128)(2,1)S(1)} %fusion.16) | data formatting | bytes 1048576 | tf_op jit(solution)/shard_map/convert_element_type | solution.py:216
  (1 shorter events, 0.0 us)
Async XLA Ops:
  2.7 33.5 %all-to-all-start = ((bf16[32,2,64,128]{3,2,1,0:T(8,128)(2,1)}), bf16[32,2,64,128]{3,2,1,0:T(8,128)(2,1)S(1)}, u32[]{:S(2)}, u32[]{:S(2)}) async-start(bf16[32,2,64,128]{3,2,1,0:T(8,128)(2,1)} %shard_map.64), calls=%async_computation | async-start | bytes 2097152 | tf_op jit(solution)/shard_map/all_to_all | solution.py:195
  43.9 6.6 %copy-start = (bf16[128,2048]{1,0:T(8,128)(2,1)S(1)}, bf16[128,2048]{1,0:T(8,128)(2,1)}, u32[]{:S(2)}) copy-start(bf16[128,2048]{1,0:T(8,128)(2,1)} %key_ref.1) | copy-start | bytes 1572868
  45.8 4.9 %copy-start.1 = (bf16[128,2048]{1,0:T(8,128)(2,1)S(1)}, bf16[128,2048]{1,0:T(8,128)(2,1)}, u32[]{:S(2)}) copy-start(bf16[128,2048]{1,0:T(8,128)(2,1)} %value_ref.1) | copy-start | bytes 1572868
  45.8 5.2 %copy-start.2 = (bf16[128,2048]{1,0:T(8,128)(2,1)S(1)}, bf16[128,2048]{1,0:T(8,128)(2,1)}, u32[]{:S(2)}) copy-start(bf16[128,2048]{1,0:T(8,128)(2,1)} %param.6) | copy-start | bytes 1572868
  46.8 19.2 %copy-start.3 = (f32[2048]{0:T(1024)S(1)}, f32[2048]{0:T(1024)}, u32[]{:S(2)}) copy-start(f32[2048]{0:T(1024)} %param.11) | copy-start | bytes 24580
  46.8 19.2 %all-to-all-start.1 = ((bf16[32,1,64,128]{3,2,1,0:T(8,128)(2,1)}), bf16[32,1,64,128]{3,2,1,0:T(8,128)(2,1)S(1)}, u32[]{:S(2)}, u32[]{:S(2)}) async-start(bf16[32,1,64,128]{3,2,1,0:T(8,128)(2,1)} %copy.22), calls=%async_computation.1 | async-start | bytes 1048576 | tf_op jit(solution)/shard_map/all_to_all | solution.py:206
